TPU v7x, 512 devices: a whole 4x8x8 slice. The times are simulated.
512 devices in a mesh: chan: 16 (over y, core), tm: 32 (over z, x).
Axes of the slice: x: 4, y: 8, z: 8, core: 2. Of those that a mesh axis runs over, the one named last changes fastest.
Arguments:
- spike_sample: int32 [16, 131072], P('chan', 'tm'), may hold values from 0 to 245759, as said below
- spike_unit: int32 [16, 131072], P('chan', 'tm'), may hold values from 0 to 6143, as said below
- spike_amp: bfloat16 [16, 131072], P('chan', 'tm'), may hold values from 0.2 to 12, as said below
- pair_units: int32 [2, 16384], P(None, 'chan'), may hold values from 0 to 6143, as said below
Outputs:
- corr: float32 [101, 16384], P(None, ('chan', 'tm'))
Inputs may be any that keep to these rules, and one draw needn't show every extreme that they name: `spike_sample`: the spike in column c of a row lies in time shard s = c // 4096: its sample index is at least s * 256 * 30 and below (s + 1) * 256 * 30. `spike_unit`: row g holds only spikes of units g * 384 to (g + 1) * 384 - 1. `spike_amp`: amplitudes are positive. `pair_units`: column c belongs to group g = c // 1024: its first unit is a unit of group g; its second is a unit of group g or, unless g is the last group, one of the first 64 units of group g + 1.
All inputs are finite; a program needn't handle non-finite values.
Results may differ from a plain program's by a relative error of at most 0.0031.
Values may be sent and summed in bfloat16 or wider, within the bound.
No kernel may reach another device: no remote copies, remote signals or barrier semaphores. Data moves between devices by JAX's collectives and lax.ppermute only.
A program may use at most 64 MiB of HBM per device.

v0:
```python
import math

import jax
import jax.numpy as jnp
from jax import lax
from jax.sharding import PartitionSpec as P

U_GRP = 384
BORDER = 64
BINS_DEV = 256
MAXLAG = 50
SPB = 30


def passed_along(array, axis, by):
    peers = lax.axis_size(axis)
    pairs = [(i, i + by) for i in range(peers) if 0 <= i + by < peers]
    return lax.ppermute(array, axis, pairs)


def extended_2(cells, sides, width):
    for axis, dim in sides:
        count = lax.axis_size(axis)
        ends = count - 1
        head = lax.slice_in_dim(cells, 0, width, axis=dim)
        tail = lax.slice_in_dim(cells, cells.shape[dim] - width, cells.shape[dim], axis=dim)
        cells = jnp.concatenate(
            [
                lax.ppermute(tail, axis, [(i, (i + 1) % count) for i in range(ends)]),
                cells,
                lax.ppermute(head, axis, [((i + 1) % count, i) for i in range(ends)]),
            ],
            axis=dim,
        )
    return cells


def lag_window(left_rows, right_rows):
    width = left_rows.shape[1]
    windows = jnp.stack([right_rows[:, k : k + width] for k in range(2 * MAXLAG + 1)], axis=1)
    return jnp.einsum("nt,nlt->nl", left_rows, windows, preferred_element_type=jnp.float32)


def pair_terms(centred, padded, first_units, second_units):
    total_pairs = first_units.shape[0]
    block_rows = math.gcd(total_pairs, 256)

    def one_block(indices):
        return lag_window(
            jnp.take(centred, indices[0], axis=0), jnp.take(padded, indices[1], axis=0)
        )

    results = lax.map(
        one_block, (first_units.reshape(-1, block_rows), second_units.reshape(-1, block_rows))
    )
    return results.reshape(total_pairs, -1).T


def shard_prelude(spike_sample, spike_unit, spike_amp, group_index, shard_index, shard_count):
    bin_index = spike_sample[0] // SPB - shard_index * BINS_DEV
    within = spike_unit[0] - group_index * U_GRP
    unit_onehot = (within[None, :] == jnp.arange(U_GRP, dtype=jnp.int32)[:, None]).astype(
        jnp.bfloat16
    )
    weighted = jnp.where(
        bin_index[:, None] == jnp.arange(BINS_DEV, dtype=jnp.int32)[None, :],
        spike_amp[0][:, None],
        jnp.zeros((), jnp.bfloat16),
    )
    trains = jnp.dot(unit_onehot, weighted, preferred_element_type=jnp.float32)
    totals = lax.psum(jnp.sum(trains, axis=1), "tm")
    means = totals / float(BINS_DEV * shard_count)
    centred = (trains - means[:, None]).astype(jnp.bfloat16)
    border_rows = passed_along(centred[:BORDER], "chan", -1)
    extended = jnp.concatenate([centred, border_rows], axis=0)
    padded = extended_2(extended, (("tm", 1),), MAXLAG)
    return (centred, padded)


def local(spike_sample, spike_unit, spike_amp, pair_units):
    group_index = lax.axis_index("chan")
    shard_index = lax.axis_index("tm")
    shard_count = lax.axis_size("tm")
    first_units = pair_units[0] - group_index * U_GRP
    second_units = pair_units[1] - group_index * U_GRP
    per_shard = first_units.shape[0] // shard_count
    centred, padded = shard_prelude(
        spike_sample, spike_unit, spike_amp, group_index, shard_index, shard_count
    )
    summed = lax.psum(pair_terms(centred, padded, first_units, second_units), "tm")
    return lax.dynamic_slice_in_dim(summed, shard_index * per_shard, per_shard, 1)


def solution(mesh):
    in_specs = (P("chan", "tm"), P("chan", "tm"), P("chan", "tm"), P(None, "chan"))
    out_specs = P(None, ("chan", "tm"))
    return jax.shard_map(local, mesh=mesh, in_specs=in_specs, out_specs=out_specs, check_vma=False)
```

profile of v0, /device:TPU:1, one launch (start us, length us, event | category | flops | bytes accessed | tf_op | source)
XLA Modules:
  0.0 392.2 jit_solution(884954820506347946)
XLA Ops:
  6.5 0.8 broadcast_divide_fusion
  7.3 0.8 and_reduce_fusion
  8.1 0.7 broadcast_subtract_fusion
  8.9 0.8 reduce.2
  9.7 1.7 fusion.13
  11.3 67.5 %psum.14 = f32[384]{0:T(512)S(1)} all-reduce(f32[384]{0:T(512)S(1)} %get-tuple-element.60), channel_id=1, replica_groups=mesh['chan'=16,'tm'=32] {'tm'}, use_global_device_ids=true, to_apply=%region_1.2 | all-reduce | flops 384 | bytes 3072 | tf_op jit(solution)/shard_map/psum | solution.py:71
  78.8 0.1 subtract_convert_fusion
  79.0 16.8 %collective-permute-start = (bf16[64,256]{1,0:T(8,128)(2,1)S(1)}, bf16[64,256]{1,0:T(8,128)(2,1)S(1)}, u32[]{:S(2)}, u32[]{:S(2)}) collective-permute-start(bf16[64,256]{1,0:T(8,128)(2,1)S(1)} %slice.428), channel_id=1, source_target_pairs={{32,0},{64,32},{96,64},{128,96},{160,128},{192,160},{224,192},{256... | collective-permute-start | bytes 98312 | tf_op jit(solution)/shard_map/ppermute | solution.py:18
  95.7 2.8 collective-permute-done
  98.6 1.3 collective-permute-start.1
  99.9 1.3 collective-permute-start.2
  101.2 0.8 subtract_reduce_fusion
  102.1 3.5 collective-permute-done.2
  105.6 0.2 pad_maximum_fusion
  105.8 124.1 %while.10 = (s32[]{:T(128)}, f32[4,256,101]{2,1,0:T(8,128)}, s32[4,256]{1,0:T(4,128)S(1)}, bf16[384,256]{1,0:T(8,128)(2,1)S(1)}, s32[4,256]{1,0:T(4,128)S(1)}, /*index=5*/bf16[448,356]{1,0:T(8,128)(2,1)S(1)}, s32[]{:T(128)}) while((s32[]{:T(128)}, f32[4,256,101]{2,1,0:T(8,128)}, s32[4,256]{1,0:T(4,128)S(1)}, bf16[384,256]{1,0:T(8,128)(2,1)S(1)}, ...), condition=%wide.region_3.4_spmd, body=%wide.region_2.3_spmd.sunk | while | flops 13401602 | bytes 94412400 | solution.py:53
  106.0 1.2 gather_fusion
  107.2 0.1 broadcast_select_fusion.2
  107.9 0.1 constant_dynamic-update-slice_fusion.208
  108.0 0.1 constant_dynamic-update-slice_fusion.209
  108.1 0.1 constant_dynamic-update-slice_fusion.210
  108.2 0.1 constant_dynamic-update-slice_fusion.211
  108.3 0.1 constant_dynamic-update-slice_fusion.212
  108.4 0.1 constant_dynamic-update-slice_fusion.213
  108.5 0.1 constant_dynamic-update-slice_fusion.214
  118.5 4.7 %copy-done = bf16[256,101,256]{2,0,1:T(8,128)(2,1)} copy-done((bf16[256,101,256]{2,0,1:T(8,128)(2,1)}, bf16[256,101,256]{2,0,1:T(8,128)(2,1)S(1)}, u32[]{:S(2)}) %copy-start) | copy-done | bytes 13238296 | tf_op jit(solution)/shard_map/while
  123.2 1.1 gather_fusion.1
  124.5 11.8 %fusion.19 = f32[256,1,101]{2,1,0:T(1,128)S(1)} fusion(bf16[256,101,256]{2,0,1:T(8,128)(2,1)} %copy-done, bf16[256,256,1]{1,0,2:T(8,128)(2,1)S(1)} %select_bitcast_fusion.2), kind=kOutput, calls=%fused_computation.2.clone.1 | convolution fusion | flops 13238272 | bytes 13472768 | tf_op jit(solution)/shard_map/while/body/eval_jaxpr/nt,nlt->nl/dot_general | solution.py:41
  136.3 0.7 bitcast_dynamic-update-slice_fusion.2
  137.0 1.2 gather_fusion
  138.2 0.1 broadcast_select_fusion.2
  149.5 4.7 %copy-done = bf16[256,101,256]{2,0,1:T(8,128)(2,1)} copy-done((bf16[256,101,256]{2,0,1:T(8,128)(2,1)}, bf16[256,101,256]{2,0,1:T(8,128)(2,1)S(1)}, u32[]{:S(2)}) %copy-start) | copy-done | bytes 13238296 | tf_op jit(solution)/shard_map/while
  154.2 1.1 gather_fusion.1
  155.4 11.8 %fusion.19 = f32[256,1,101]{2,1,0:T(1,128)S(1)} fusion(bf16[256,101,256]{2,0,1:T(8,128)(2,1)} %copy-done, bf16[256,256,1]{1,0,2:T(8,128)(2,1)S(1)} %select_bitcast_fusion.2), kind=kOutput, calls=%fused_computation.2.clone.1 | convolution fusion | flops 13238272 | bytes 13472768 | tf_op jit(solution)/shard_map/while/body/eval_jaxpr/nt,nlt->nl/dot_general | solution.py:41
  167.3 0.7 bitcast_dynamic-update-slice_fusion.2
  168.0 1.2 gather_fusion
  169.1 0.1 broadcast_select_fusion.2
  180.5 4.7 %copy-done = bf16[256,101,256]{2,0,1:T(8,128)(2,1)} copy-done((bf16[256,101,256]{2,0,1:T(8,128)(2,1)}, bf16[256,101,256]{2,0,1:T(8,128)(2,1)S(1)}, u32[]{:S(2)}) %copy-start) | copy-done | bytes 13238296 | tf_op jit(solution)/shard_map/while
  185.1 1.1 gather_fusion.1
  186.4 11.8 %fusion.19 = f32[256,1,101]{2,1,0:T(1,128)S(1)} fusion(bf16[256,101,256]{2,0,1:T(8,128)(2,1)} %copy-done, bf16[256,256,1]{1,0,2:T(8,128)(2,1)S(1)} %select_bitcast_fusion.2), kind=kOutput, calls=%fused_computation.2.clone.1 | convolution fusion | flops 13238272 | bytes 13472768 | tf_op jit(solution)/shard_map/while/body/eval_jaxpr/nt,nlt->nl/dot_general | solution.py:41
  198.3 0.7 bitcast_dynamic-update-slice_fusion.2
  198.9 1.2 gather_fusion
  200.1 0.1 broadcast_select_fusion.2
  211.4 4.7 %copy-done = bf16[256,101,256]{2,0,1:T(8,128)(2,1)} copy-done((bf16[256,101,256]{2,0,1:T(8,128)(2,1)}, bf16[256,101,256]{2,0,1:T(8,128)(2,1)S(1)}, u32[]{:S(2)}) %copy-start) | copy-done | bytes 13238296 | tf_op jit(solution)/shard_map/while
  216.1 1.1 gather_fusion.1
  217.4 11.8 %fusion.19 = f32[256,1,101]{2,1,0:T(1,128)S(1)} fusion(bf16[256,101,256]{2,0,1:T(8,128)(2,1)} %copy-done, bf16[256,256,1]{1,0,2:T(8,128)(2,1)S(1)} %select_bitcast_fusion.2), kind=kOutput, calls=%fused_computation.2.clone.1 | convolution fusion | flops 13238272 | bytes 13472768 | tf_op jit(solution)/shard_map/while/body/eval_jaxpr/nt,nlt->nl/dot_general | solution.py:41
  229.2 0.7 bitcast_dynamic-update-slice_fusion.2
  229.9 154.1 %all-reduce.2.cloned.1.call-done = f32[101,1024]{0,1:T(8,128)} async-done(((f32[101,1024]{0,1:T(8,128)}), f32[101,1024]{0,1:T(8,128)}) %all-reduce.2.cloned.1.call-update) | async-done | bytes 413712 | tf_op jit(solution)/shard_map/psum | solution.py:90
  384.1 1.3 constant_dynamic-slice_fusion.2
  (435 shorter events, 41.7 us)
Async XLA Ops:
  6.5 377.5 %all-reduce.2.cloned.1.call-start = ((), (), s32[]{:S(2)}) async-start(), calls=%async_computation | async-start | bytes 1048576 | tf_op jit(solution)/shard_map/psum | solution.py:90
  79.0 19.5 %collective-permute-start = (bf16[64,256]{1,0:T(8,128)(2,1)S(1)}, bf16[64,256]{1,0:T(8,128)(2,1)S(1)}, u32[]{:S(2)}, u32[]{:S(2)}) collective-permute-start(bf16[64,256]{1,0:T(8,128)(2,1)S(1)} %slice.428), channel_id=1, source_target_pairs={{32,0},{64,32},{96,64},{128,96},{160,128},{192,160},{224,192},{256... | collective-permute-start | bytes 98312 | tf_op jit(solution)/shard_map/ppermute | solution.py:18
  98.6 3.4 collective-permute-start.1
  99.9 5.6 %collective-permute-start.2 = (bf16[448,50]{1,0:T(8,128)(2,1)S(1)}, bf16[448,50]{1,0:T(8,128)(2,1)S(1)}, u32[]{:S(2)}, u32[]{:S(2)}) collective-permute-start(bf16[448,50]{1,0:T(8,128)(2,1)S(1)} %get-tuple-element.59), channel_id=1, source_target_pairs={{1,0},{2,1},{3,2},{4,3},{5,4},{6,5},{7,6},{8,7},{9,8},{10,9},{11,1... | collective-permute-start | bytes 134408 | tf_op jit(solution)/shard_map/ppermute | solution.py:31
  118.5 4.7 %copy-start = (bf16[256,101,256]{2,0,1:T(8,128)(2,1)}, bf16[256,101,256]{2,0,1:T(8,128)(2,1)S(1)}, u32[]{:S(2)}) copy-start(bf16[256,101,256]{2,0,1:T(8,128)(2,1)S(1)} %constant_dynamic-update-slice_fusion.302) | copy-start | bytes 39714820 | tf_op jit(solution)/shard_map/while
  149.5 4.7 %copy-start = (bf16[256,101,256]{2,0,1:T(8,128)(2,1)}, bf16[256,101,256]{2,0,1:T(8,128)(2,1)S(1)}, u32[]{:S(2)}) copy-start(bf16[256,101,256]{2,0,1:T(8,128)(2,1)S(1)} %constant_dynamic-update-slice_fusion.302) | copy-start | bytes 39714820 | tf_op jit(solution)/shard_map/while
  180.4 4.7 %copy-start = (bf16[256,101,256]{2,0,1:T(8,128)(2,1)}, bf16[256,101,256]{2,0,1:T(8,128)(2,1)S(1)}, u32[]{:S(2)}) copy-start(bf16[256,101,256]{2,0,1:T(8,128)(2,1)S(1)} %constant_dynamic-update-slice_fusion.302) | copy-start | bytes 39714820 | tf_op jit(solution)/shard_map/while
  211.4 4.7 %copy-start = (bf16[256,101,256]{2,0,1:T(8,128)(2,1)}, bf16[256,101,256]{2,0,1:T(8,128)(2,1)S(1)}, u32[]{:S(2)}) copy-start(bf16[256,101,256]{2,0,1:T(8,128)(2,1)S(1)} %constant_dynamic-update-slice_fusion.302) | copy-start | bytes 39714820 | tf_op jit(solution)/shard_map/while
Sparse Core Ops, SparseCore 0:
  230.1 153.9 all-reduce.1
where the time goes:
time: 397 us; the launch traced here: 392 us
  waiting for transfers between devices  160 us (40%)
  local copies, waits for them, and re-layouts  73.7 us (19%)
  blocking collectives  67.5 us (17%)
  matrix products  49.1 us (12%)
  starting transfers between devices  19.4 us (5%)
  between operations  13.5 us (3%)
  other arithmetic  5.34 us (1%)
    psum x1, waiting for transfers between devices, local(): lax.psum(pair_terms(centred, padded, first_units, second_units), 'tm')  154 us
    psum x1, blocking collectives, shard_prelude(): totals = lax.psum(jnp.sum(trains, axis=1), 'tm')  67.5 us
    while x408, local copies, waits for them, and re-layouts  60 us
    dot_general x4, matrix products, lag_window(): jnp.einsum('nt,nlt->nl', left_rows, windows, preferred_element_type=jnp.f...  47.4 us
    ppermute x1, starting transfers between devices, passed_along(): return lax.ppermute(array, axis, pairs)  16.8 us
  transfers between devices with their start and end apart: 4, of which 3 were waited for; matrix products, arithmetic and copies ran while one was open for 0% of the time, Pallas kernels for 0%

commit v1 on v0

v1 whole, which is shorter than its diff:
```python
import jax
import jax.numpy as jnp
from jax import lax
from jax.experimental import pallas as pl
from jax.sharding import PartitionSpec as P

U_GRP = 384
BORDER = 64
BINS_DEV = 256
MAXLAG = 50
SPB = 30
NLAG = 2 * MAXLAG + 1
LANES = 128
KCHUNK = 16


def corr_kernel(l_ref, r_ref, o_ref):
    steps = l_ref.shape[0] // 8
    for first in range(0, NLAG, KCHUNK):
        lags = list(range(first, min(first + KCHUNK, NLAG)))

        def body(i, accs):
            t = pl.multiple_of(i * 8, 8)
            left = l_ref[pl.ds(t, 8), :]
            return tuple(a + left * r_ref[pl.ds(t + k, 8), :] for a, k in zip(accs, lags))

        accs = lax.fori_loop(
            0, steps, body, tuple(jnp.zeros((8, LANES), jnp.float32) for _ in lags)
        )
        for a, k in zip(accs, lags):
            o_ref[pl.ds(k, 1), :] = jnp.sum(a, axis=0, keepdims=True)


def lagged_products(left_t, right_t):
    pairs = left_t.shape[1]
    return pl.pallas_call(
        corr_kernel,
        grid=(pairs // LANES,),
        in_specs=[
            pl.BlockSpec((left_t.shape[0], LANES), lambda j: (0, j)),
            pl.BlockSpec((right_t.shape[0], LANES), lambda j: (0, j)),
        ],
        out_specs=pl.BlockSpec((NLAG, LANES), lambda j: (0, j)),
        out_shape=jax.ShapeDtypeStruct((NLAG, pairs), jnp.float32),
        cost_estimate=pl.CostEstimate(
            flops=2 * NLAG * pairs * left_t.shape[0],
            bytes_accessed=4 * pairs * (left_t.shape[0] + right_t.shape[0] + NLAG),
            transcendentals=0,
        ),
    )(left_t, right_t)


def summed_over(values, axis):
    peers = lax.axis_size(axis)
    spread = jnp.broadcast_to(values[None], (peers,) + values.shape)
    return jnp.sum(lax.all_to_all(spread, axis, 0, 0, tiled=False), axis=0)


def gather_columns(rows, index):
    onehot = (lax.broadcasted_iota(jnp.int32, (rows.shape[0], index.shape[0]), 0) == index[None, :])
    return lax.dot_general(
        rows, onehot.astype(rows.dtype), (((0,), (0,)), ((), ())),
        preferred_element_type=jnp.float32,
    )


def local(spike_sample, spike_unit, spike_amp, pair_units):
    group_index = lax.axis_index("chan")
    shard_index = lax.axis_index("tm")
    shard_count = lax.axis_size("tm")
    group_count = lax.axis_size("chan")

    bin_index = spike_sample[0] // SPB - shard_index * BINS_DEV
    within = spike_unit[0] - group_index * U_GRP
    unit_onehot = (within[None, :] == jnp.arange(U_GRP, dtype=jnp.int32)[:, None]).astype(
        jnp.bfloat16
    )
    weighted = jnp.where(
        bin_index[:, None] == jnp.arange(BINS_DEV, dtype=jnp.int32)[None, :],
        spike_amp[0][:, None],
        jnp.zeros((), jnp.bfloat16),
    )
    trains = jnp.dot(unit_onehot, weighted, preferred_element_type=jnp.float32)

    to_next = [(i, i + 1) for i in range(shard_count - 1)]
    to_prev = [(i + 1, i) for i in range(shard_count - 1)]
    left_raw = lax.ppermute(trains[:, BINS_DEV - MAXLAG :], "tm", to_next)
    right_raw = lax.ppermute(trains[:, :MAXLAG], "tm", to_prev)

    totals = summed_over(jnp.sum(trains, axis=1), "tm")
    means = totals / float(BINS_DEV * shard_count)

    def centre(x):
        return (x - means[:, None]).astype(jnp.bfloat16)

    zero = jnp.zeros((), jnp.bfloat16)
    left_halo = jnp.where(shard_index > 0, centre(left_raw), zero)
    right_halo = jnp.where(shard_index < shard_count - 1, centre(right_raw), zero)
    centred = centre(trains)
    padded_own = jnp.concatenate([left_halo, centred, right_halo], axis=1)
    border = lax.ppermute(
        padded_own[:BORDER], "chan", [(i + 1, i) for i in range(group_count - 1)]
    )
    padded = jnp.concatenate([padded_own, border], axis=0)

    first_units = pair_units[0] - group_index * U_GRP
    second_units = pair_units[1] - group_index * U_GRP
    left_t = gather_columns(centred, first_units)
    right_t = gather_columns(padded, second_units)
    partial = lagged_products(left_t, right_t)

    per_shard = partial.shape[1] // shard_count
    blocks = jnp.transpose(partial.reshape(NLAG, shard_count, per_shard), (1, 0, 2))
    return jnp.sum(lax.all_to_all(blocks, "tm", 0, 0, tiled=False), axis=0)


def solution(mesh):
    in_specs = (P("chan", "tm"), P("chan", "tm"), P("chan", "tm"), P(None, "chan"))
    out_specs = P(None, ("chan", "tm"))
    return jax.shard_map(local, mesh=mesh, in_specs=in_specs, out_specs=out_specs, check_vma=False)
```

time: 397 us -> 88.7 us (0.22); the launches traced: 392 us -> 88 us
  waiting for transfers between devices: 160 us -> 6.19 us
  local copies, waits for them, and re-layouts: 73.7 us -> 1.88 us
  matrix products: 49.1 us -> 5.71 us
  blocking collectives: 67.5 us -> 27.7 us
  Pallas kernels: 0 us -> 20.2 us
  between operations: 13.5 us -> 0.14 us
    psum x1 -> x0, waiting for transfers between devices: 154 us -> none  [local(): lax.psum(pair_terms(centred, padded, first_units, second_units), 'tm')]
    psum x1 -> x0, blocking collectives: 67.5 us -> none  [shard_prelude(): totals = lax.psum(jnp.sum(trains, axis=1), 'tm')]
    while x408 -> x0, local copies, waits for them, and re-layouts: 60 us -> none
    dot_general x5 -> x3, matrix products: 49.1 us -> 5.71 us  [the longest x2 3.3 us: gather_columns(): lax.dot_general(rows, onehot.astype(rows.dtype), (((0,), (0,)), ((), ()))...]
    all_to_all x0 -> x1, blocking collectives: none -> 27.7 us  [local(): return jnp.sum(lax.all_to_all(blocks, 'tm', 0, 0, tiled=False), axis=0)]
    pallas_call x0 -> x1, Pallas kernels: none -> 20.2 us  [lagged_products(): pl.pallas_call(corr_kernel, grid=(pairs // LANES,), in_specs=[pl.BlockSpe...]
    all_to_all x0 -> x1, starting transfers between devices: none -> 13.7 us  [summed_over(): return jnp.sum(lax.all_to_all(spread, axis, 0, 0, tiled=False), axis=0)]
    ppermute x3, starting transfers between devices: 19.4 us -> 8.48 us  [the longest x1 4.05 us: local(): lax.ppermute(padded_own[:BORDER], 'chan', [(i + 1, i) for i in range(grou...]
  transfers between devices with their start and end apart: 4 -> 4, of which waited for: 3 -> 2; matrix products, arithmetic and copies ran while one was open for 0% -> 2% of each run, Pallas kernels for 0% -> 0%
where the time goes in v1:
time: 88.7 us; the launch traced here: 88 us
  blocking collectives  27.7 us (31%)
  starting transfers between devices  22.2 us (25%)
  Pallas kernels  20.2 us (23%)
  waiting for transfers between devices  6.19 us (7%)
  matrix products  5.71 us (6%)
  other arithmetic  3.93 us (4%)
  local copies, waits for them, and re-layouts  1.88 us (2%)
    all_to_all x1, blocking collectives, local(): return jnp.sum(lax.all_to_all(blocks, 'tm', 0, 0, tiled=False), axis=0)  27.7 us
    pallas_call x1, Pallas kernels, lagged_products(): pl.pallas_call(corr_kernel, grid=(pairs // LANES,), in_specs=[pl.BlockSpe...  20.2 us
    all_to_all x1, starting transfers between devices, summed_over(): return jnp.sum(lax.all_to_all(spread, axis, 0, 0, tiled=False), axis=0)  13.7 us
    all_to_all x1, waiting for transfers between devices, summed_over(): return jnp.sum(lax.all_to_all(spread, axis, 0, 0, tiled=False), axis=0)  4.28 us
    ppermute x1, starting transfers between devices, local(): lax.ppermute(padded_own[:BORDER], 'chan', [(i + 1, i) for i in range(grou...  4.05 us
    dot_general x2, matrix products, gather_columns(): lax.dot_general(rows, onehot.astype(rows.dtype), (((0,), (0,)), ((), ()))...  3.3 us
    ppermute x1, starting transfers between devices, local(): left_raw = lax.ppermute(trains[:, BINS_DEV - MAXLAG:], 'tm', to_next)  3.14 us
    dot_general x1, matrix products, local(): trains = jnp.dot(unit_onehot, weighted, preferred_element_type=jnp.float32)  2.41 us
  transfers between devices with their start and end apart: 4, of which 2 were waited for; matrix products, arithmetic and copies ran while one was open for 2% of the time, Pallas kernels for 0%

profile of v1, /device:TPU:1, one launch (start us, length us, event | category | flops | bytes accessed | tf_op | source)
XLA Modules:
  0.0 88.0 jit_solution(1814690401763091606)
XLA Ops:
  0.0 0.8 and_reduce_fusion
  0.8 0.8 broadcast_divide_fusion
  1.6 0.8 reduce.2
  2.4 0.7 broadcast_subtract_fusion
  3.1 0.0 copy-start
  3.1 2.4 %fusion.24 = (f32[384]{0:T(512)S(1)}, f32[384,256]{0,1:T(8,128)S(1)}) fusion(s32[4096]{0:T(1024)S(1)} %fusion.20, bf16[4096]{0:T(1024)(128)(2,1)S(1)} %reduce.2, s32[4096]{0:T(1024)S(1)} %bitcast.11), kind=kOutput, calls=%fused_computation.39 | convolution fusion | flops 809074304 | bytes 435712 | tf_op jit(solution)/shard_map/dot_general | solution.py:83
  5.6 0.6 broadcast_in_dim.37
  6.2 13.7 %all-to-all-start = ((f32[32,1,384]{2,1,0:T(1,128)}), f32[32,1,384]{2,1,0:T(1,128)S(1)}, u32[]{:S(2)}, u32[]{:S(2)}) async-start(f32[32,1,384]{2,1,0:T(1,128)} %broadcast_in_dim.37), calls=%async_computation | async-start | bytes 98304 | tf_op jit(solution)/shard_map/all_to_all | solution.py:56
  19.9 3.1 %collective-permute-start = (f32[384,50]{0,1:T(8,128)S(1)}, f32[384,50]{0,1:T(8,128)S(1)}, u32[]{:S(2)}, u32[]{:S(2)}) collective-permute-start(f32[384,50]{0,1:T(8,128)S(1)} %get-tuple-element.5), channel_id=1, source_target_pairs={{0,1},{1,2},{2,3},{3,4},{4,5},{5,6},{6,7},{7,8},{8,9},{9,10},{10,1... | collective-permute-start | bytes 230408 | tf_op jit(solution)/shard_map/ppermute | solution.py:87
  23.1 1.3 %collective-permute-start.1 = (f32[384,50]{0,1:T(8,128)S(1)}, f32[384,50]{0,1:T(8,128)S(1)}, u32[]{:S(2)}, u32[]{:S(2)}) collective-permute-start(f32[384,50]{0,1:T(8,128)S(1)} %get-tuple-element.6), channel_id=1, source_target_pairs={{1,0},{2,1},{3,2},{4,3},{5,4},{6,5},{7,6},{8,7},{9,8},{10,9},{11,1... | collective-permute-start | bytes 230408 | tf_op jit(solution)/shard_map/ppermute | solution.py:88
  24.4 0.0 copy-done
  24.4 4.3 %all-to-all-done = f32[32,1,384]{2,1,0:T(1,128)S(1)} async-done(((f32[32,1,384]{2,1,0:T(1,128)}), f32[32,1,384]{2,1,0:T(1,128)S(1)}, u32[]{:S(2)}, u32[]{:S(2)}) %all-to-all-start) | async-done | bytes 49184 | tf_op jit(solution)/shard_map/all_to_all | solution.py:56
  28.7 0.1 reduce_sum.28
  28.8 0.0 collective-permute-done
  28.8 0.0 collective-permute-done.1
  28.9 4.0 %collective-permute-start.2 = (bf16[64,356]{0,1:T(8,128)(2,1)S(1)}, bf16[64,356]{0,1:T(8,128)(2,1)S(1)}, u32[]{:S(2)}, u32[]{:S(2)}) collective-permute-start(bf16[64,356]{0,1:T(8,128)(2,1)S(1)} %pad_maximum_fusion), channel_id=1, source_target_pairs={{32,0},{64,32},{96,64},{128,96},{160,128},{192,160},{224,192},{256... | collective-permute-start | bytes 136712 | tf_op jit(solution)/shard_map/ppermute | solution.py:101
  33.0 1.5 %fusion.6.l_ref = f32[256,1024]{1,0:T(8,128)} fusion(bf16[384,256]{0,1:T(8,128)(2,1)S(1)} %subtract_convert_fusion, s32[1024]{0:T(1024)S(1)} %bitcast.10), kind=kOutput, calls=%fused_computation.9 | convolution fusion | flops 201719808 | bytes 1249280 | tf_op jit(solution)/shard_map/dot_general | solution.py:61
  34.5 1.9 %collective-permute-done.2 = bf16[64,356]{0,1:T(8,128)(2,1)S(1)} collective-permute-done((bf16[64,356]{0,1:T(8,128)(2,1)S(1)}, bf16[64,356]{0,1:T(8,128)(2,1)S(1)}, u32[]{:S(2)}, u32[]{:S(2)}) %collective-permute-start.2) | collective-permute-done | bytes 45600 | tf_op jit(solution)/shard_map/ppermute | solution.py:101
  36.4 1.8 %fusion.5.r_ref = f32[356,1024]{1,0:T(8,128)} fusion(s32[1024]{0:T(1024)S(1)} %bitcast.12, bf16[64,356]{0,1:T(8,128)(2,1)S(1)} %collective-permute-done.2, bf16[384,50]{0,1:T(8,128)(2,1)S(1)} %get-tuple-element.10, bf16[384,256]{0,1:T(8,128)(2,1)S(1)} %subtract_convert_fusion, bf16[384,50]{0,1:T(8,128)(2,1)S(1)} %get-tuple-element.9), kind=kOutput, calls=%fused_computation.7 | convolution fusion | flops 328366080 | bytes 1781248 | tf_op jit(solution)/shard_map/dot_general | solution.py:61
  38.2 20.2 %shard_map.46 = f32[101,1024]{1,0:T(8,128)} custom-call(f32[256,1024]{1,0:T(8,128)} %fusion.6.l_ref, f32[356,1024]{1,0:T(8,128)} %fusion.5.r_ref), custom_call_target="tpu_custom_call" | custom-call | flops 52953088 | bytes 2920448 | tf_op jit(solution)/shard_map/pallas_call | solution.py:36
  58.4 1.2 %copy.8 = f32[101,1024]{0,1:T(8,128)S(1)} copy(f32[101,1024]{1,0:T(8,128)} %shard_map.46) | data formatting | bytes 827392 | tf_op jit(solution)/shard_map/pallas_call | solution.py:36
  59.6 27.7 %all_to_all.11 = f32[32,101,32]{1,2,0:T(8,128)S(1)} all-to-all(f32[32,101,32]{1,2,0:T(8,128)S(1)} %bitcast.8), channel_id=1, replica_groups=mesh['chan'=16,'tm'=32] {'tm'}, dimensions={0} | all-to-all | bytes 827392 | tf_op jit(solution)/shard_map/all_to_all | solution.py:114
  87.3 0.7 reduce_sum.29
  (7 shorter events, 0.1 us)
Async XLA Ops:
  3.1 21.3 %copy-start = (s32[2,1024]{1,0:T(2,128)S(1)}, s32[2,1024]{1,0:T(2,128)}, u32[]{:S(2)}) copy-start(s32[2,1024]{1,0:T(2,128)} %param.7) | copy-start | bytes 24580
  6.2 22.5 %all-to-all-start = ((f32[32,1,384]{2,1,0:T(1,128)}), f32[32,1,384]{2,1,0:T(1,128)S(1)}, u32[]{:S(2)}, u32[]{:S(2)}) async-start(f32[32,1,384]{2,1,0:T(1,128)} %broadcast_in_dim.37), calls=%async_computation | async-start | bytes 98304 | tf_op jit(solution)/shard_map/all_to_all | solution.py:56
  19.9 8.9 %collective-permute-start = (f32[384,50]{0,1:T(8,128)S(1)}, f32[384,50]{0,1:T(8,128)S(1)}, u32[]{:S(2)}, u32[]{:S(2)}) collective-permute-start(f32[384,50]{0,1:T(8,128)S(1)} %get-tuple-element.5), channel_id=1, source_target_pairs={{0,1},{1,2},{2,3},{3,4},{4,5},{5,6},{6,7},{7,8},{8,9},{9,10},{10,1... | collective-permute-start | bytes 230408 | tf_op jit(solution)/shard_map/ppermute | solution.py:87
  23.1 5.7 %collective-permute-start.1 = (f32[384,50]{0,1:T(8,128)S(1)}, f32[384,50]{0,1:T(8,128)S(1)}, u32[]{:S(2)}, u32[]{:S(2)}) collective-permute-start(f32[384,50]{0,1:T(8,128)S(1)} %get-tuple-element.6), channel_id=1, source_target_pairs={{1,0},{2,1},{3,2},{4,3},{5,4},{6,5},{7,6},{8,7},{9,8},{10,9},{11,1... | collective-permute-start | bytes 230408 | tf_op jit(solution)/shard_map/ppermute | solution.py:88
  28.9 7.5 %collective-permute-start.2 = (bf16[64,356]{0,1:T(8,128)(2,1)S(1)}, bf16[64,356]{0,1:T(8,128)(2,1)S(1)}, u32[]{:S(2)}, u32[]{:S(2)}) collective-permute-start(bf16[64,356]{0,1:T(8,128)(2,1)S(1)} %pad_maximum_fusion), channel_id=1, source_target_pairs={{32,0},{64,32},{96,64},{128,96},{160,128},{192,160},{224,192},{256... | collective-permute-start | bytes 136712 | tf_op jit(solution)/shard_map/ppermute | solution.py:101

commit v2 on v1

--- a/solution.py
+++ b/solution.py
@@ -2,6 +2,7 @@
 import jax.numpy as jnp
 from jax import lax
 from jax.experimental import pallas as pl
+from jax.experimental.pallas import tpu as pltpu
 from jax.sharding import PartitionSpec as P
 
 U_GRP = 384
@@ -11,21 +12,28 @@
 SPB = 30
 NLAG = 2 * MAXLAG + 1
 LANES = 128
-KCHUNK = 16
+KCHUNK = 13
 
 
-def corr_kernel(l_ref, r_ref, o_ref):
+def corr_kernel(l_ref, r_ref, o_ref, shifted_ref):
     steps = l_ref.shape[0] // 8
+    width = shifted_ref.shape[1]
+    for r in range(8):
+        shifted_ref[r] = r_ref[pl.ds(r, width), :]
     for first in range(0, NLAG, KCHUNK):
         lags = list(range(first, min(first + KCHUNK, NLAG)))
 
         def body(i, accs):
             t = pl.multiple_of(i * 8, 8)
             left = l_ref[pl.ds(t, 8), :]
-            return tuple(a + left * r_ref[pl.ds(t + k, 8), :] for a, k in zip(accs, lags))
+            return tuple(
+                a + left * shifted_ref[k % 8, pl.ds(t + 8 * (k // 8), 8), :]
+                for a, k in zip(accs, lags)
+            )
 
         accs = lax.fori_loop(
-            0, steps, body, tuple(jnp.zeros((8, LANES), jnp.float32) for _ in lags)
+            0, steps, body, tuple(jnp.zeros((8, LANES), jnp.float32) for _ in lags),
+            unroll=True,
         )
         for a, k in zip(accs, lags):
             o_ref[pl.ds(k, 1), :] = jnp.sum(a, axis=0, keepdims=True)
@@ -42,6 +50,7 @@
         ],
         out_specs=pl.BlockSpec((NLAG, LANES), lambda j: (0, j)),
         out_shape=jax.ShapeDtypeStruct((NLAG, pairs), jnp.float32),
+        scratch_shapes=[pltpu.VMEM((8, left_t.shape[0] + 96, LANES), jnp.float32)],
         cost_estimate=pl.CostEstimate(
             flops=2 * NLAG * pairs * left_t.shape[0],
             bytes_accessed=4 * pairs * (left_t.shape[0] + right_t.shape[0] + NLAG),
@@ -97,7 +106,8 @@
     left_halo = jnp.where(shard_index > 0, centre(left_raw), zero)
     right_halo = jnp.where(shard_index < shard_count - 1, centre(right_raw), zero)
     centred = centre(trains)
-    padded_own = jnp.concatenate([left_halo, centred, right_halo], axis=1)
+    tail_pad = jnp.zeros((U_GRP, 4), jnp.bfloat16)
+    padded_own = jnp.concatenate([left_halo, centred, right_halo, tail_pad], axis=1)
     border = lax.ppermute(
         padded_own[:BORDER], "chan", [(i + 1, i) for i in range(group_count - 1)]
     )

time: 88.7 us -> 78 us (0.88)
  Pallas kernels: 20.2 us -> 9.43 us
    pallas_call x1, Pallas kernels: 20.2 us -> 9.43 us  [lagged_products(): pl.pallas_call(corr_kernel, grid=(pairs // LANES,), in_specs=[pl.BlockSpe...]
where the time goes in v2:
time: 78 us; the launch traced here: 77.2 us
  blocking collectives  27.7 us (36%)
  starting transfers between devices  22.2 us (28%)
  Pallas kernels  9.43 us (12%)
  waiting for transfers between devices  6.2 us (8%)
  matrix products  5.7 us (7%)
  other arithmetic  3.93 us (5%)
  local copies, waits for them, and re-layouts  1.88 us (2%)
    all_to_all x1, blocking collectives, local(): return jnp.sum(lax.all_to_all(blocks, 'tm', 0, 0, tiled=False), axis=0)  27.7 us
    all_to_all x1, starting transfers between devices, summed_over(): return jnp.sum(lax.all_to_all(spread, axis, 0, 0, tiled=False), axis=0)  13.7 us
    pallas_call x1, Pallas kernels, lagged_products(): pl.pallas_call(corr_kernel, grid=(pairs // LANES,), in_specs=[pl.BlockSpe...  9.43 us
    all_to_all x1, waiting for transfers between devices, summed_over(): return jnp.sum(lax.all_to_all(spread, axis, 0, 0, tiled=False), axis=0)  4.28 us
    ppermute x1, starting transfers between devices, local(): lax.ppermute(padded_own[:BORDER], 'chan', [(i + 1, i) for i in range(grou...  4.05 us
    dot_general x2, matrix products, gather_columns(): lax.dot_general(rows, onehot.astype(rows.dtype), (((0,), (0,)), ((), ()))...  3.3 us
    ppermute x1, starting transfers between devices, local(): left_raw = lax.ppermute(trains[:, BINS_DEV - MAXLAG:], 'tm', to_next)  3.14 us
    dot_general x1, matrix products, local(): trains = jnp.dot(unit_onehot, weighted, preferred_element_type=jnp.float32)  2.41 us
  transfers between devices with their start and end apart: 4, of which 2 were waited for; matrix products, arithmetic and copies ran while one was open for 2% of the time, Pallas kernels for 0%

profile of v2, /device:TPU:1, one launch (start us, length us, event | category | flops | bytes accessed | tf_op | source)
XLA Modules:
  0.0 77.2 jit_solution(10468862840350576706)
XLA Ops:
  0.0 0.8 %and_reduce_fusion = pred[4096]{0:T(1024)(128)(4,1)S(1)} fusion(s32[1,4096]{1,0:T(1,128)} %param.4), kind=kLoop, calls=%fused_computation.29 | loop fusion | flops 20480 | bytes 20480 | tf_op jit(solution)/shard_map/jit(floor_divide)/and | solution.py:82
  0.8 0.8 broadcast_divide_fusion
  1.6 0.8 reduce.2
  2.4 0.7 broadcast_subtract_fusion
  3.1 0.0 copy-start
  3.1 2.4 %fusion.26 = (f32[384]{0:T(512)S(1)}, f32[384,256]{0,1:T(8,128)S(1)}) fusion(s32[4096]{0:T(1024)S(1)} %fusion.22, bf16[4096]{0:T(1024)(128)(2,1)S(1)} %reduce.2, s32[4096]{0:T(1024)S(1)} %bitcast.11), kind=kOutput, calls=%fused_computation.42 | convolution fusion | flops 809074304 | bytes 435712 | tf_op jit(solution)/shard_map/dot_general | solution.py:92
  5.6 0.6 broadcast_in_dim.40
  6.2 13.7 %all-to-all-start = ((f32[32,1,384]{2,1,0:T(1,128)}), f32[32,1,384]{2,1,0:T(1,128)S(1)}, u32[]{:S(2)}, u32[]{:S(2)}) async-start(f32[32,1,384]{2,1,0:T(1,128)} %broadcast_in_dim.40), calls=%async_computation | async-start | bytes 98304 | tf_op jit(solution)/shard_map/all_to_all | solution.py:65
  19.9 3.1 %collective-permute-start = (f32[384,50]{0,1:T(8,128)S(1)}, f32[384,50]{0,1:T(8,128)S(1)}, u32[]{:S(2)}, u32[]{:S(2)}) collective-permute-start(f32[384,50]{0,1:T(8,128)S(1)} %get-tuple-element.5), channel_id=1, source_target_pairs={{0,1},{1,2},{2,3},{3,4},{4,5},{5,6},{6,7},{7,8},{8,9},{9,10},{10,1... | collective-permute-start | bytes 230408 | tf_op jit(solution)/shard_map/ppermute | solution.py:96
  23.1 1.3 %collective-permute-start.1 = (f32[384,50]{0,1:T(8,128)S(1)}, f32[384,50]{0,1:T(8,128)S(1)}, u32[]{:S(2)}, u32[]{:S(2)}) collective-permute-start(f32[384,50]{0,1:T(8,128)S(1)} %get-tuple-element.6), channel_id=1, source_target_pairs={{1,0},{2,1},{3,2},{4,3},{5,4},{6,5},{7,6},{8,7},{9,8},{10,9},{11,1... | collective-permute-start | bytes 230408 | tf_op jit(solution)/shard_map/ppermute | solution.py:97
  24.4 0.0 copy-done
  24.4 4.3 %all-to-all-done = f32[32,1,384]{2,1,0:T(1,128)S(1)} async-done(((f32[32,1,384]{2,1,0:T(1,128)}), f32[32,1,384]{2,1,0:T(1,128)S(1)}, u32[]{:S(2)}, u32[]{:S(2)}) %all-to-all-start) | async-done | bytes 49184 | tf_op jit(solution)/shard_map/all_to_all | solution.py:65
  28.7 0.1 reduce_sum.28
  28.8 0.0 collective-permute-done
  28.8 0.0 collective-permute-done.1
  28.9 4.0 %collective-permute-start.2 = (bf16[64,360]{0,1:T(8,128)(2,1)S(1)}, bf16[64,360]{0,1:T(8,128)(2,1)S(1)}, u32[]{:S(2)}, u32[]{:S(2)}) collective-permute-start(bf16[64,360]{0,1:T(8,128)(2,1)S(1)} %pad_maximum_fusion), channel_id=1, source_target_pairs={{32,0},{64,32},{96,64},{128,96},{160,128},{192,160},{224,192},{256... | collective-permute-start | bytes 138248 | tf_op jit(solution)/shard_map/ppermute | solution.py:111
  33.0 1.5 %fusion.6.l_ref = f32[256,1024]{1,0:T(8,128)} fusion(bf16[384,256]{0,1:T(8,128)(2,1)S(1)} %subtract_convert_fusion, s32[1024]{0:T(1024)S(1)} %bitcast.10), kind=kOutput, calls=%fused_computation.9 | convolution fusion | flops 201719808 | bytes 1249280 | tf_op jit(solution)/shard_map/dot_general | solution.py:70
  34.5 1.9 %collective-permute-done.2 = bf16[64,360]{0,1:T(8,128)(2,1)S(1)} collective-permute-done((bf16[64,360]{0,1:T(8,128)(2,1)S(1)}, bf16[64,360]{0,1:T(8,128)(2,1)S(1)}, u32[]{:S(2)}, u32[]{:S(2)}) %collective-permute-start.2) | collective-permute-done | bytes 46112 | tf_op jit(solution)/shard_map/ppermute | solution.py:111
  36.4 1.8 %fusion.5.r_ref = f32[360,1024]{1,0:T(8,128)} fusion(s32[1024]{0:T(1024)S(1)} %bitcast.12, bf16[64,360]{0,1:T(8,128)(2,1)S(1)} %collective-permute-done.2, bf16[384,4]{0,1:T(4,128)(2,1)S(1)} %broadcast_in_dim.42, bf16[384,50]{0,1:T(8,128)(2,1)S(1)} %get-tuple-element.10, bf16[384,256]{0,1:T(8,128)(2,1)S(1)} %subtract_convert_fusion, ...), kind=kOutput, calls=%fused_computation.7 | convolution fusion | flops 332372992 | bytes 1801216 | tf_op jit(solution)/shard_map/dot_general | solution.py:70
  38.2 9.4 %shard_map.46 = f32[101,1024]{1,0:T(8,128)} custom-call(f32[256,1024]{1,0:T(8,128)} %fusion.6.l_ref, f32[360,1024]{1,0:T(8,128)} %fusion.5.r_ref), custom_call_target="tpu_custom_call" | custom-call | flops 52953088 | bytes 2936832 | tf_op jit(solution)/shard_map/pallas_call | solution.py:44
  47.6 1.2 %copy.8 = f32[101,1024]{0,1:T(8,128)S(1)} copy(f32[101,1024]{1,0:T(8,128)} %shard_map.46) | data formatting | bytes 827392 | tf_op jit(solution)/shard_map/pallas_call | solution.py:44
  48.8 27.7 %all_to_all.11 = f32[32,101,32]{1,2,0:T(8,128)S(1)} all-to-all(f32[32,101,32]{1,2,0:T(8,128)S(1)} %bitcast.8), channel_id=1, replica_groups=mesh['chan'=16,'tm'=32] {'tm'}, dimensions={0} | all-to-all | bytes 827392 | tf_op jit(solution)/shard_map/all_to_all | solution.py:124
  76.5 0.7 reduce_sum.29
  (8 shorter events, 0.1 us)
Async XLA Ops:
  3.1 21.3 %copy-start = (s32[2,1024]{1,0:T(2,128)S(1)}, s32[2,1024]{1,0:T(2,128)}, u32[]{:S(2)}) copy-start(s32[2,1024]{1,0:T(2,128)} %param.7) | copy-start | bytes 24580
  6.2 22.5 %all-to-all-start = ((f32[32,1,384]{2,1,0:T(1,128)}), f32[32,1,384]{2,1,0:T(1,128)S(1)}, u32[]{:S(2)}, u32[]{:S(2)}) async-start(f32[32,1,384]{2,1,0:T(1,128)} %broadcast_in_dim.40), calls=%async_computation | async-start | bytes 98304 | tf_op jit(solution)/shard_map/all_to_all | solution.py:65
  19.9 8.9 %collective-permute-start = (f32[384,50]{0,1:T(8,128)S(1)}, f32[384,50]{0,1:T(8,128)S(1)}, u32[]{:S(2)}, u32[]{:S(2)}) collective-permute-start(f32[384,50]{0,1:T(8,128)S(1)} %get-tuple-element.5), channel_id=1, source_target_pairs={{0,1},{1,2},{2,3},{3,4},{4,5},{5,6},{6,7},{7,8},{8,9},{9,10},{10,1... | collective-permute-start | bytes 230408 | tf_op jit(solution)/shard_map/ppermute | solution.py:96
  23.1 5.7 %collective-permute-start.1 = (f32[384,50]{0,1:T(8,128)S(1)}, f32[384,50]{0,1:T(8,128)S(1)}, u32[]{:S(2)}, u32[]{:S(2)}) collective-permute-start(f32[384,50]{0,1:T(8,128)S(1)} %get-tuple-element.6), channel_id=1, source_target_pairs={{1,0},{2,1},{3,2},{4,3},{5,4},{6,5},{7,6},{8,7},{9,8},{10,9},{11,1... | collective-permute-start | bytes 230408 | tf_op jit(solution)/shard_map/ppermute | solution.py:97
  28.9 7.5 %collective-permute-start.2 = (bf16[64,360]{0,1:T(8,128)(2,1)S(1)}, bf16[64,360]{0,1:T(8,128)(2,1)S(1)}, u32[]{:S(2)}, u32[]{:S(2)}) collective-permute-start(bf16[64,360]{0,1:T(8,128)(2,1)S(1)} %pad_maximum_fusion), channel_id=1, source_target_pairs={{32,0},{64,32},{96,64},{128,96},{160,128},{192,160},{224,192},{256... | collective-permute-start | bytes 138248 | tf_op jit(solution)/shard_map/ppermute | solution.py:111

commit v3 on v2

--- a/solution.py
+++ b/solution.py
@@ -15,7 +15,7 @@
 KCHUNK = 13
 
 
-def corr_kernel(l_ref, r_ref, o_ref, shifted_ref):
+def corr_kernel(l_ref, r_ref, o_ref, shifted_ref, lags_ref):
     steps = l_ref.shape[0] // 8
     width = shifted_ref.shape[1]
     for r in range(8):
@@ -36,7 +36,9 @@
             unroll=True,
         )
         for a, k in zip(accs, lags):
-            o_ref[pl.ds(k, 1), :] = jnp.sum(a, axis=0, keepdims=True)
+            lags_ref[pl.ds(k, 1), :] = jnp.sum(a, axis=0, keepdims=True)
+    lags_ref[pl.ds(NLAG, LANES - NLAG), :] = jnp.zeros((LANES - NLAG, LANES), jnp.float32)
+    o_ref[...] = lags_ref[...].T
 
 
 def lagged_products(left_t, right_t):
@@ -48,12 +50,15 @@
             pl.BlockSpec((left_t.shape[0], LANES), lambda j: (0, j)),
             pl.BlockSpec((right_t.shape[0], LANES), lambda j: (0, j)),
         ],
-        out_specs=pl.BlockSpec((NLAG, LANES), lambda j: (0, j)),
-        out_shape=jax.ShapeDtypeStruct((NLAG, pairs), jnp.float32),
-        scratch_shapes=[pltpu.VMEM((8, left_t.shape[0] + 96, LANES), jnp.float32)],
+        out_specs=pl.BlockSpec((LANES, LANES), lambda j: (j, 0)),
+        out_shape=jax.ShapeDtypeStruct((pairs, LANES), jnp.float32),
+        scratch_shapes=[
+            pltpu.VMEM((8, left_t.shape[0] + 96, LANES), jnp.float32),
+            pltpu.VMEM((LANES, LANES), jnp.float32),
+        ],
         cost_estimate=pl.CostEstimate(
             flops=2 * NLAG * pairs * left_t.shape[0],
-            bytes_accessed=4 * pairs * (left_t.shape[0] + right_t.shape[0] + NLAG),
+            bytes_accessed=4 * pairs * (left_t.shape[0] + right_t.shape[0] + LANES),
             transcendentals=0,
         ),
     )(left_t, right_t)
@@ -79,17 +84,17 @@
     shard_count = lax.axis_size("tm")
     group_count = lax.axis_size("chan")
 
-    bin_index = spike_sample[0] // SPB - shard_index * BINS_DEV
-    within = spike_unit[0] - group_index * U_GRP
-    unit_onehot = (within[None, :] == jnp.arange(U_GRP, dtype=jnp.int32)[:, None]).astype(
-        jnp.bfloat16
-    )
+    bin_index = lax.div(spike_sample, SPB) - shard_index * BINS_DEV
+    within = spike_unit - group_index * U_GRP
+    unit_onehot = (within == lax.broadcasted_iota(jnp.int32, (U_GRP, 1), 0)).astype(jnp.bfloat16)
     weighted = jnp.where(
-        bin_index[:, None] == jnp.arange(BINS_DEV, dtype=jnp.int32)[None, :],
-        spike_amp[0][:, None],
+        bin_index == lax.broadcasted_iota(jnp.int32, (BINS_DEV, 1), 0),
+        spike_amp,
         jnp.zeros((), jnp.bfloat16),
     )
-    trains = jnp.dot(unit_onehot, weighted, preferred_element_type=jnp.float32)
+    trains = lax.dot_general(
+        unit_onehot, weighted, (((1,), (1,)), ((), ())), preferred_element_type=jnp.float32
+    )
 
     to_next = [(i, i + 1) for i in range(shard_count - 1)]
     to_prev = [(i + 1, i) for i in range(shard_count - 1)]
@@ -119,9 +124,10 @@
     right_t = gather_columns(padded, second_units)
     partial = lagged_products(left_t, right_t)
 
-    per_shard = partial.shape[1] // shard_count
-    blocks = jnp.transpose(partial.reshape(NLAG, shard_count, per_shard), (1, 0, 2))
-    return jnp.sum(lax.all_to_all(blocks, "tm", 0, 0, tiled=False), axis=0)
+    per_shard = partial.shape[0] // shard_count
+    blocks = partial.reshape(shard_count, per_shard, LANES)
+    summed = jnp.sum(lax.all_to_all(blocks, "tm", 0, 0, tiled=False), axis=0)
+    return summed[:, :NLAG].T
 
 
 def solution(mesh):

time: 78 us -> 75.9 us (0.973)
  other arithmetic: 3.93 us -> 2.47 us
    pallas_call x1 -> x0, local copies, waits for them, and re-layouts: 1.21 us -> none  [lagged_products(): pl.pallas_call(corr_kernel, grid=(pairs // LANES,), in_specs=[pl.BlockSpe...]
    and x1 -> x0, other arithmetic: 0.84 us -> none  [local(): bin_index = spike_sample[0] // SPB - shard_index * BINS_DEV]
where the time goes in v3:
time: 75.9 us; the launch traced here: 75.2 us
  blocking collectives  27.9 us (37%)
  starting transfers between devices  22.2 us (29%)
  Pallas kernels  9.77 us (13%)
  waiting for transfers between devices  6.2 us (8%)
  matrix products  5.23 us (7%)
  other arithmetic  2.47 us (3%)
  local copies, waits for them, and re-layouts  1.28 us (2%)
    all_to_all x1, blocking collectives, local(): summed = jnp.sum(lax.all_to_all(blocks, 'tm', 0, 0, tiled=False), axis=0)  27.9 us
    all_to_all x1, starting transfers between devices, summed_over(): return jnp.sum(lax.all_to_all(spread, axis, 0, 0, tiled=False), axis=0)  13.7 us
    pallas_call x1, Pallas kernels, lagged_products(): pl.pallas_call(corr_kernel, grid=(pairs // LANES,), in_specs=[pl.BlockSpe...  9.77 us
    all_to_all x1, waiting for transfers between devices, summed_over(): return jnp.sum(lax.all_to_all(spread, axis, 0, 0, tiled=False), axis=0)  4.29 us
    ppermute x1, starting transfers between devices, local(): lax.ppermute(padded_own[:BORDER], 'chan', [(i + 1, i) for i in range(grou...  4.05 us
    dot_general x2, matrix products, gather_columns(): lax.dot_general(rows, onehot.astype(rows.dtype), (((0,), (0,)), ((), ()))...  3.3 us
    ppermute x1, starting transfers between devices, local(): left_raw = lax.ppermute(trains[:, BINS_DEV - MAXLAG:], 'tm', to_next)  3.14 us
    dot_general x1, matrix products, local(): lax.dot_general(unit_onehot, weighted, (((1,), (1,)), ((), ())), preferre...  1.93 us
  transfers between devices with their start and end apart: 4, of which 2 were waited for; matrix products, arithmetic and copies ran while one was open for 2% of the time, Pallas kernels for 0%

profile of v3, /device:TPU:1, one launch (start us, length us, event | category | flops | bytes accessed | tf_op | source)
XLA Modules:
  0.0 75.2 jit_solution(10137560471897475338)
XLA Ops:
  0.0 0.8 %reduce.1 = bf16[4096]{0:T(1024)(128)(2,1)S(1)} reduce(bf16[1,4096]{1,0:T(2,128)(2,1)} %param.6, bf16[]{:T(256)} %constant.30), dimensions={0}, to_apply=%param.6.reduce_sub_computation | reduce | bytes 16386 | tf_op args[2]
  0.8 0.7 broadcast_subtract_fusion
  1.5 0.8 %divide_subtract_fusion = s32[1,4096]{1,0:T(1,128)S(1)} fusion(s32[1,4096]{1,0:T(1,128)} %param.4, s32[]{:T(128)S(6)} %mul.9), kind=kLoop, calls=%fused_computation.32 | loop fusion | flops 8192 | bytes 32772 | tf_op jit(solution)/shard_map/sub | solution.py:87
  2.3 0.0 copy-start
  2.3 1.9 %fusion.25 = (f32[384]{0:T(512)S(1)}, f32[384,256]{0,1:T(8,128)S(1)}) fusion(s32[4096]{0:T(1024)S(1)} %bitcast.11, bf16[4096]{0:T(1024)(128)(2,1)S(1)} %reduce.1, s32[4096]{0:T(1024)S(1)} %bitcast.10), kind=kOutput, calls=%fused_computation.40 | convolution fusion | flops 809074304 | bytes 435712 | tf_op jit(solution)/shard_map/dot_general | solution.py:95
  4.2 0.6 broadcast_in_dim.36
  4.9 13.7 %all-to-all-start = ((f32[32,1,384]{2,1,0:T(1,128)}), f32[32,1,384]{2,1,0:T(1,128)S(1)}, u32[]{:S(2)}, u32[]{:S(2)}) async-start(f32[32,1,384]{2,1,0:T(1,128)} %broadcast_in_dim.36), calls=%async_computation | async-start | bytes 98304 | tf_op jit(solution)/shard_map/all_to_all | solution.py:70
  18.6 3.1 %collective-permute-start = (f32[384,50]{0,1:T(8,128)S(1)}, f32[384,50]{0,1:T(8,128)S(1)}, u32[]{:S(2)}, u32[]{:S(2)}) collective-permute-start(f32[384,50]{0,1:T(8,128)S(1)} %get-tuple-element.5), channel_id=1, source_target_pairs={{0,1},{1,2},{2,3},{3,4},{4,5},{5,6},{6,7},{7,8},{8,9},{9,10},{10,1... | collective-permute-start | bytes 230408 | tf_op jit(solution)/shard_map/ppermute | solution.py:101
  21.8 1.3 %collective-permute-start.1 = (f32[384,50]{0,1:T(8,128)S(1)}, f32[384,50]{0,1:T(8,128)S(1)}, u32[]{:S(2)}, u32[]{:S(2)}) collective-permute-start(f32[384,50]{0,1:T(8,128)S(1)} %get-tuple-element.6), channel_id=1, source_target_pairs={{1,0},{2,1},{3,2},{4,3},{5,4},{6,5},{7,6},{8,7},{9,8},{10,9},{11,1... | collective-permute-start | bytes 230408 | tf_op jit(solution)/shard_map/ppermute | solution.py:102
  23.1 0.0 copy-done
  23.1 4.3 %all-to-all-done = f32[32,1,384]{2,1,0:T(1,128)S(1)} async-done(((f32[32,1,384]{2,1,0:T(1,128)}), f32[32,1,384]{2,1,0:T(1,128)S(1)}, u32[]{:S(2)}, u32[]{:S(2)}) %all-to-all-start) | async-done | bytes 49184 | tf_op jit(solution)/shard_map/all_to_all | solution.py:70
  27.4 0.1 reduce_sum.28
  27.5 0.0 collective-permute-done
  27.5 0.0 collective-permute-done.1
  27.6 4.0 %collective-permute-start.2 = (bf16[64,360]{0,1:T(8,128)(2,1)S(1)}, bf16[64,360]{0,1:T(8,128)(2,1)S(1)}, u32[]{:S(2)}, u32[]{:S(2)}) collective-permute-start(bf16[64,360]{0,1:T(8,128)(2,1)S(1)} %pad_maximum_fusion), channel_id=1, source_target_pairs={{32,0},{64,32},{96,64},{128,96},{160,128},{192,160},{224,192},{256... | collective-permute-start | bytes 138248 | tf_op jit(solution)/shard_map/ppermute | solution.py:116
  31.6 1.5 %fusion.6.l_ref = f32[256,1024]{1,0:T(8,128)} fusion(bf16[384,256]{0,1:T(8,128)(2,1)S(1)} %subtract_convert_fusion, s32[1024]{0:T(1024)S(1)} %bitcast.9), kind=kOutput, calls=%fused_computation.9 | convolution fusion | flops 201719808 | bytes 1249280 | tf_op jit(solution)/shard_map/dot_general | solution.py:75
  33.1 1.9 %collective-permute-done.2 = bf16[64,360]{0,1:T(8,128)(2,1)S(1)} collective-permute-done((bf16[64,360]{0,1:T(8,128)(2,1)S(1)}, bf16[64,360]{0,1:T(8,128)(2,1)S(1)}, u32[]{:S(2)}, u32[]{:S(2)}) %collective-permute-start.2) | collective-permute-done | bytes 46112 | tf_op jit(solution)/shard_map/ppermute | solution.py:116
  35.0 1.8 %fusion.5.r_ref = f32[360,1024]{1,0:T(8,128)} fusion(s32[1024]{0:T(1024)S(1)} %bitcast.12, bf16[64,360]{0,1:T(8,128)(2,1)S(1)} %collective-permute-done.2, bf16[384,4]{0,1:T(4,128)(2,1)S(1)} %broadcast_in_dim.38, bf16[384,50]{0,1:T(8,128)(2,1)S(1)} %get-tuple-element.10, bf16[384,256]{0,1:T(8,128)(2,1)S(1)} %subtract_convert_fusion, ...), kind=kOutput, calls=%fused_computation.7 | convolution fusion | flops 332372992 | bytes 1801216 | tf_op jit(solution)/shard_map/dot_general | solution.py:75
  36.8 9.8 %shard_map.46 = f32[1024,128]{1,0:T(8,128)} custom-call(f32[256,1024]{1,0:T(8,128)} %fusion.6.l_ref, f32[360,1024]{1,0:T(8,128)} %fusion.5.r_ref), custom_call_target="tpu_custom_call" | custom-call | flops 52953088 | bytes 3047424 | tf_op jit(solution)/shard_map/pallas_call | solution.py:46
  46.6 27.9 %all_to_all.11 = f32[32,32,128]{2,1,0:T(8,128)S(1)} all-to-all(f32[32,32,128]{2,1,0:T(8,128)} %bitcast.8), channel_id=1, replica_groups=mesh['chan'=16,'tm'=32] {'tm'}, dimensions={0} | all-to-all | bytes 1048576 | tf_op jit(solution)/shard_map/all_to_all | solution.py:129
  74.6 0.6 slice_bitcast_fusion
  (8 shorter events, 0.2 us)
Async XLA Ops:
  2.3 20.8 %copy-start = (s32[2,1024]{1,0:T(2,128)S(1)}, s32[2,1024]{1,0:T(2,128)}, u32[]{:S(2)}) copy-start(s32[2,1024]{1,0:T(2,128)} %param.7) | copy-start | bytes 24580
  4.9 22.5 %all-to-all-start = ((f32[32,1,384]{2,1,0:T(1,128)}), f32[32,1,384]{2,1,0:T(1,128)S(1)}, u32[]{:S(2)}, u32[]{:S(2)}) async-start(f32[32,1,384]{2,1,0:T(1,128)} %broadcast_in_dim.36), calls=%async_computation | async-start | bytes 98304 | tf_op jit(solution)/shard_map/all_to_all | solution.py:70
  18.6 8.9 %collective-permute-start = (f32[384,50]{0,1:T(8,128)S(1)}, f32[384,50]{0,1:T(8,128)S(1)}, u32[]{:S(2)}, u32[]{:S(2)}) collective-permute-start(f32[384,50]{0,1:T(8,128)S(1)} %get-tuple-element.5), channel_id=1, source_target_pairs={{0,1},{1,2},{2,3},{3,4},{4,5},{5,6},{6,7},{7,8},{8,9},{9,10},{10,1... | collective-permute-start | bytes 230408 | tf_op jit(solution)/shard_map/ppermute | solution.py:101
  21.8 5.7 %collective-permute-start.1 = (f32[384,50]{0,1:T(8,128)S(1)}, f32[384,50]{0,1:T(8,128)S(1)}, u32[]{:S(2)}, u32[]{:S(2)}) collective-permute-start(f32[384,50]{0,1:T(8,128)S(1)} %get-tuple-element.6), channel_id=1, source_target_pairs={{1,0},{2,1},{3,2},{4,3},{5,4},{6,5},{7,6},{8,7},{9,8},{10,9},{11,1... | collective-permute-start | bytes 230408 | tf_op jit(solution)/shard_map/ppermute | solution.py:102
  27.6 7.5 %collective-permute-start.2 = (bf16[64,360]{0,1:T(8,128)(2,1)S(1)}, bf16[64,360]{0,1:T(8,128)(2,1)S(1)}, u32[]{:S(2)}, u32[]{:S(2)}) collective-permute-start(bf16[64,360]{0,1:T(8,128)(2,1)S(1)} %pad_maximum_fusion), channel_id=1, source_target_pairs={{32,0},{64,32},{96,64},{128,96},{160,128},{192,160},{224,192},{256... | collective-permute-start | bytes 138248 | tf_op jit(solution)/shard_map/ppermute | solution.py:116

commit v4 on v3

--- a/solution.py
+++ b/solution.py
@@ -118,16 +118,24 @@
     )
     padded = jnp.concatenate([padded_own, border], axis=0)
 
-    first_units = pair_units[0] - group_index * U_GRP
-    second_units = pair_units[1] - group_index * U_GRP
-    left_t = gather_columns(centred, first_units)
-    right_t = gather_columns(padded, second_units)
-    partial = lagged_products(left_t, right_t)
+    per_shard = pair_units.shape[1] // shard_count
+    halves = 2
 
-    per_shard = partial.shape[0] // shard_count
-    blocks = partial.reshape(shard_count, per_shard, LANES)
-    summed = jnp.sum(lax.all_to_all(blocks, "tm", 0, 0, tiled=False), axis=0)
-    return summed[:, :NLAG].T
+    def in_halves(index):
+        return jnp.transpose(
+            index.reshape(shard_count, halves, per_shard // halves), (1, 0, 2)
+        ).reshape(halves, -1)
+
+    first_units = in_halves(pair_units[0] - group_index * U_GRP)
+    second_units = in_halves(pair_units[1] - group_index * U_GRP)
+    summed = []
+    for h in range(halves):
+        left_t = gather_columns(centred, first_units[h])
+        right_t = gather_columns(padded, second_units[h])
+        partial = lagged_products(left_t, right_t)
+        blocks = partial.reshape(shard_count, per_shard // halves, LANES)
+        summed.append(jnp.sum(lax.all_to_all(blocks, "tm", 0, 0, tiled=False), axis=0))
+    return jnp.concatenate(summed, axis=0)[:, :NLAG].T
 
 
 def solution(mesh):

time: 75.9 us -> 83.5 us (1.10)
  blocking collectives: 27.9 us -> 0 us
  waiting for transfers between devices: 6.2 us -> 25.8 us
  starting transfers between devices: 22.2 us -> 34.1 us
  Pallas kernels: 9.77 us -> 11.4 us
  matrix products: 5.23 us -> 6.86 us
    all_to_all x1 -> x0, blocking collectives: 27.9 us -> none  [local(): summed = jnp.sum(lax.all_to_all(blocks, 'tm', 0, 0, tiled=False), axis=0)]
    all_to_all x0 -> x2, waiting for transfers between devices: none -> 15.4 us  [local(): lax.all_to_all(blocks, 'tm', 0, 0, tiled=False)]
    all_to_all x0 -> x2, starting transfers between devices: none -> 9.71 us  [local(): lax.all_to_all(blocks, 'tm', 0, 0, tiled=False)]
    all_to_all x1, waiting for transfers between devices: 4.29 us -> 8.13 us  [summed_over(): return jnp.sum(lax.all_to_all(spread, axis, 0, 0, tiled=False), axis=0)]
    dot_general x2 -> x4, matrix products: 3.3 us -> 4.93 us  [gather_columns(): lax.dot_general(rows, onehot.astype(rows.dtype), (((0,), (0,)), ((), ()))...]
    pallas_call x1 -> x2, Pallas kernels: 9.77 us -> 11.4 us  [lagged_products(): pl.pallas_call(corr_kernel, grid=(pairs // LANES,), in_specs=[pl.BlockSpe...]
    all_to_all x1, starting transfers between devices: 13.7 us -> 14.6 us  [summed_over(): return jnp.sum(lax.all_to_all(spread, axis, 0, 0, tiled=False), axis=0)]
  transfers between devices with their start and end apart: 4 -> 6, of which waited for: 2 -> 4; matrix products, arithmetic and copies ran while one was open for 2% -> 6% of each run, Pallas kernels for 0% -> 7%
where the time goes in v4:
time: 83.5 us; the launch traced here: 82.8 us
  starting transfers between devices  34.1 us (41%)
  waiting for transfers between devices  25.8 us (31%)
  Pallas kernels  11.4 us (14%)
  matrix products  6.86 us (8%)
  other arithmetic  3.13 us (4%)
  local copies, waits for them, and re-layouts  1.36 us (2%)
    all_to_all x2, waiting for transfers between devices, local(): lax.all_to_all(blocks, 'tm', 0, 0, tiled=False)  15.4 us
    all_to_all x1, starting transfers between devices, summed_over(): return jnp.sum(lax.all_to_all(spread, axis, 0, 0, tiled=False), axis=0)  14.6 us
    pallas_call x2, Pallas kernels, lagged_products(): pl.pallas_call(corr_kernel, grid=(pairs // LANES,), in_specs=[pl.BlockSpe...  11.4 us
    all_to_all x2, starting transfers between devices, local(): lax.all_to_all(blocks, 'tm', 0, 0, tiled=False)  9.71 us
    all_to_all x1, waiting for transfers between devices, summed_over(): return jnp.sum(lax.all_to_all(spread, axis, 0, 0, tiled=False), axis=0)  8.13 us
    dot_general x4, matrix products, gather_columns(): lax.dot_general(rows, onehot.astype(rows.dtype), (((0,), (0,)), ((), ()))...  4.93 us
    ppermute x1, starting transfers between devices, local(): lax.ppermute(padded_own[:BORDER], 'chan', [(i + 1, i) for i in range(grou...  4.57 us
    ppermute x1, starting transfers between devices, local(): left_raw = lax.ppermute(trains[:, BINS_DEV - MAXLAG:], 'tm', to_next)  3.95 us
  transfers between devices with their start and end apart: 6, of which 4 were waited for; matrix products, arithmetic and copies ran while one was open for 6% of the time, Pallas kernels for 7%

profile of v4, /device:TPU:1, one launch (start us, length us, event | category | flops | bytes accessed | tf_op | source)
XLA Modules:
  0.0 82.8 jit_solution(18117652419375397982)
XLA Ops:
  0.0 0.8 divide_subtract_fusion
  0.8 0.7 broadcast_subtract_fusion
  1.5 0.8 reduce.1
  2.3 0.0 copy-start
  2.3 1.9 %fusion.20 = (f32[384]{0:T(512)S(1)}, f32[384,256]{0,1:T(8,128)S(1)}) fusion(s32[4096]{0:T(1024)S(1)} %bitcast.14, bf16[4096]{0:T(1024)(128)(2,1)S(1)} %reduce.1, s32[4096]{0:T(1024)S(1)} %bitcast.15), kind=kOutput, calls=%fused_computation.42 | convolution fusion | flops 809074304 | bytes 435712 | tf_op jit(solution)/shard_map/dot_general | solution.py:95
  4.2 3.9 %collective-permute-start = (f32[384,50]{0,1:T(8,128)S(1)}, f32[384,50]{0,1:T(8,128)S(1)}, u32[]{:S(2)}, u32[]{:S(2)}) collective-permute-start(f32[384,50]{0,1:T(8,128)S(1)} %get-tuple-element.11), channel_id=1, source_target_pairs={{0,1},{1,2},{2,3},{3,4},{4,5},{5,6},{6,7},{7,8},{8,9},{9,10},{10,1... | collective-permute-start | bytes 230408 | tf_op jit(solution)/shard_map/ppermute | solution.py:101
  8.2 1.3 %collective-permute-start.1 = (f32[384,50]{0,1:T(8,128)S(1)}, f32[384,50]{0,1:T(8,128)S(1)}, u32[]{:S(2)}, u32[]{:S(2)}) collective-permute-start(f32[384,50]{0,1:T(8,128)S(1)} %get-tuple-element.12), channel_id=1, source_target_pairs={{1,0},{2,1},{3,2},{4,3},{5,4},{6,5},{7,6},{8,7},{9,8},{10,9},{11,1... | collective-permute-start | bytes 230408 | tf_op jit(solution)/shard_map/ppermute | solution.py:102
  9.5 0.6 broadcast_in_dim.34
  10.1 14.6 %all-to-all-start = ((f32[32,1,384]{2,1,0:T(1,128)}), f32[32,1,384]{2,1,0:T(1,128)S(1)}, u32[]{:S(2)}, u32[]{:S(2)}) async-start(f32[32,1,384]{2,1,0:T(1,128)} %broadcast_in_dim.34), calls=%async_computation | async-start | bytes 98304 | tf_op jit(solution)/shard_map/all_to_all | solution.py:70
  24.7 0.0 copy-done
  24.8 0.1 sub.60
  24.9 0.1 sub.65
  25.0 0.2 slice_reduce_fusion.2
  25.2 0.1 eq.81
  25.3 0.1 eq.78
  25.3 8.1 %all-to-all-done = f32[32,1,384]{2,1,0:T(1,128)S(1)} async-done(((f32[32,1,384]{2,1,0:T(1,128)}), f32[32,1,384]{2,1,0:T(1,128)S(1)}, u32[]{:S(2)}, u32[]{:S(2)}) %all-to-all-start) | async-done | bytes 49184 | tf_op jit(solution)/shard_map/all_to_all | solution.py:70
  33.5 0.1 reduce_sum.37
  33.6 0.0 collective-permute-done
  33.6 0.0 collective-permute-done.1
  33.7 4.6 %collective-permute-start.2 = (bf16[64,360]{0,1:T(8,128)(2,1)S(1)}, bf16[64,360]{0,1:T(8,128)(2,1)S(1)}, u32[]{:S(2)}, u32[]{:S(2)}) collective-permute-start(bf16[64,360]{0,1:T(8,128)(2,1)S(1)} %pad_maximum_fusion.1), channel_id=1, source_target_pairs={{32,0},{64,32},{96,64},{128,96},{160,128},{192,160},{224,192},{256... | collective-permute-start | bytes 138248 | tf_op jit(solution)/shard_map/ppermute | solution.py:116
  38.3 1.1 %fusion.9.l_ref = f32[256,512]{1,0:T(8,128)} fusion(bf16[384,256]{0,1:T(8,128)(2,1)S(1)} %subtract_convert_fusion, s32[512]{0:T(512)S(1)} %eq.78), kind=kOutput, calls=%fused_computation.14 | convolution fusion | flops 100859904 | bytes 722944 | tf_op jit(solution)/shard_map/dot_general | solution.py:75
  39.4 2.3 %collective-permute-done.2 = bf16[64,360]{0,1:T(8,128)(2,1)S(1)} collective-permute-done((bf16[64,360]{0,1:T(8,128)(2,1)S(1)}, bf16[64,360]{0,1:T(8,128)(2,1)S(1)}, u32[]{:S(2)}, u32[]{:S(2)}) %collective-permute-start.2) | collective-permute-done | bytes 46112 | tf_op jit(solution)/shard_map/ppermute | solution.py:116
  41.7 1.3 %fusion.7.r_ref = f32[360,512]{1,0:T(8,128)} fusion(s32[512]{0:T(512)S(1)} %eq.81, bf16[64,360]{0,1:T(8,128)(2,1)S(1)} %collective-permute-done.2, bf16[384,4]{0,1:T(4,128)(2,1)S(1)} %broadcast_in_dim.36, bf16[384,50]{0,1:T(8,128)(2,1)S(1)} %get-tuple-element.14, bf16[384,256]{0,1:T(8,128)(2,1)S(1)} %subtract_convert_fusion, ...), kind=kOutput, calls=%fused_computation.10 | convolution fusion | flops 166992896 | bytes 1061888 | tf_op jit(solution)/shard_map/dot_general | solution.py:75
  43.0 5.7 %shard_map.46 = f32[512,128]{1,0:T(8,128)} custom-call(f32[256,512]{1,0:T(8,128)} %fusion.9.l_ref, f32[360,512]{1,0:T(8,128)} %fusion.7.r_ref), custom_call_target="tpu_custom_call" | custom-call | flops 26476544 | bytes 1523712 | tf_op jit(solution)/shard_map/pallas_call | solution.py:46
  48.7 3.9 %all-to-all-start.1 = ((f32[32,16,128]{2,1,0:T(8,128)}), f32[32,16,128]{2,1,0:T(8,128)S(1)}, u32[]{:S(2)}, u32[]{:S(2)}) async-start(f32[32,16,128]{2,1,0:T(8,128)} %bitcast.10), calls=%async_computation.1 | async-start | bytes 524288 | tf_op jit(solution)/shard_map/all_to_all | solution.py:137
  52.5 0.1 eq.87
  52.6 0.1 eq.84
  52.7 1.2 %fusion.10.l_ref = f32[256,512]{1,0:T(8,128)} fusion(bf16[384,256]{0,1:T(8,128)(2,1)S(1)} %subtract_convert_fusion, s32[512]{0:T(512)S(1)} %eq.84), kind=kOutput, calls=%fused_computation.15 | convolution fusion | flops 100859904 | bytes 722944 | tf_op jit(solution)/shard_map/dot_general | solution.py:75
  53.9 1.3 %fusion.8.r_ref = f32[360,512]{1,0:T(8,128)} fusion(s32[512]{0:T(512)S(1)} %eq.87, bf16[64,360]{0,1:T(8,128)(2,1)S(1)} %collective-permute-done.2, bf16[384,4]{0,1:T(4,128)(2,1)S(1)} %broadcast_in_dim.36, bf16[384,50]{0,1:T(8,128)(2,1)S(1)} %get-tuple-element.14, bf16[384,256]{0,1:T(8,128)(2,1)S(1)} %subtract_convert_fusion, ...), kind=kOutput, calls=%fused_computation.11 | convolution fusion | flops 166992896 | bytes 1061888 | tf_op jit(solution)/shard_map/dot_general | solution.py:75
  55.2 5.7 %shard_map.47 = f32[512,128]{1,0:T(8,128)} custom-call(f32[256,512]{1,0:T(8,128)} %fusion.10.l_ref, f32[360,512]{1,0:T(8,128)} %fusion.8.r_ref), custom_call_target="tpu_custom_call" | custom-call | flops 26476544 | bytes 1523712 | tf_op jit(solution)/shard_map/pallas_call | solution.py:46
  60.9 3.4 %all-to-all-done.1 = f32[32,16,128]{2,1,0:T(8,128)S(1)} async-done(((f32[32,16,128]{2,1,0:T(8,128)}), f32[32,16,128]{2,1,0:T(8,128)S(1)}, u32[]{:S(2)}, u32[]{:S(2)}) %all-to-all-start.1) | async-done | bytes 262176 | tf_op jit(solution)/shard_map/all_to_all | solution.py:137
  64.2 5.8 %all-to-all-start.2 = ((f32[32,16,128]{2,1,0:T(8,128)}), f32[32,16,128]{2,1,0:T(8,128)S(1)}, u32[]{:S(2)}, u32[]{:S(2)}) async-start(f32[32,16,128]{2,1,0:T(8,128)} %bitcast.11), calls=%async_computation.2 | async-start | bytes 524288 | tf_op jit(solution)/shard_map/all_to_all | solution.py:137
  70.1 12.0 %all-to-all-done.2 = f32[32,16,128]{2,1,0:T(8,128)S(1)} async-done(((f32[32,16,128]{2,1,0:T(8,128)}), f32[32,16,128]{2,1,0:T(8,128)S(1)}, u32[]{:S(2)}, u32[]{:S(2)}) %all-to-all-start.2) | async-done | bytes 262176 | tf_op jit(solution)/shard_map/all_to_all | solution.py:137
  82.2 0.6 fusion.17
  (9 shorter events, 0.2 us)
Async XLA Ops:
  2.3 22.5 %copy-start = (s32[2,1024]{1,0:T(2,128)S(1)}, s32[2,1024]{1,0:T(2,128)}, u32[]{:S(2)}) copy-start(s32[2,1024]{1,0:T(2,128)} %param.7) | copy-start | bytes 24580
  4.2 29.3 %collective-permute-start = (f32[384,50]{0,1:T(8,128)S(1)}, f32[384,50]{0,1:T(8,128)S(1)}, u32[]{:S(2)}, u32[]{:S(2)}) collective-permute-start(f32[384,50]{0,1:T(8,128)S(1)} %get-tuple-element.11), channel_id=1, source_target_pairs={{0,1},{1,2},{2,3},{3,4},{4,5},{5,6},{6,7},{7,8},{8,9},{9,10},{10,1... | collective-permute-start | bytes 230408 | tf_op jit(solution)/shard_map/ppermute | solution.py:101
  8.2 25.4 %collective-permute-start.1 = (f32[384,50]{0,1:T(8,128)S(1)}, f32[384,50]{0,1:T(8,128)S(1)}, u32[]{:S(2)}, u32[]{:S(2)}) collective-permute-start(f32[384,50]{0,1:T(8,128)S(1)} %get-tuple-element.12), channel_id=1, source_target_pairs={{1,0},{2,1},{3,2},{4,3},{5,4},{6,5},{7,6},{8,7},{9,8},{10,9},{11,1... | collective-permute-start | bytes 230408 | tf_op jit(solution)/shard_map/ppermute | solution.py:102
  10.1 23.3 %all-to-all-start = ((f32[32,1,384]{2,1,0:T(1,128)}), f32[32,1,384]{2,1,0:T(1,128)S(1)}, u32[]{:S(2)}, u32[]{:S(2)}) async-start(f32[32,1,384]{2,1,0:T(1,128)} %broadcast_in_dim.34), calls=%async_computation | async-start | bytes 98304 | tf_op jit(solution)/shard_map/all_to_all | solution.py:70
  33.7 8.0 %collective-permute-start.2 = (bf16[64,360]{0,1:T(8,128)(2,1)S(1)}, bf16[64,360]{0,1:T(8,128)(2,1)S(1)}, u32[]{:S(2)}, u32[]{:S(2)}) collective-permute-start(bf16[64,360]{0,1:T(8,128)(2,1)S(1)} %pad_maximum_fusion.1), channel_id=1, source_target_pairs={{32,0},{64,32},{96,64},{128,96},{160,128},{192,160},{224,192},{256... | collective-permute-start | bytes 138248 | tf_op jit(solution)/shard_map/ppermute | solution.py:116
  48.7 15.6 %all-to-all-start.1 = ((f32[32,16,128]{2,1,0:T(8,128)}), f32[32,16,128]{2,1,0:T(8,128)S(1)}, u32[]{:S(2)}, u32[]{:S(2)}) async-start(f32[32,16,128]{2,1,0:T(8,128)} %bitcast.10), calls=%async_computation.1 | async-start | bytes 524288 | tf_op jit(solution)/shard_map/all_to_all | solution.py:137
  64.2 17.9 %all-to-all-start.2 = ((f32[32,16,128]{2,1,0:T(8,128)}), f32[32,16,128]{2,1,0:T(8,128)S(1)}, u32[]{:S(2)}, u32[]{:S(2)}) async-start(f32[32,16,128]{2,1,0:T(8,128)} %bitcast.11), calls=%async_computation.2 | async-start | bytes 524288 | tf_op jit(solution)/shard_map/all_to_all | solution.py:137

commit v5 on v3

--- a/solution.py
+++ b/solution.py
@@ -13,21 +13,22 @@
 NLAG = 2 * MAXLAG + 1
 LANES = 128
 KCHUNK = 13
+WINDOW_PAD = 6
 
 
-def corr_kernel(l_ref, r_ref, o_ref, shifted_ref, lags_ref):
-    steps = l_ref.shape[0] // 8
-    width = shifted_ref.shape[1]
+def corr_kernel(l_ref, r_ref, o_ref, left_ref, right_ref, lags_ref):
+    steps = (l_ref.shape[0] - MAXLAG) // 8
+    width = left_ref.shape[1]
     for r in range(8):
-        shifted_ref[r] = r_ref[pl.ds(r, width), :]
-    for first in range(0, NLAG, KCHUNK):
-        lags = list(range(first, min(first + KCHUNK, NLAG)))
+        left_ref[r] = l_ref[pl.ds(r, width), :]
+        right_ref[r] = r_ref[pl.ds(r, width), :]
 
+    def lag_rows(fixed_ref, moving_ref, lags, shift_of):
         def body(i, accs):
             t = pl.multiple_of(i * 8, 8)
-            left = l_ref[pl.ds(t, 8), :]
+            fixed = fixed_ref[MAXLAG % 8, pl.ds(t + 8 * (MAXLAG // 8), 8), :]
             return tuple(
-                a + left * shifted_ref[k % 8, pl.ds(t + 8 * (k // 8), 8), :]
+                a + fixed * moving_ref[shift_of(k) % 8, pl.ds(t + 8 * (shift_of(k) // 8), 8), :]
                 for a, k in zip(accs, lags)
             )
 
@@ -37,12 +38,21 @@
         )
         for a, k in zip(accs, lags):
             lags_ref[pl.ds(k, 1), :] = jnp.sum(a, axis=0, keepdims=True)
+
+    for first in range(0, MAXLAG, KCHUNK):
+        lag_rows(left_ref, right_ref, list(range(first, min(first + KCHUNK, MAXLAG))), lambda k: k)
+    for first in range(MAXLAG, NLAG, KCHUNK):
+        lag_rows(
+            right_ref, left_ref, list(range(first, min(first + KCHUNK, NLAG))),
+            lambda k: 2 * MAXLAG - k,
+        )
     lags_ref[pl.ds(NLAG, LANES - NLAG), :] = jnp.zeros((LANES - NLAG, LANES), jnp.float32)
     o_ref[...] = lags_ref[...].T
 
 
 def lagged_products(left_t, right_t):
     pairs = left_t.shape[1]
+    bins = left_t.shape[0] - MAXLAG - WINDOW_PAD
     return pl.pallas_call(
         corr_kernel,
         grid=(pairs // LANES,),
@@ -53,11 +63,12 @@
         out_specs=pl.BlockSpec((LANES, LANES), lambda j: (j, 0)),
         out_shape=jax.ShapeDtypeStruct((pairs, LANES), jnp.float32),
         scratch_shapes=[
-            pltpu.VMEM((8, left_t.shape[0] + 96, LANES), jnp.float32),
+            pltpu.VMEM((8, left_t.shape[0] - 8, LANES), jnp.float32),
+            pltpu.VMEM((8, left_t.shape[0] - 8, LANES), jnp.float32),
             pltpu.VMEM((LANES, LANES), jnp.float32),
         ],
         cost_estimate=pl.CostEstimate(
-            flops=2 * NLAG * pairs * left_t.shape[0],
+            flops=2 * NLAG * pairs * bins,
             bytes_accessed=4 * pairs * (left_t.shape[0] + right_t.shape[0] + LANES),
             transcendentals=0,
         ),
@@ -97,9 +108,7 @@
     )
 
     to_next = [(i, i + 1) for i in range(shard_count - 1)]
-    to_prev = [(i + 1, i) for i in range(shard_count - 1)]
     left_raw = lax.ppermute(trains[:, BINS_DEV - MAXLAG :], "tm", to_next)
-    right_raw = lax.ppermute(trains[:, :MAXLAG], "tm", to_prev)
 
     totals = summed_over(jnp.sum(trains, axis=1), "tm")
     means = totals / float(BINS_DEV * shard_count)
@@ -107,21 +116,19 @@
     def centre(x):
         return (x - means[:, None]).astype(jnp.bfloat16)
 
-    zero = jnp.zeros((), jnp.bfloat16)
-    left_halo = jnp.where(shard_index > 0, centre(left_raw), zero)
-    right_halo = jnp.where(shard_index < shard_count - 1, centre(right_raw), zero)
-    centred = centre(trains)
-    tail_pad = jnp.zeros((U_GRP, 4), jnp.bfloat16)
-    padded_own = jnp.concatenate([left_halo, centred, right_halo, tail_pad], axis=1)
+    left_halo = jnp.where(shard_index > 0, centre(left_raw), jnp.zeros((), jnp.bfloat16))
+    window_own = jnp.concatenate(
+        [left_halo, centre(trains), jnp.zeros((U_GRP, WINDOW_PAD), jnp.bfloat16)], axis=1
+    )
     border = lax.ppermute(
-        padded_own[:BORDER], "chan", [(i + 1, i) for i in range(group_count - 1)]
+        window_own[:BORDER], "chan", [(i + 1, i) for i in range(group_count - 1)]
     )
-    padded = jnp.concatenate([padded_own, border], axis=0)
+    window = jnp.concatenate([window_own, border], axis=0)
 
     first_units = pair_units[0] - group_index * U_GRP
     second_units = pair_units[1] - group_index * U_GRP
-    left_t = gather_columns(centred, first_units)
-    right_t = gather_columns(padded, second_units)
+    left_t = gather_columns(window_own, first_units)
+    right_t = gather_columns(window, second_units)
     partial = lagged_products(left_t, right_t)
 
     per_shard = partial.shape[0] // shard_count

time: 75.9 us -> 71.1 us (0.937)
  blocking collectives: 27.9 us -> 23.6 us
  starting transfers between devices: 22.2 us -> 20.8 us
  waiting for transfers between devices: 6.2 us -> 7.24 us
    all_to_all x1, blocking collectives: 27.9 us -> 23.6 us  [local(): summed = jnp.sum(lax.all_to_all(blocks, 'tm', 0, 0, tiled=False), axis=0)]
    ppermute x2 -> x1, starting transfers between devices: 5.34 us -> 3.91 us  [local(): lax.ppermute(window_own[:BORDER], 'chan', [(i + 1, i) for i in range(grou...]
    all_to_all x1, waiting for transfers between devices: 4.29 us -> 5.59 us  [summed_over(): return jnp.sum(lax.all_to_all(spread, axis, 0, 0, tiled=False), axis=0)]
    ppermute x2 -> x1, waiting for transfers between devices: 1.91 us -> 1.65 us  [local(): lax.ppermute(window_own[:BORDER], 'chan', [(i + 1, i) for i in range(grou...]
  transfers between devices with their start and end apart: 4 -> 3, of which waited for: 2 -> 2; matrix products, arithmetic and copies ran while one was open for 2% -> 2% of each run, Pallas kernels for 0% -> 0%
where the time goes in v5:
time: 71.1 us; the launch traced here: 70.4 us
  blocking collectives  23.6 us (33%)
  starting transfers between devices  20.8 us (29%)
  Pallas kernels  9.76 us (14%)
  waiting for transfers between devices  7.24 us (10%)
  matrix products  5.25 us (7%)
  other arithmetic  2.46 us (3%)
  local copies, waits for them, and re-layouts  1.28 us (2%)
    all_to_all x1, blocking collectives, local(): summed = jnp.sum(lax.all_to_all(blocks, 'tm', 0, 0, tiled=False), axis=0)  23.6 us
    all_to_all x1, starting transfers between devices, summed_over(): return jnp.sum(lax.all_to_all(spread, axis, 0, 0, tiled=False), axis=0)  13.7 us
    pallas_call x1, Pallas kernels, lagged_products(): pl.pallas_call(corr_kernel, grid=(pairs // LANES,), in_specs=[pl.BlockSpe...  9.76 us
    all_to_all x1, waiting for transfers between devices, summed_over(): return jnp.sum(lax.all_to_all(spread, axis, 0, 0, tiled=False), axis=0)  5.59 us
    ppermute x1, starting transfers between devices, local(): lax.ppermute(window_own[:BORDER], 'chan', [(i + 1, i) for i in range(grou...  3.91 us
    dot_general x2, matrix products, gather_columns(): lax.dot_general(rows, onehot.astype(rows.dtype), (((0,), (0,)), ((), ()))...  3.32 us
    ppermute x1, starting transfers between devices, local(): left_raw = lax.ppermute(trains[:, BINS_DEV - MAXLAG:], 'tm', to_next)  3.14 us
    dot_general x1, matrix products, local(): lax.dot_general(unit_onehot, weighted, (((1,), (1,)), ((), ())), preferre...  1.93 us
  transfers between devices with their start and end apart: 3, of which 2 were waited for; matrix products, arithmetic and copies ran while one was open for 2% of the time, Pallas kernels for 0%

profile of v5, /device:TPU:1, one launch (start us, length us, event | category | flops | bytes accessed | tf_op | source)
XLA Modules:
  0.0 70.4 jit_solution(1021537385492381029)
XLA Ops:
  0.0 0.8 %reduce.1 = bf16[4096]{0:T(1024)(128)(2,1)S(1)} reduce(bf16[1,4096]{1,0:T(2,128)(2,1)} %param.6, bf16[]{:T(256)} %constant.28), dimensions={0}, to_apply=%param.6.reduce_sub_computation | reduce | bytes 16386 | tf_op args[2]
  0.8 0.7 %broadcast_subtract_fusion = s32[1,4096]{1,0:T(1,128)S(1)} fusion(s32[1,4096]{1,0:T(1,128)} %param.5, s32[]{:T(128)S(6)} %mul.8), kind=kLoop, calls=%fused_computation.32 | loop fusion | flops 4096 | bytes 32772 | tf_op jit(solution)/shard_map/sub | solution.py:99
  1.5 0.8 %divide_subtract_fusion = s32[1,4096]{1,0:T(1,128)S(1)} fusion(s32[1,4096]{1,0:T(1,128)} %param.4, s32[]{:T(128)S(6)} %mul.9), kind=kLoop, calls=%fused_computation.31 | loop fusion | flops 8192 | bytes 32772 | tf_op jit(solution)/shard_map/sub | solution.py:98
  2.3 0.0 copy-start
  2.3 1.9 %fusion.27 = (f32[384]{0:T(512)S(1)}, f32[384,256]{0,1:T(8,128)S(1)}) fusion(s32[4096]{0:T(1024)S(1)} %bitcast.9, bf16[4096]{0:T(1024)(128)(2,1)S(1)} %reduce.1, s32[4096]{0:T(1024)S(1)} %bitcast.8), kind=kOutput, calls=%fused_computation.39 | convolution fusion | flops 809074304 | bytes 435712 | tf_op jit(solution)/shard_map/dot_general | solution.py:106
  4.2 0.6 broadcast_in_dim.34
  4.9 13.7 %all-to-all-start = ((f32[32,1,384]{2,1,0:T(1,128)}), f32[32,1,384]{2,1,0:T(1,128)S(1)}, u32[]{:S(2)}, u32[]{:S(2)}) async-start(f32[32,1,384]{2,1,0:T(1,128)} %broadcast_in_dim.34), calls=%async_computation | async-start | bytes 98304 | tf_op jit(solution)/shard_map/all_to_all | solution.py:81
  18.6 3.1 %collective-permute-start = (f32[384,50]{0,1:T(8,128)S(1)}, f32[384,50]{0,1:T(8,128)S(1)}, u32[]{:S(2)}, u32[]{:S(2)}) collective-permute-start(f32[384,50]{0,1:T(8,128)S(1)} %slice.20), channel_id=1, source_target_pairs={{0,1},{1,2},{2,3},{3,4},{4,5},{5,6},{6,7},{7,8},{8,9},{9,10},{10,1... | collective-permute-start | bytes 230408 | tf_op jit(solution)/shard_map/ppermute | solution.py:111
  21.7 0.0 copy-done
  21.8 5.6 %all-to-all-done = f32[32,1,384]{2,1,0:T(1,128)S(1)} async-done(((f32[32,1,384]{2,1,0:T(1,128)}), f32[32,1,384]{2,1,0:T(1,128)S(1)}, u32[]{:S(2)}, u32[]{:S(2)}) %all-to-all-start) | async-done | bytes 49184 | tf_op jit(solution)/shard_map/all_to_all | solution.py:81
  27.4 0.1 reduce_sum.28
  27.5 0.0 collective-permute-done
  27.6 3.9 %collective-permute-start.1 = (bf16[64,312]{0,1:T(8,128)(2,1)S(1)}, bf16[64,312]{0,1:T(8,128)(2,1)S(1)}, u32[]{:S(2)}, u32[]{:S(2)}) collective-permute-start(bf16[64,312]{0,1:T(8,128)(2,1)S(1)} %pad_maximum_fusion), channel_id=1, source_target_pairs={{32,0},{64,32},{96,64},{128,96},{160,128},{192,160},{224,192},{256... | collective-permute-start | bytes 119816 | tf_op jit(solution)/shard_map/ppermute | solution.py:123
  31.5 1.6 %fusion.6.l_ref = f32[312,1024]{1,0:T(8,128)} fusion(s32[1024]{0:T(1024)S(1)} %bitcast.11, bf16[384,6]{0,1:T(8,128)(2,1)S(1)} %broadcast_in_dim.36, bf16[384,256]{0,1:T(8,128)(2,1)S(1)} %subtract_convert_fusion, bf16[384,50]{0,1:T(8,128)(2,1)S(1)} %fusion.23), kind=kOutput, calls=%fused_computation.9 | convolution fusion | flops 246478848 | bytes 1521664 | tf_op jit(solution)/shard_map/dot_general | solution.py:86
  33.1 1.6 %collective-permute-done.1 = bf16[64,312]{0,1:T(8,128)(2,1)S(1)} collective-permute-done((bf16[64,312]{0,1:T(8,128)(2,1)S(1)}, bf16[64,312]{0,1:T(8,128)(2,1)S(1)}, u32[]{:S(2)}, u32[]{:S(2)}) %collective-permute-start.1) | collective-permute-done | bytes 39968 | tf_op jit(solution)/shard_map/ppermute | solution.py:123
  34.8 1.7 %fusion.5.r_ref = f32[312,1024]{1,0:T(8,128)} fusion(s32[1024]{0:T(1024)S(1)} %bitcast.10, bf16[64,312]{0,1:T(8,128)(2,1)S(1)} %collective-permute-done.1, bf16[384,6]{0,1:T(8,128)(2,1)S(1)} %broadcast_in_dim.36, bf16[384,256]{0,1:T(8,128)(2,1)S(1)} %subtract_convert_fusion, bf16[384,50]{0,1:T(8,128)(2,1)S(1)} %fusion.23), kind=kOutput, calls=%fused_computation.7 | convolution fusion | flops 287838208 | bytes 1561600 | tf_op jit(solution)/shard_map/dot_general | solution.py:86
  36.5 9.8 %shard_map.46 = f32[1024,128]{1,0:T(8,128)} custom-call(f32[312,1024]{1,0:T(8,128)} %fusion.6.l_ref, f32[312,1024]{1,0:T(8,128)} %fusion.5.r_ref), custom_call_target="tpu_custom_call" | custom-call | flops 52953088 | bytes 3080192 | tf_op jit(solution)/shard_map/pallas_call | solution.py:56
  46.2 23.6 %all_to_all.11 = f32[32,32,128]{2,1,0:T(8,128)S(1)} all-to-all(f32[32,32,128]{2,1,0:T(8,128)} %bitcast.7), channel_id=1, replica_groups=mesh['chan'=16,'tm'=32] {'tm'}, dimensions={0} | all-to-all | bytes 1048576 | tf_op jit(solution)/shard_map/all_to_all | solution.py:136
  69.8 0.6 slice_bitcast_fusion
  (8 shorter events, 0.1 us)
Async XLA Ops:
  2.3 19.5 %copy-start = (s32[2,1024]{1,0:T(2,128)S(1)}, s32[2,1024]{1,0:T(2,128)}, u32[]{:S(2)}) copy-start(s32[2,1024]{1,0:T(2,128)} %param.7) | copy-start | bytes 24580
  4.9 22.5 %all-to-all-start = ((f32[32,1,384]{2,1,0:T(1,128)}), f32[32,1,384]{2,1,0:T(1,128)S(1)}, u32[]{:S(2)}, u32[]{:S(2)}) async-start(f32[32,1,384]{2,1,0:T(1,128)} %broadcast_in_dim.34), calls=%async_computation | async-start | bytes 98304 | tf_op jit(solution)/shard_map/all_to_all | solution.py:81
  18.6 8.9 %collective-permute-start = (f32[384,50]{0,1:T(8,128)S(1)}, f32[384,50]{0,1:T(8,128)S(1)}, u32[]{:S(2)}, u32[]{:S(2)}) collective-permute-start(f32[384,50]{0,1:T(8,128)S(1)} %slice.20), channel_id=1, source_target_pairs={{0,1},{1,2},{2,3},{3,4},{4,5},{5,6},{6,7},{7,8},{8,9},{9,10},{10,1... | collective-permute-start | bytes 230408 | tf_op jit(solution)/shard_map/ppermute | solution.py:111
  27.6 7.2 %collective-permute-start.1 = (bf16[64,312]{0,1:T(8,128)(2,1)S(1)}, bf16[64,312]{0,1:T(8,128)(2,1)S(1)}, u32[]{:S(2)}, u32[]{:S(2)}) collective-permute-start(bf16[64,312]{0,1:T(8,128)(2,1)S(1)} %pad_maximum_fusion), channel_id=1, source_target_pairs={{32,0},{64,32},{96,64},{128,96},{160,128},{192,160},{224,192},{256... | collective-permute-start | bytes 119816 | tf_op jit(solution)/shard_map/ppermute | solution.py:123

commit v6 on v5

--- a/solution.py
+++ b/solution.py
@@ -75,11 +75,31 @@
     )(left_t, right_t)
 
 
-def summed_over(values, axis):
-    peers = lax.axis_size(axis)
-    spread = jnp.broadcast_to(values[None], (peers,) + values.shape)
-    return jnp.sum(lax.all_to_all(spread, axis, 0, 0, tiled=False), axis=0)
+def trains_kernel(offsets_ref, sample_ref, unit_ref, amp_ref, trains_ref, spread_ref):
+    spikes = sample_ref.shape[1]
+    bins = lax.div(sample_ref[...], SPB) - offsets_ref[1]
+    within = unit_ref[...] - offsets_ref[0]
+    amp = amp_ref[...]
+    zero = jnp.zeros((), jnp.bfloat16)
+    one = jnp.ones((), jnp.bfloat16)
+    unit_onehot = jnp.where(within == lax.broadcasted_iota(jnp.int32, (U_GRP, spikes), 0), one, zero)
+    weighted = jnp.where(bins == lax.broadcasted_iota(jnp.int32, (BINS_DEV, spikes), 0), amp, zero)
+    trains_ref[...] = lax.dot_general(unit_onehot, weighted, (((1,), (1,)), ((), ())), preferred_element_type=jnp.float32)
+    sums = lax.dot_general(jnp.broadcast_to(amp, (8, spikes)), unit_onehot, (((1,), (1,)), ((), ())), preferred_element_type=jnp.float32)
+    spread_ref[...] = jnp.broadcast_to(sums[0:1], spread_ref.shape)
 
+def trains_and_sums(offsets, sample, unit, amp, peers):
+    spikes = sample.shape[1]
+    return pl.pallas_call(
+        trains_kernel,
+        in_specs=[pl.BlockSpec(memory_space=pltpu.SMEM)]
+        + [pl.BlockSpec(memory_space=pltpu.VMEM)] * 3,
+        out_specs=[pl.BlockSpec(memory_space=pltpu.VMEM)] * 2,
+        out_shape=[
+            jax.ShapeDtypeStruct((U_GRP, BINS_DEV), jnp.float32),
+            jax.ShapeDtypeStruct((peers, U_GRP), jnp.float32),
+        ],
+    )(offsets, sample, unit, amp)
 
 def gather_columns(rows, index):
     onehot = (lax.broadcasted_iota(jnp.int32, (rows.shape[0], index.shape[0]), 0) == index[None, :])
@@ -95,22 +115,13 @@
     shard_count = lax.axis_size("tm")
     group_count = lax.axis_size("chan")
 
-    bin_index = lax.div(spike_sample, SPB) - shard_index * BINS_DEV
-    within = spike_unit - group_index * U_GRP
-    unit_onehot = (within == lax.broadcasted_iota(jnp.int32, (U_GRP, 1), 0)).astype(jnp.bfloat16)
-    weighted = jnp.where(
-        bin_index == lax.broadcasted_iota(jnp.int32, (BINS_DEV, 1), 0),
-        spike_amp,
-        jnp.zeros((), jnp.bfloat16),
-    )
-    trains = lax.dot_general(
-        unit_onehot, weighted, (((1,), (1,)), ((), ())), preferred_element_type=jnp.float32
-    )
+    offsets = jnp.stack([group_index * U_GRP, shard_index * BINS_DEV]).astype(jnp.int32)
+    trains, spread = trains_and_sums(offsets, spike_sample, spike_unit, spike_amp, shard_count)
 
     to_next = [(i, i + 1) for i in range(shard_count - 1)]
     left_raw = lax.ppermute(trains[:, BINS_DEV - MAXLAG :], "tm", to_next)
 
-    totals = summed_over(jnp.sum(trains, axis=1), "tm")
+    totals = jnp.sum(lax.all_to_all(spread[:, None, :], "tm", 0, 0, tiled=False), axis=(0, 1))
     means = totals / float(BINS_DEV * shard_count)
 
     def centre(x):

time: 71.1 us -> 74.6 us (1.049)
  Pallas kernels: 9.76 us -> 13.1 us
  waiting for transfers between devices: 7.24 us -> 4.96 us
  local copies, waits for them, and re-layouts: 1.28 us -> 3.12 us
  blocking collectives: 23.6 us -> 25.4 us
  matrix products: 5.25 us -> 3.56 us
    pallas_call x0 -> x1, Pallas kernels: none -> 3.35 us  [trains_and_sums(): pl.pallas_call(trains_kernel, in_specs=[pl.BlockSpec(memory_space=pltpu.S...]
    dot_general x1 -> x0, matrix products: 1.93 us -> none  [local(): lax.dot_general(unit_onehot, weighted, (((1,), (1,)), ((), ())), preferre...]
    all_to_all x1, waiting for transfers between devices: 5.59 us -> 3.75 us  [local(): lax.all_to_all(spread[:, None, :], 'tm', 0, 0, tiled=False)]
    all_to_all x1, blocking collectives: 23.6 us -> 25.4 us  [local(): summed = jnp.sum(lax.all_to_all(blocks, 'tm', 0, 0, tiled=False), axis=0)]
    sub x2 -> x0, other arithmetic: 1.5 us -> none  [the longest x1 0.76 us: local(): bin_index = lax.div(spike_sample, SPB) - shard_index * BINS_DEV]
    convert_element_type x1, other arithmetic: 0.03 us -> 1.11 us  [centre(): return (x - means[:, None]).astype(jnp.bfloat16)]
    slice x1, local copies, waits for them, and re-layouts: 0.01 us -> 1.03 us  [local(): left_raw = lax.ppermute(trains[:, BINS_DEV - MAXLAG:], 'tm', to_next)]
    broadcast_in_dim x1, local copies, waits for them, and re-layouts: 0.65 us -> 1.46 us  [local(): spread[:, None, :]]
  transfers between devices with their start and end apart: 3 -> 3, of which waited for: 2 -> 2; matrix products, arithmetic and copies ran while one was open for 2% -> 6% of each run, Pallas kernels for 0% -> 0%
where the time goes in v6:
time: 74.6 us; the launch traced here: 74 us
  blocking collectives  25.4 us (34%)
  starting transfers between devices  20.9 us (28%)
  Pallas kernels  13.1 us (18%)
  waiting for transfers between devices  4.96 us (7%)
  matrix products  3.56 us (5%)
  local copies, waits for them, and re-layouts  3.12 us (4%)
  other arithmetic  2.86 us (4%)
    all_to_all x1, blocking collectives, local(): summed = jnp.sum(lax.all_to_all(blocks, 'tm', 0, 0, tiled=False), axis=0)  25.4 us
    all_to_all x1, starting transfers between devices, local(): lax.all_to_all(spread[:, None, :], 'tm', 0, 0, tiled=False)  13.7 us
    pallas_call x1, Pallas kernels, lagged_products(): pl.pallas_call(corr_kernel, grid=(pairs // LANES,), in_specs=[pl.BlockSpe...  9.77 us
    ppermute x1, starting transfers between devices, local(): lax.ppermute(window_own[:BORDER], 'chan', [(i + 1, i) for i in range(grou...  4.04 us
    all_to_all x1, waiting for transfers between devices, local(): lax.all_to_all(spread[:, None, :], 'tm', 0, 0, tiled=False)  3.75 us
    dot_general x2, matrix products, gather_columns(): lax.dot_general(rows, onehot.astype(rows.dtype), (((0,), (0,)), ((), ()))...  3.56 us
    pallas_call x1, Pallas kernels, trains_and_sums(): pl.pallas_call(trains_kernel, in_specs=[pl.BlockSpec(memory_space=pltpu.S...  3.35 us
    ppermute x1, starting transfers between devices, local(): left_raw = lax.ppermute(trains[:, BINS_DEV - MAXLAG:], 'tm', to_next)  3.15 us
  transfers between devices with their start and end apart: 3, of which 2 were waited for; matrix products, arithmetic and copies ran while one was open for 6% of the time, Pallas kernels for 0%

profile of v6, /device:TPU:1, one launch (start us, length us, event | category | flops | bytes accessed | tf_op | source)
XLA Modules:
  0.0 74.0 jit_solution(889590594074916697)
XLA Ops:
  0.0 0.6 pad_add_fusion.offsets_ref
  0.6 3.3 %shard_map.46 = (f32[384,256]{1,0:T(8,128)}, f32[32,384]{1,0:T(8,128)}) custom-call(s32[2]{0:T(128)} %pad_add_fusion.offsets_ref, s32[1,4096]{1,0:T(1,128)} %sample_ref.1, s32[1,4096]{1,0:T(1,128)} %unit_ref.1, bf16[1,4096]{1,0:T(2,128)(2,1)} %amp_ref.1), custom_call_target="tpu_custom_call" | custom-call | tf_op jit(solution)/shard_map/pallas_call | solution.py:93
  4.0 1.5 %copy.5 = f32[32,1,384]{2,1,0:T(1,128)} copy(f32[32,1,384]{2,0,1:T(8,128)} %bitcast.9) | data formatting | bytes 98304 | tf_op jit(solution)/shard_map/broadcast_in_dim | solution.py:124
  5.5 13.7 %all-to-all-start = ((f32[32,1,384]{2,1,0:T(1,128)}), f32[32,1,384]{2,1,0:T(1,128)S(1)}, u32[]{:S(2)}, u32[]{:S(2)}) async-start(f32[32,1,384]{2,1,0:T(1,128)} %copy.5), calls=%async_computation | async-start | bytes 98304 | tf_op jit(solution)/shard_map/all_to_all | solution.py:124
  19.2 1.0 %slice.15 = f32[384,50]{1,0:T(8,128)S(1)} slice(f32[384,256]{1,0:T(8,128)} %get-tuple-element.7), slice={[0:384], [206:256]} | slice | bytes 153600 | tf_op jit(solution)/shard_map/slice | solution.py:122
  20.2 3.1 %collective-permute-start = (f32[384,50]{1,0:T(8,128)S(1)}, f32[384,50]{1,0:T(8,128)S(1)}, u32[]{:S(2)}, u32[]{:S(2)}) collective-permute-start(f32[384,50]{1,0:T(8,128)S(1)} %slice.15), channel_id=1, source_target_pairs={{0,1},{1,2},{2,3},{3,4},{4,5},{5,6},{6,7},{7,8},{8,9},{9,10},{10,1... | collective-permute-start | bytes 230408 | tf_op jit(solution)/shard_map/ppermute | solution.py:122
  23.4 0.8 %slice_subtract_fusion = (s32[1,1024]{1,0:T(1,128)S(1)}, s32[1,1024]{1,0:T(1,128)S(1)}) fusion(s32[2,1024]{1,0:T(2,128)} %param.7, s32[]{:T(128)} %mul.8), kind=kLoop, calls=%fused_computation.23 | loop fusion | flops 2048 | bytes 16388 | tf_op jit(solution)/shard_map/sub | solution.py:140
  24.2 3.8 %all-to-all-done = f32[32,1,384]{2,1,0:T(1,128)S(1)} async-done(((f32[32,1,384]{2,1,0:T(1,128)}), f32[32,1,384]{2,1,0:T(1,128)S(1)}, u32[]{:S(2)}, u32[]{:S(2)}) %all-to-all-start) | async-done | bytes 49184 | tf_op jit(solution)/shard_map/all_to_all | solution.py:124
  27.9 0.1 reduce_sum.18
  28.0 1.1 %subtract_convert_fusion = bf16[384,256]{1,0:T(8,128)(2,1)S(1)} fusion(f32[384,256]{1,0:T(8,128)} %get-tuple-element.7, f32[384]{0:T(512)S(1)} %broadcast_multiply_fusion), kind=kLoop, calls=%fused_computation.6 | loop fusion | flops 196608 | bytes 591360 | tf_op jit(solution)/shard_map/convert_element_type | solution.py:128
  29.1 0.0 collective-permute-done
  29.1 0.1 fusion.16
  29.3 0.1 pad_maximum_fusion
  29.4 4.0 %collective-permute-start.1 = (bf16[64,312]{1,0:T(8,128)(2,1)S(1)}, bf16[64,312]{1,0:T(8,128)(2,1)S(1)}, u32[]{:S(2)}, u32[]{:S(2)}) collective-permute-start(bf16[64,312]{1,0:T(8,128)(2,1)S(1)} %pad_maximum_fusion), channel_id=1, source_target_pairs={{32,0},{64,32},{96,64},{128,96},{160,128},{192,160},{224,192},{256... | collective-permute-start | bytes 119816 | tf_op jit(solution)/shard_map/ppermute | solution.py:134
  33.4 1.7 %fusion.1.l_ref = f32[312,1024]{1,0:T(8,128)} fusion(s32[1024]{0:T(1024)S(1)} %bitcast.11, bf16[384,6]{1,0:T(8,128)(2,1)S(1)} %broadcast_in_dim.16, bf16[384,256]{1,0:T(8,128)(2,1)S(1)} %subtract_convert_fusion, bf16[384,50]{1,0:T(8,128)(2,1)S(1)} %fusion.16), kind=kOutput, calls=%fused_computation.3 | convolution fusion | flops 246478848 | bytes 1521664 | tf_op jit(solution)/shard_map/dot_general | solution.py:106
  35.1 1.2 %collective-permute-done.1 = bf16[64,312]{1,0:T(8,128)(2,1)S(1)} collective-permute-done((bf16[64,312]{1,0:T(8,128)(2,1)S(1)}, bf16[64,312]{1,0:T(8,128)(2,1)S(1)}, u32[]{:S(2)}, u32[]{:S(2)}) %collective-permute-start.1) | collective-permute-done | bytes 39968 | tf_op jit(solution)/shard_map/ppermute | solution.py:134
  36.4 1.8 %fusion.r_ref = f32[312,1024]{1,0:T(8,128)} fusion(s32[1024]{0:T(1024)S(1)} %bitcast.10, bf16[64,312]{1,0:T(8,128)(2,1)S(1)} %collective-permute-done.1, bf16[384,6]{1,0:T(8,128)(2,1)S(1)} %broadcast_in_dim.16, bf16[384,256]{1,0:T(8,128)(2,1)S(1)} %subtract_convert_fusion, bf16[384,50]{1,0:T(8,128)(2,1)S(1)} %fusion.16), kind=kOutput, calls=%fused_computation.1 | convolution fusion | flops 287838208 | bytes 1561600 | tf_op jit(solution)/shard_map/dot_general | solution.py:106
  38.2 9.8 %shard_map.47 = f32[1024,128]{1,0:T(8,128)} custom-call(f32[312,1024]{1,0:T(8,128)} %fusion.1.l_ref, f32[312,1024]{1,0:T(8,128)} %fusion.r_ref), custom_call_target="tpu_custom_call" | custom-call | flops 52953088 | bytes 3080192 | tf_op jit(solution)/shard_map/pallas_call | solution.py:56
  47.9 25.4 %all_to_all.10 = f32[32,32,128]{2,1,0:T(8,128)S(1)} all-to-all(f32[32,32,128]{2,1,0:T(8,128)} %bitcast.8), channel_id=1, replica_groups=mesh['chan'=16,'tm'=32] {'tm'}, dimensions={0} | all-to-all | bytes 1048576 | tf_op jit(solution)/shard_map/all_to_all | solution.py:147
  73.4 0.6 slice_bitcast_fusion
  (3 shorter events, 0.1 us)
Async XLA Ops:
  5.5 22.5 %all-to-all-start = ((f32[32,1,384]{2,1,0:T(1,128)}), f32[32,1,384]{2,1,0:T(1,128)S(1)}, u32[]{:S(2)}, u32[]{:S(2)}) async-start(f32[32,1,384]{2,1,0:T(1,128)} %copy.5), calls=%async_computation | async-start | bytes 98304 | tf_op jit(solution)/shard_map/all_to_all | solution.py:124
  20.2 8.9 %collective-permute-start = (f32[384,50]{1,0:T(8,128)S(1)}, f32[384,50]{1,0:T(8,128)S(1)}, u32[]{:S(2)}, u32[]{:S(2)}) collective-permute-start(f32[384,50]{1,0:T(8,128)S(1)} %slice.15), channel_id=1, source_target_pairs={{0,1},{1,2},{2,3},{3,4},{4,5},{5,6},{6,7},{7,8},{8,9},{9,10},{10,1... | collective-permute-start | bytes 230408 | tf_op jit(solution)/shard_map/ppermute | solution.py:122
  29.4 7.0 %collective-permute-start.1 = (bf16[64,312]{1,0:T(8,128)(2,1)S(1)}, bf16[64,312]{1,0:T(8,128)(2,1)S(1)}, u32[]{:S(2)}, u32[]{:S(2)}) collective-permute-start(bf16[64,312]{1,0:T(8,128)(2,1)S(1)} %pad_maximum_fusion), channel_id=1, source_target_pairs={{32,0},{64,32},{96,64},{128,96},{160,128},{192,160},{224,192},{256... | collective-permute-start | bytes 119816 | tf_op jit(solution)/shard_map/ppermute | solution.py:134

commit v7 on v5

--- a/solution.py
+++ b/solution.py
@@ -103,14 +103,20 @@
         spike_amp,
         jnp.zeros((), jnp.bfloat16),
     )
-    trains = lax.dot_general(
-        unit_onehot, weighted, (((1,), (1,)), ((), ())), preferred_element_type=jnp.float32
+    trains = lax.optimization_barrier(
+        lax.dot_general(
+            unit_onehot, weighted, (((1,), (1,)), ((), ())), preferred_element_type=jnp.float32
+        )
     )
+
+    unit_sums = lax.dot_general(
+        unit_onehot, spike_amp, (((1,), (1,)), ((), ())), preferred_element_type=jnp.float32
+    )[:, 0]
 
     to_next = [(i, i + 1) for i in range(shard_count - 1)]
     left_raw = lax.ppermute(trains[:, BINS_DEV - MAXLAG :], "tm", to_next)
 
-    totals = summed_over(jnp.sum(trains, axis=1), "tm")
+    totals = summed_over(unit_sums, "tm")
     means = totals / float(BINS_DEV * shard_count)
 
     def centre(x):

time: 71.1 us -> 72.9 us (1.025)
  blocking collectives: 23.6 us -> 27 us
  waiting for transfers between devices: 7.24 us -> 5.07 us
  matrix products: 5.25 us -> 6.8 us
  other arithmetic: 2.46 us -> 1.3 us
    all_to_all x1, blocking collectives: 23.6 us -> 27 us  [local(): summed = jnp.sum(lax.all_to_all(blocks, 'tm', 0, 0, tiled=False), axis=0)]
    dot_general x0 -> x1, matrix products: none -> 1.82 us  [local(): lax.dot_general(unit_onehot, spike_amp, (((1,), (1,)), ((), ())), preferr...]
    all_to_all x1, waiting for transfers between devices: 5.59 us -> 3.85 us  [summed_over(): return jnp.sum(lax.all_to_all(spread, axis, 0, 0, tiled=False), axis=0)]
  transfers between devices with their start and end apart: 3 -> 3, of which waited for: 2 -> 2; matrix products, arithmetic and copies ran while one was open for 2% -> 5% of each run, Pallas kernels for 0% -> 0%
where the time goes in v7:
time: 72.9 us; the launch traced here: 72.4 us
  blocking collectives  27 us (37%)
  starting transfers between devices  20.9 us (29%)
  Pallas kernels  9.76 us (13%)
  matrix products  6.8 us (9%)
  waiting for transfers between devices  5.07 us (7%)
  local copies, waits for them, and re-layouts  1.39 us (2%)
  other arithmetic  1.3 us (2%)
    all_to_all x1, blocking collectives, local(): summed = jnp.sum(lax.all_to_all(blocks, 'tm', 0, 0, tiled=False), axis=0)  27 us
    all_to_all x1, starting transfers between devices, summed_over(): return jnp.sum(lax.all_to_all(spread, axis, 0, 0, tiled=False), axis=0)  13.7 us
    pallas_call x1, Pallas kernels, lagged_products(): pl.pallas_call(corr_kernel, grid=(pairs // LANES,), in_specs=[pl.BlockSpe...  9.76 us
    ppermute x1, starting transfers between devices, local(): lax.ppermute(window_own[:BORDER], 'chan', [(i + 1, i) for i in range(grou...  4.04 us
    all_to_all x1, waiting for transfers between devices, summed_over(): return jnp.sum(lax.all_to_all(spread, axis, 0, 0, tiled=False), axis=0)  3.85 us
    dot_general x2, matrix products, gather_columns(): lax.dot_general(rows, onehot.astype(rows.dtype), (((0,), (0,)), ((), ()))...  3.54 us
    ppermute x1, starting transfers between devices, local(): left_raw = lax.ppermute(trains[:, BINS_DEV - MAXLAG:], 'tm', to_next)  3.15 us
    dot_general x1, matrix products, local(): lax.dot_general(unit_onehot, spike_amp, (((1,), (1,)), ((), ())), preferr...  1.82 us
  transfers between devices with their start and end apart: 3, of which 2 were waited for; matrix products, arithmetic and copies ran while one was open for 5% of the time, Pallas kernels for 0%

profile of v7, /device:TPU:1, one launch (start us, length us, event | category | flops | bytes accessed | tf_op | source)
XLA Modules:
  0.0 72.4 jit_solution(8951444874465586875)
XLA Ops:
  0.0 0.0 copy-start
  0.0 0.0 copy-start.1
  0.0 0.7 %broadcast_subtract_fusion = s32[1,4096]{1,0:T(1,128)S(1)} fusion(s32[1,4096]{1,0:T(1,128)} %param.5, s32[]{:T(128)S(6)} %mul.8), kind=kLoop, calls=%fused_computation.36 | loop fusion | flops 4096 | bytes 32772 | tf_op jit(solution)/shard_map/sub | solution.py:99
  0.8 1.8 %fusion.9 = f32[384]{0:T(512)S(1)} fusion(s32[4096]{0:T(1024)S(1)} %bitcast.11, bf16[1,4096]{1,0:T(2,128)(2,1)} %param.6), kind=kOutput, calls=%fused_computation.12 | convolution fusion | flops 4718592 | bytes 26112 | tf_op jit(solution)/shard_map/dot_general | solution.py:112
  2.6 0.6 broadcast_in_dim.33
  3.2 13.7 %all-to-all-start = ((f32[32,1,384]{2,1,0:T(1,128)}), f32[32,1,384]{2,1,0:T(1,128)S(1)}, u32[]{:S(2)}, u32[]{:S(2)}) async-start(f32[32,1,384]{2,1,0:T(1,128)} %broadcast_in_dim.33), calls=%async_computation | async-start | bytes 98304 | tf_op jit(solution)/shard_map/all_to_all | solution.py:81
  16.9 0.0 copy-done
  17.0 0.1 reduce.1
  17.0 0.0 copy-done.1
  17.1 0.0 copy-start.2
  17.1 1.4 %fusion.1 = f32[384,256]{1,0:T(8,128)S(1)} fusion(s32[4096]{0:T(1024)S(1)} %bitcast.12, s32[4096]{0:T(1024)S(1)} %bitcast.13, bf16[4096]{0:T(1024)(128)(2,1)S(1)} %reduce.1), kind=kOutput, calls=%fused_computation.2 | convolution fusion | flops 808976384 | bytes 434176 | tf_op jit(solution)/shard_map/dot_general | solution.py:107
  18.5 0.1 slice.20
  18.7 3.1 %collective-permute-start = (f32[384,50]{1,0:T(8,128)S(1)}, f32[384,50]{1,0:T(8,128)S(1)}, u32[]{:S(2)}, u32[]{:S(2)}) collective-permute-start(f32[384,50]{1,0:T(8,128)S(1)} %slice.20), channel_id=1, source_target_pairs={{0,1},{1,2},{2,3},{3,4},{4,5},{5,6},{6,7},{7,8},{8,9},{9,10},{10,1... | collective-permute-start | bytes 230408 | tf_op jit(solution)/shard_map/ppermute | solution.py:117
  21.8 0.0 copy-done.2
  21.8 3.8 %all-to-all-done = f32[32,1,384]{2,1,0:T(1,128)S(1)} async-done(((f32[32,1,384]{2,1,0:T(1,128)}), f32[32,1,384]{2,1,0:T(1,128)S(1)}, u32[]{:S(2)}, u32[]{:S(2)}) %all-to-all-start) | async-done | bytes 49184 | tf_op jit(solution)/shard_map/all_to_all | solution.py:81
  25.7 0.1 reduce_sum.18
  25.8 0.1 subtract_convert_fusion
  25.9 0.0 collective-permute-done
  25.9 0.1 fusion.26
  26.1 0.1 pad_maximum_fusion
  26.1 4.0 %collective-permute-start.1 = (bf16[64,312]{1,0:T(8,128)(2,1)S(1)}, bf16[64,312]{1,0:T(8,128)(2,1)S(1)}, u32[]{:S(2)}, u32[]{:S(2)}) collective-permute-start(bf16[64,312]{1,0:T(8,128)(2,1)S(1)} %pad_maximum_fusion), channel_id=1, source_target_pairs={{32,0},{64,32},{96,64},{128,96},{160,128},{192,160},{224,192},{256... | collective-permute-start | bytes 119816 | tf_op jit(solution)/shard_map/ppermute | solution.py:129
  30.2 1.7 %fusion.8.l_ref = f32[312,1024]{1,0:T(8,128)} fusion(s32[1024]{0:T(1024)S(1)} %bitcast.15, bf16[384,6]{1,0:T(8,128)(2,1)S(1)} %broadcast_in_dim.35, bf16[384,256]{1,0:T(8,128)(2,1)S(1)} %subtract_convert_fusion, bf16[384,50]{1,0:T(8,128)(2,1)S(1)} %fusion.26), kind=kOutput, calls=%fused_computation.11 | convolution fusion | flops 246478848 | bytes 1521664 | tf_op jit(solution)/shard_map/dot_general | solution.py:86
  31.9 1.2 %collective-permute-done.1 = bf16[64,312]{1,0:T(8,128)(2,1)S(1)} collective-permute-done((bf16[64,312]{1,0:T(8,128)(2,1)S(1)}, bf16[64,312]{1,0:T(8,128)(2,1)S(1)}, u32[]{:S(2)}, u32[]{:S(2)}) %collective-permute-start.1) | collective-permute-done | bytes 39968 | tf_op jit(solution)/shard_map/ppermute | solution.py:129
  33.1 1.8 %fusion.7.r_ref = f32[312,1024]{1,0:T(8,128)} fusion(s32[1024]{0:T(1024)S(1)} %bitcast.14, bf16[64,312]{1,0:T(8,128)(2,1)S(1)} %collective-permute-done.1, bf16[384,6]{1,0:T(8,128)(2,1)S(1)} %broadcast_in_dim.35, bf16[384,256]{1,0:T(8,128)(2,1)S(1)} %subtract_convert_fusion, bf16[384,50]{1,0:T(8,128)(2,1)S(1)} %fusion.26), kind=kOutput, calls=%fused_computation.9 | convolution fusion | flops 287838208 | bytes 1561600 | tf_op jit(solution)/shard_map/dot_general | solution.py:86
  35.0 9.8 %shard_map.46 = f32[1024,128]{1,0:T(8,128)} custom-call(f32[312,1024]{1,0:T(8,128)} %fusion.8.l_ref, f32[312,1024]{1,0:T(8,128)} %fusion.7.r_ref), custom_call_target="tpu_custom_call" | custom-call | flops 52953088 | bytes 3080192 | tf_op jit(solution)/shard_map/pallas_call | solution.py:56
  44.7 27.0 %all_to_all.11 = f32[32,32,128]{2,1,0:T(8,128)S(1)} all-to-all(f32[32,32,128]{2,1,0:T(8,128)} %bitcast.10), channel_id=1, replica_groups=mesh['chan'=16,'tm'=32] {'tm'}, dimensions={0} | all-to-all | bytes 1048576 | tf_op jit(solution)/shard_map/all_to_all | solution.py:142
  71.8 0.6 slice_bitcast_fusion
  (5 shorter events, 0.1 us)
Async XLA Ops:
  0.0 16.9 %copy-start = (bf16[1,4096]{1,0:T(2,128)(2,1)S(1)}, bf16[1,4096]{1,0:T(2,128)(2,1)}, u32[]{:S(2)}) copy-start(bf16[1,4096]{1,0:T(2,128)(2,1)} %param.6) | copy-start | bytes 24580
  0.0 17.0 %copy-start.1 = (s32[1,4096]{1,0:T(1,128)S(1)}, s32[1,4096]{1,0:T(1,128)}, u32[]{:S(2)}) copy-start(s32[1,4096]{1,0:T(1,128)} %param.4) | copy-start | bytes 49156
  3.2 22.5 %all-to-all-start = ((f32[32,1,384]{2,1,0:T(1,128)}), f32[32,1,384]{2,1,0:T(1,128)S(1)}, u32[]{:S(2)}, u32[]{:S(2)}) async-start(f32[32,1,384]{2,1,0:T(1,128)} %broadcast_in_dim.33), calls=%async_computation | async-start | bytes 98304 | tf_op jit(solution)/shard_map/all_to_all | solution.py:81
  17.1 4.7 %copy-start.2 = (s32[2,1024]{1,0:T(2,128)S(1)}, s32[2,1024]{1,0:T(2,128)}, u32[]{:S(2)}) copy-start(s32[2,1024]{1,0:T(2,128)} %param.7) | copy-start | bytes 24580
  18.7 7.2 %collective-permute-start = (f32[384,50]{1,0:T(8,128)S(1)}, f32[384,50]{1,0:T(8,128)S(1)}, u32[]{:S(2)}, u32[]{:S(2)}) collective-permute-start(f32[384,50]{1,0:T(8,128)S(1)} %slice.20), channel_id=1, source_target_pairs={{0,1},{1,2},{2,3},{3,4},{4,5},{5,6},{6,7},{7,8},{8,9},{9,10},{10,1... | collective-permute-start | bytes 230408 | tf_op jit(solution)/shard_map/ppermute | solution.py:117
  26.1 7.0 %collective-permute-start.1 = (bf16[64,312]{1,0:T(8,128)(2,1)S(1)}, bf16[64,312]{1,0:T(8,128)(2,1)S(1)}, u32[]{:S(2)}, u32[]{:S(2)}) collective-permute-start(bf16[64,312]{1,0:T(8,128)(2,1)S(1)} %pad_maximum_fusion), channel_id=1, source_target_pairs={{32,0},{64,32},{96,64},{128,96},{160,128},{192,160},{224,192},{256... | collective-permute-start | bytes 119816 | tf_op jit(solution)/shard_map/ppermute | solution.py:129

commit v8 on v7

--- a/solution.py
+++ b/solution.py
@@ -16,7 +16,14 @@
 WINDOW_PAD = 6
 
 
-def corr_kernel(l_ref, r_ref, o_ref, left_ref, right_ref, lags_ref):
+def corr_kernel(
+    own_ref, all_ref, first_ref, second_ref, o_ref, l_ref, r_ref, left_ref, right_ref, lags_ref
+):
+    for units_ref, index_ref, out_ref in ((own_ref, first_ref, l_ref), (all_ref, second_ref, r_ref)):
+        onehot = lax.broadcasted_iota(jnp.int32, (units_ref.shape[1], LANES), 0) == index_ref[...]
+        out_ref[...] = jnp.dot(
+            units_ref[...], onehot.astype(units_ref.dtype), preferred_element_type=jnp.float32
+        )
     steps = (l_ref.shape[0] - MAXLAG) // 8
     width = left_ref.shape[1]
     for r in range(8):
@@ -50,43 +57,40 @@
     o_ref[...] = lags_ref[...].T
 
 
-def lagged_products(left_t, right_t):
-    pairs = left_t.shape[1]
-    bins = left_t.shape[0] - MAXLAG - WINDOW_PAD
+def lagged_products(own_t, all_t, first_units, second_units):
+    pairs = first_units.shape[1]
+    window = own_t.shape[0]
+    bins = window - MAXLAG - WINDOW_PAD
     return pl.pallas_call(
         corr_kernel,
         grid=(pairs // LANES,),
         in_specs=[
-            pl.BlockSpec((left_t.shape[0], LANES), lambda j: (0, j)),
-            pl.BlockSpec((right_t.shape[0], LANES), lambda j: (0, j)),
+            pl.BlockSpec(own_t.shape, lambda j: (0, 0)),
+            pl.BlockSpec(all_t.shape, lambda j: (0, 0)),
+            pl.BlockSpec((1, LANES), lambda j: (0, j)),
+            pl.BlockSpec((1, LANES), lambda j: (0, j)),
         ],
         out_specs=pl.BlockSpec((LANES, LANES), lambda j: (j, 0)),
         out_shape=jax.ShapeDtypeStruct((pairs, LANES), jnp.float32),
         scratch_shapes=[
-            pltpu.VMEM((8, left_t.shape[0] - 8, LANES), jnp.float32),
-            pltpu.VMEM((8, left_t.shape[0] - 8, LANES), jnp.float32),
+            pltpu.VMEM((window, LANES), jnp.float32),
+            pltpu.VMEM((window, LANES), jnp.float32),
+            pltpu.VMEM((8, window - 8, LANES), jnp.float32),
+            pltpu.VMEM((8, window - 8, LANES), jnp.float32),
             pltpu.VMEM((LANES, LANES), jnp.float32),
         ],
         cost_estimate=pl.CostEstimate(
-            flops=2 * NLAG * pairs * bins,
-            bytes_accessed=4 * pairs * (left_t.shape[0] + right_t.shape[0] + LANES),
+            flops=2 * pairs * (NLAG * bins + window * (own_t.shape[1] + all_t.shape[1])),
+            bytes_accessed=2 * window * (own_t.shape[1] + all_t.shape[1]) + 4 * pairs * (2 + LANES),
             transcendentals=0,
         ),
-    )(left_t, right_t)
+    )(own_t, all_t, first_units, second_units)
 
 
 def summed_over(values, axis):
     peers = lax.axis_size(axis)
     spread = jnp.broadcast_to(values[None], (peers,) + values.shape)
     return jnp.sum(lax.all_to_all(spread, axis, 0, 0, tiled=False), axis=0)
-
-
-def gather_columns(rows, index):
-    onehot = (lax.broadcasted_iota(jnp.int32, (rows.shape[0], index.shape[0]), 0) == index[None, :])
-    return lax.dot_general(
-        rows, onehot.astype(rows.dtype), (((0,), (0,)), ((), ())),
-        preferred_element_type=jnp.float32,
-    )
 
 
 def local(spike_sample, spike_unit, spike_amp, pair_units):
@@ -105,7 +109,7 @@
     )
     trains = lax.optimization_barrier(
         lax.dot_general(
-            unit_onehot, weighted, (((1,), (1,)), ((), ())), preferred_element_type=jnp.float32
+            weighted, unit_onehot, (((1,), (1,)), ((), ())), preferred_element_type=jnp.float32
         )
     )
 
@@ -114,28 +118,26 @@
     )[:, 0]
 
     to_next = [(i, i + 1) for i in range(shard_count - 1)]
-    left_raw = lax.ppermute(trains[:, BINS_DEV - MAXLAG :], "tm", to_next)
+    left_raw = lax.ppermute(trains[BINS_DEV - MAXLAG :], "tm", to_next)
 
     totals = summed_over(unit_sums, "tm")
     means = totals / float(BINS_DEV * shard_count)
 
     def centre(x):
-        return (x - means[:, None]).astype(jnp.bfloat16)
+        return (x - means[None, :]).astype(jnp.bfloat16)
 
     left_halo = jnp.where(shard_index > 0, centre(left_raw), jnp.zeros((), jnp.bfloat16))
     window_own = jnp.concatenate(
-        [left_halo, centre(trains), jnp.zeros((U_GRP, WINDOW_PAD), jnp.bfloat16)], axis=1
+        [left_halo, centre(trains), jnp.zeros((WINDOW_PAD, U_GRP), jnp.bfloat16)], axis=0
     )
     border = lax.ppermute(
-        window_own[:BORDER], "chan", [(i + 1, i) for i in range(group_count - 1)]
+        window_own[:, :BORDER], "chan", [(i + 1, i) for i in range(group_count - 1)]
     )
-    window = jnp.concatenate([window_own, border], axis=0)
+    window = jnp.concatenate([window_own, border], axis=1)
 
-    first_units = pair_units[0] - group_index * U_GRP
-    second_units = pair_units[1] - group_index * U_GRP
-    left_t = gather_columns(window_own, first_units)
-    right_t = gather_columns(window, second_units)
-    partial = lagged_products(left_t, right_t)
+    first_units = pair_units[0:1] - group_index * U_GRP
+    second_units = pair_units[1:2] - group_index * U_GRP
+    partial = lagged_products(window_own, window, first_units, second_units)
 
     per_shard = partial.shape[0] // shard_count
     blocks = partial.reshape(shard_count, per_shard, LANES)

time: 72.9 us -> 79 us (1.084)
  Pallas kernels: 9.76 us -> 18.2 us
  matrix products: 6.8 us -> 3.78 us
  blocking collectives: 27 us -> 25.6 us
  waiting for transfers between devices: 5.07 us -> 6.28 us
  other arithmetic: 1.3 us -> 2.45 us
    pallas_call x1, Pallas kernels: 9.76 us -> 18.2 us  [lagged_products(): pl.pallas_call(corr_kernel, grid=(pairs // LANES,), in_specs=[pl.BlockSpe...]
    dot_general x3 -> x1, matrix products: 4.98 us -> 1.91 us  [local(): lax.dot_general(weighted, unit_onehot, (((1,), (1,)), ((), ())), preferre...]
    ppermute x2, waiting for transfers between devices: 1.22 us -> 2.65 us  [the longest x1 2.65 us: local(): lax.ppermute(window_own[:, :BORDER], 'chan', [(i + 1, i) for i in range(g...]
    all_to_all x1, blocking collectives: 27 us -> 25.6 us  [local(): summed = jnp.sum(lax.all_to_all(blocks, 'tm', 0, 0, tiled=False), axis=0)]
    concatenate x0 -> x2, other arithmetic: none -> 0.85 us  [the longest x1 0.79 us: local(): window = jnp.concatenate([window_own, border], axis=1)]
  transfers between devices with their start and end apart: 3 -> 3, of which waited for: 2 -> 2; matrix products, arithmetic and copies ran while one was open for 5% -> 3% of each run, Pallas kernels for 0% -> 0%
where the time goes in v8:
time: 79 us; the launch traced here: 78.5 us
  blocking collectives  25.6 us (32%)
  starting transfers between devices  20.7 us (26%)
  Pallas kernels  18.2 us (23%)
  waiting for transfers between devices  6.28 us (8%)
  matrix products  3.78 us (5%)
  other arithmetic  2.45 us (3%)
  local copies, waits for them, and re-layouts  1.3 us (2%)
    all_to_all x1, blocking collectives, local(): summed = jnp.sum(lax.all_to_all(blocks, 'tm', 0, 0, tiled=False), axis=0)  25.6 us
    pallas_call x1, Pallas kernels, lagged_products(): pl.pallas_call(corr_kernel, grid=(pairs // LANES,), in_specs=[pl.BlockSpe...  18.2 us
    all_to_all x1, starting transfers between devices, summed_over(): return jnp.sum(lax.all_to_all(spread, axis, 0, 0, tiled=False), axis=0)  13.7 us
    ppermute x1, starting transfers between devices, local(): lax.ppermute(window_own[:, :BORDER], 'chan', [(i + 1, i) for i in range(g...  3.86 us
    all_to_all x1, waiting for transfers between devices, summed_over(): return jnp.sum(lax.all_to_all(spread, axis, 0, 0, tiled=False), axis=0)  3.63 us
    ppermute x1, starting transfers between devices, local(): left_raw = lax.ppermute(trains[BINS_DEV - MAXLAG:], 'tm', to_next)  3.14 us
    ppermute x1, waiting for transfers between devices, local(): lax.ppermute(window_own[:, :BORDER], 'chan', [(i + 1, i) for i in range(g...  2.65 us
    dot_general x1, matrix products, local(): lax.dot_general(weighted, unit_onehot, (((1,), (1,)), ((), ())), preferre...  1.91 us
  transfers between devices with their start and end apart: 3, of which 2 were waited for; matrix products, arithmetic and copies ran while one was open for 3% of the time, Pallas kernels for 0%

profile of v8, /device:TPU:1, one launch (start us, length us, event | category | flops | bytes accessed | tf_op | source)
XLA Modules:
  0.0 78.5 jit_solution(16613831745557697966)
XLA Ops:
  0.0 0.7 broadcast_subtract_fusion
  0.7 0.0 copy-start.1
  0.7 0.0 copy-start.2
  0.8 1.9 %fusion.7 = f32[384]{0:T(512)S(1)} fusion(s32[4096]{0:T(1024)S(1)} %bitcast.9, bf16[1,4096]{1,0:T(2,128)(2,1)} %param.6), kind=kOutput, calls=%fused_computation.8 | convolution fusion | flops 4718592 | bytes 26112 | tf_op jit(solution)/shard_map/dot_general | solution.py:116
  2.6 0.6 broadcast_in_dim.31
  3.3 13.7 %all-to-all-start = ((f32[32,1,384]{2,1,0:T(1,128)}), f32[32,1,384]{2,1,0:T(1,128)S(1)}, u32[]{:S(2)}, u32[]{:S(2)}) async-start(f32[32,1,384]{2,1,0:T(1,128)} %broadcast_in_dim.31), calls=%async_computation | async-start | bytes 98304 | tf_op jit(solution)/shard_map/all_to_all | solution.py:93
  17.0 0.0 copy-done.1
  17.0 0.1 reduce.1
  17.1 0.0 copy-done.2
  17.1 1.9 %fusion.1 = f32[256,384]{1,0:T(8,128)S(1)} fusion(s32[4096]{0:T(1024)S(1)} %bitcast.10, s32[4096]{0:T(1024)S(1)} %bitcast.11, bf16[4096]{0:T(1024)(128)(2,1)S(1)} %reduce.1), kind=kOutput, calls=%fused_computation.2 | convolution fusion | flops 808976384 | bytes 434176 | tf_op jit(solution)/shard_map/dot_general | solution.py:111
  19.1 3.1 %collective-permute-start = (f32[50,384]{1,0:T(8,128)S(1)}, f32[50,384]{1,0:T(8,128)S(1)}, u32[]{:S(2)}, u32[]{:S(2)}) collective-permute-start(f32[50,384]{1,0:T(8,128)S(1)} %slice.20), channel_id=1, source_target_pairs={{0,1},{1,2},{2,3},{3,4},{4,5},{5,6},{6,7},{7,8},{8,9},{9,10},{10,1... | collective-permute-start | bytes 230408 | tf_op jit(solution)/shard_map/ppermute | solution.py:121
  22.2 3.6 %all-to-all-done = f32[32,1,384]{2,1,0:T(1,128)S(1)} async-done(((f32[32,1,384]{2,1,0:T(1,128)}), f32[32,1,384]{2,1,0:T(1,128)S(1)}, u32[]{:S(2)}, u32[]{:S(2)}) %all-to-all-start) | async-done | bytes 49184 | tf_op jit(solution)/shard_map/all_to_all | solution.py:93
  25.8 0.1 reduce_sum.18
  25.9 0.0 copy-start.3
  26.0 0.0 collective-permute-done
  26.0 0.1 pad_maximum_fusion.1.own_ref
  26.1 0.0 copy-start
  26.1 3.9 %collective-permute-start.1 = (bf16[312,64]{1,0:T(8,128)(2,1)S(1)}, bf16[312,64]{1,0:T(8,128)(2,1)S(1)}, u32[]{:S(2)}, u32[]{:S(2)}) collective-permute-start(bf16[312,64]{1,0:T(8,128)(2,1)S(1)} %slice.21), channel_id=1, source_target_pairs={{32,0},{64,32},{96,64},{128,96},{160,128},{192,160},{224,192},{256... | collective-permute-start | bytes 119816 | tf_op jit(solution)/shard_map/ppermute | solution.py:133
  30.0 0.0 copy-done.3
  30.0 0.6 slice_subtract_fusion
  30.6 2.6 %collective-permute-done.1 = bf16[312,64]{1,0:T(8,128)(2,1)S(1)} collective-permute-done((bf16[312,64]{1,0:T(8,128)(2,1)S(1)}, bf16[312,64]{1,0:T(8,128)(2,1)S(1)}, u32[]{:S(2)}, u32[]{:S(2)}) %collective-permute-start.1) | collective-permute-done | bytes 39968 | tf_op jit(solution)/shard_map/ppermute | solution.py:133
  33.2 0.8 %pad_maximum_fusion.all_ref = bf16[312,448]{1,0:T(8,128)(2,1)} fusion(bf16[312,64]{1,0:T(8,128)(2,1)S(1)} %collective-permute-done.1, bf16[6,384]{1,0:T(8,128)(2,1)S(1)} %broadcast_in_dim.33, bf16[256,384]{1,0:T(8,128)(2,1)S(1)} %subtract_convert_fusion, bf16[50,384]{1,0:T(8,128)(2,1)S(1)} %fusion.10), kind=kLoop, calls=%fused_computation.12 | loop fusion | flops 1118208 | bytes 559104 | tf_op jit(solution)/shard_map/concatenate | solution.py:136
  34.0 0.0 copy-done
  34.0 18.2 %shard_map.46 = f32[1024,128]{1,0:T(8,128)} custom-call(bf16[312,384]{1,0:T(8,128)(2,1)} %copy-done, bf16[312,448]{1,0:T(8,128)(2,1)} %pad_maximum_fusion.all_ref, s32[1,1024]{1,0:T(1,128)} %get-tuple-element.6.first_ref, s32[1,1024]{1,0:T(1,128)} %get-tuple-element.5.second_ref), custom_call_target="tpu_custom_call" | custom-call | flops 584581120 | bytes 1051648 | tf_op jit(solution)/shard_map/pallas_call | solution.py:64
  52.2 25.6 %all_to_all.11 = f32[32,32,128]{2,1,0:T(8,128)S(1)} all-to-all(f32[32,32,128]{2,1,0:T(8,128)} %bitcast.8), channel_id=1, replica_groups=mesh['chan'=16,'tm'=32] {'tm'}, dimensions={0} | all-to-all | bytes 1048576 | tf_op jit(solution)/shard_map/all_to_all | solution.py:144
  77.9 0.6 slice_bitcast_fusion
  (8 shorter events, 0.2 us)
Async XLA Ops:
  0.7 16.3 %copy-start.1 = (bf16[1,4096]{1,0:T(2,128)(2,1)S(1)}, bf16[1,4096]{1,0:T(2,128)(2,1)}, u32[]{:S(2)}) copy-start(bf16[1,4096]{1,0:T(2,128)(2,1)} %param.6) | copy-start | bytes 24580
  0.7 16.3 %copy-start.2 = (s32[1,4096]{1,0:T(1,128)S(1)}, s32[1,4096]{1,0:T(1,128)}, u32[]{:S(2)}) copy-start(s32[1,4096]{1,0:T(1,128)} %param.4) | copy-start | bytes 49156
  3.3 22.6 %all-to-all-start = ((f32[32,1,384]{2,1,0:T(1,128)}), f32[32,1,384]{2,1,0:T(1,128)S(1)}, u32[]{:S(2)}, u32[]{:S(2)}) async-start(f32[32,1,384]{2,1,0:T(1,128)} %broadcast_in_dim.31), calls=%async_computation | async-start | bytes 98304 | tf_op jit(solution)/shard_map/all_to_all | solution.py:93
  19.1 6.9 %collective-permute-start = (f32[50,384]{1,0:T(8,128)S(1)}, f32[50,384]{1,0:T(8,128)S(1)}, u32[]{:S(2)}, u32[]{:S(2)}) collective-permute-start(f32[50,384]{1,0:T(8,128)S(1)} %slice.20), channel_id=1, source_target_pairs={{0,1},{1,2},{2,3},{3,4},{4,5},{5,6},{6,7},{7,8},{8,9},{9,10},{10,1... | collective-permute-start | bytes 230408 | tf_op jit(solution)/shard_map/ppermute | solution.py:121
  25.9 4.0 %copy-start.3 = (s32[2,1024]{1,0:T(2,128)S(1)}, s32[2,1024]{1,0:T(2,128)}, u32[]{:S(2)}) copy-start(s32[2,1024]{1,0:T(2,128)} %param.7) | copy-start | bytes 24580
  26.1 8.0 %copy-start = (bf16[312,384]{1,0:T(8,128)(2,1)}, bf16[312,384]{1,0:T(8,128)(2,1)S(1)}, u32[]{:S(2)}) copy-start(bf16[312,384]{1,0:T(8,128)(2,1)S(1)} %pad_maximum_fusion.1.own_ref) | copy-start | bytes 718852
  26.1 7.1 %collective-permute-start.1 = (bf16[312,64]{1,0:T(8,128)(2,1)S(1)}, bf16[312,64]{1,0:T(8,128)(2,1)S(1)}, u32[]{:S(2)}, u32[]{:S(2)}) collective-permute-start(bf16[312,64]{1,0:T(8,128)(2,1)S(1)} %slice.21), channel_id=1, source_target_pairs={{32,0},{64,32},{96,64},{128,96},{160,128},{192,160},{224,192},{256... | collective-permute-start | bytes 119816 | tf_op jit(solution)/shard_map/ppermute | solution.py:133

commit v9 on v5

--- a/solution.py
+++ b/solution.py
@@ -95,14 +95,13 @@
     shard_count = lax.axis_size("tm")
     group_count = lax.axis_size("chan")
 
-    bin_index = lax.div(spike_sample, SPB) - shard_index * BINS_DEV
-    within = spike_unit - group_index * U_GRP
-    unit_onehot = (within == lax.broadcasted_iota(jnp.int32, (U_GRP, 1), 0)).astype(jnp.bfloat16)
+    bin_starts = SPB * (shard_index * BINS_DEV + lax.broadcasted_iota(jnp.int32, (BINS_DEV, 1), 0))
+    offset = spike_sample - bin_starts
+    unit_ids = group_index * U_GRP + lax.broadcasted_iota(jnp.int32, (U_GRP, 1), 0)
+    unit_onehot = (spike_unit == unit_ids).astype(jnp.bfloat16)
     weighted = jnp.where(
-        bin_index == lax.broadcasted_iota(jnp.int32, (BINS_DEV, 1), 0),
-        spike_amp,
-        jnp.zeros((), jnp.bfloat16),
-    )
+        (offset >= 0) & (offset < SPB), spike_amp.astype(jnp.float32), 0.0
+    ).astype(jnp.bfloat16)
     trains = lax.dot_general(
         unit_onehot, weighted, (((1,), (1,)), ((), ())), preferred_element_type=jnp.float32
     )

time: 71.1 us -> 70.2 us (0.987)
  other arithmetic: 2.46 us -> 0.94 us
    sub x2 -> x0, other arithmetic: 1.5 us -> none  [the longest x1 0.76 us: local(): bin_index = lax.div(spike_sample, SPB) - shard_index * BINS_DEV]
    unnamed x1 -> x0, other arithmetic: 0.77 us -> none
    broadcast_in_dim x0 -> x1, other arithmetic: none -> 0.74 us  [local(): jnp.where((offset >= 0) & (offset < SPB), spike_amp.astype(jnp.float32),...]
  transfers between devices with their start and end apart: 3 -> 3, of which waited for: 2 -> 2; matrix products, arithmetic and copies ran while one was open for 2% -> 3% of each run, Pallas kernels for 0% -> 0%
where the time goes in v9:
time: 70.2 us; the launch traced here: 69.6 us
  blocking collectives  23.6 us (34%)
  starting transfers between devices  20.8 us (30%)
  Pallas kernels  9.76 us (14%)
  waiting for transfers between devices  7.24 us (10%)
  matrix products  5.93 us (8%)
  local copies, waits for them, and re-layouts  1.28 us (2%)
  other arithmetic  0.94 us (1%)
    all_to_all x1, blocking collectives, local(): summed = jnp.sum(lax.all_to_all(blocks, 'tm', 0, 0, tiled=False), axis=0)  23.6 us
    all_to_all x1, starting transfers between devices, summed_over(): return jnp.sum(lax.all_to_all(spread, axis, 0, 0, tiled=False), axis=0)  13.7 us
    pallas_call x1, Pallas kernels, lagged_products(): pl.pallas_call(corr_kernel, grid=(pairs // LANES,), in_specs=[pl.BlockSpe...  9.76 us
    all_to_all x1, waiting for transfers between devices, summed_over(): return jnp.sum(lax.all_to_all(spread, axis, 0, 0, tiled=False), axis=0)  5.59 us
    ppermute x1, starting transfers between devices, local(): lax.ppermute(window_own[:BORDER], 'chan', [(i + 1, i) for i in range(grou...  3.91 us
    dot_general x2, matrix products, gather_columns(): lax.dot_general(rows, onehot.astype(rows.dtype), (((0,), (0,)), ((), ()))...  3.32 us
    ppermute x1, starting transfers between devices, local(): left_raw = lax.ppermute(trains[:, BINS_DEV - MAXLAG:], 'tm', to_next)  3.14 us
    dot_general x1, matrix products, local(): lax.dot_general(unit_onehot, weighted, (((1,), (1,)), ((), ())), preferre...  2.61 us
  transfers between devices with their start and end apart: 3, of which 2 were waited for; matrix products, arithmetic and copies ran while one was open for 3% of the time, Pallas kernels for 0%

profile of v9, /device:TPU:1, one launch (start us, length us, event | category | flops | bytes accessed | tf_op | source)
XLA Modules:
  0.0 69.6 jit_solution(2270032201839650403)
XLA Ops:
  0.0 0.7 %broadcast_in_dim.41 = f32[1,4096]{1,0:T(1,128)S(1)} convert(bf16[1,4096]{1,0:T(2,128)(2,1)} %param.6) | non-fusion elementwise | flops 4096 | bytes 24576 | tf_op jit(solution)/shard_map/jit(_where)/broadcast_in_dim | solution.py:102
  0.8 0.0 copy-start
  0.8 2.6 %fusion.33 = (f32[384]{0:T(512)S(1)}, f32[384,256]{0,1:T(8,128)S(1)}) fusion(f32[4096]{0:T(1024)S(1)} %bitcast.9, s32[256]{0:T(256)S(1)} %add_multiply_fusion, s32[4096]{0:T(1024)} %bitcast.12, s32[4096]{0:T(1024)} %bitcast.13, s32[384]{0:T(512)S(1)} %iota_add_fusion), kind=kOutput, calls=%fused_computation.47 | convolution fusion | flops 812220032 | bytes 446464 | tf_op jit(solution)/shard_map/dot_general | solution.py:105
  3.4 0.6 broadcast_in_dim.38
  4.0 13.7 %all-to-all-start = ((f32[32,1,384]{2,1,0:T(1,128)}), f32[32,1,384]{2,1,0:T(1,128)S(1)}, u32[]{:S(2)}, u32[]{:S(2)}) async-start(f32[32,1,384]{2,1,0:T(1,128)} %broadcast_in_dim.38), calls=%async_computation | async-start | bytes 98304 | tf_op jit(solution)/shard_map/all_to_all | solution.py:81
  17.8 3.1 %collective-permute-start = (f32[384,50]{0,1:T(8,128)S(1)}, f32[384,50]{0,1:T(8,128)S(1)}, u32[]{:S(2)}, u32[]{:S(2)}) collective-permute-start(f32[384,50]{0,1:T(8,128)S(1)} %slice.20), channel_id=1, source_target_pairs={{0,1},{1,2},{2,3},{3,4},{4,5},{5,6},{6,7},{7,8},{8,9},{9,10},{10,1... | collective-permute-start | bytes 230408 | tf_op jit(solution)/shard_map/ppermute | solution.py:110
  20.9 0.0 copy-done
  20.9 5.6 %all-to-all-done = f32[32,1,384]{2,1,0:T(1,128)S(1)} async-done(((f32[32,1,384]{2,1,0:T(1,128)}), f32[32,1,384]{2,1,0:T(1,128)S(1)}, u32[]{:S(2)}, u32[]{:S(2)}) %all-to-all-start) | async-done | bytes 49184 | tf_op jit(solution)/shard_map/all_to_all | solution.py:81
  26.5 0.1 reduce_sum.28
  26.6 0.0 collective-permute-done
  26.7 3.9 %collective-permute-start.1 = (bf16[64,312]{0,1:T(8,128)(2,1)S(1)}, bf16[64,312]{0,1:T(8,128)(2,1)S(1)}, u32[]{:S(2)}, u32[]{:S(2)}) collective-permute-start(bf16[64,312]{0,1:T(8,128)(2,1)S(1)} %pad_maximum_fusion), channel_id=1, source_target_pairs={{32,0},{64,32},{96,64},{128,96},{160,128},{192,160},{224,192},{256... | collective-permute-start | bytes 119816 | tf_op jit(solution)/shard_map/ppermute | solution.py:122
  30.6 1.6 %fusion.12.l_ref = f32[312,1024]{1,0:T(8,128)} fusion(s32[1024]{0:T(1024)S(1)} %bitcast.11, bf16[384,6]{0,1:T(8,128)(2,1)S(1)} %broadcast_in_dim.40, bf16[384,256]{0,1:T(8,128)(2,1)S(1)} %subtract_convert_fusion, bf16[384,50]{0,1:T(8,128)(2,1)S(1)} %fusion.27), kind=kOutput, calls=%fused_computation.17 | convolution fusion | flops 246478848 | bytes 1521664 | tf_op jit(solution)/shard_map/dot_general | solution.py:86
  32.3 1.6 %collective-permute-done.1 = bf16[64,312]{0,1:T(8,128)(2,1)S(1)} collective-permute-done((bf16[64,312]{0,1:T(8,128)(2,1)S(1)}, bf16[64,312]{0,1:T(8,128)(2,1)S(1)}, u32[]{:S(2)}, u32[]{:S(2)}) %collective-permute-start.1) | collective-permute-done | bytes 39968 | tf_op jit(solution)/shard_map/ppermute | solution.py:122
  33.9 1.7 %fusion.11.r_ref = f32[312,1024]{1,0:T(8,128)} fusion(s32[1024]{0:T(1024)S(1)} %bitcast.10, bf16[64,312]{0,1:T(8,128)(2,1)S(1)} %collective-permute-done.1, bf16[384,6]{0,1:T(8,128)(2,1)S(1)} %broadcast_in_dim.40, bf16[384,256]{0,1:T(8,128)(2,1)S(1)} %subtract_convert_fusion, bf16[384,50]{0,1:T(8,128)(2,1)S(1)} %fusion.27), kind=kOutput, calls=%fused_computation.15 | convolution fusion | flops 287838208 | bytes 1561600 | tf_op jit(solution)/shard_map/dot_general | solution.py:86
  35.6 9.8 %shard_map.46 = f32[1024,128]{1,0:T(8,128)} custom-call(f32[312,1024]{1,0:T(8,128)} %fusion.12.l_ref, f32[312,1024]{1,0:T(8,128)} %fusion.11.r_ref), custom_call_target="tpu_custom_call" | custom-call | flops 52953088 | bytes 3080192 | tf_op jit(solution)/shard_map/pallas_call | solution.py:56
  45.4 23.6 %all_to_all.11 = f32[32,32,128]{2,1,0:T(8,128)S(1)} all-to-all(f32[32,32,128]{2,1,0:T(8,128)} %bitcast.8), channel_id=1, replica_groups=mesh['chan'=16,'tm'=32] {'tm'}, dimensions={0} | all-to-all | bytes 1048576 | tf_op jit(solution)/shard_map/all_to_all | solution.py:135
  69.0 0.6 slice_bitcast_fusion
  (10 shorter events, 0.2 us)
Async XLA Ops:
  0.8 20.2 %copy-start = (s32[2,1024]{1,0:T(2,128)S(1)}, s32[2,1024]{1,0:T(2,128)}, u32[]{:S(2)}) copy-start(s32[2,1024]{1,0:T(2,128)} %param.7) | copy-start | bytes 24580
  4.0 22.5 %all-to-all-start = ((f32[32,1,384]{2,1,0:T(1,128)}), f32[32,1,384]{2,1,0:T(1,128)S(1)}, u32[]{:S(2)}, u32[]{:S(2)}) async-start(f32[32,1,384]{2,1,0:T(1,128)} %broadcast_in_dim.38), calls=%async_computation | async-start | bytes 98304 | tf_op jit(solution)/shard_map/all_to_all | solution.py:81
  17.8 8.9 %collective-permute-start = (f32[384,50]{0,1:T(8,128)S(1)}, f32[384,50]{0,1:T(8,128)S(1)}, u32[]{:S(2)}, u32[]{:S(2)}) collective-permute-start(f32[384,50]{0,1:T(8,128)S(1)} %slice.20), channel_id=1, source_target_pairs={{0,1},{1,2},{2,3},{3,4},{4,5},{5,6},{6,7},{7,8},{8,9},{9,10},{10,1... | collective-permute-start | bytes 230408 | tf_op jit(solution)/shard_map/ppermute | solution.py:110
  26.7 7.2 %collective-permute-start.1 = (bf16[64,312]{0,1:T(8,128)(2,1)S(1)}, bf16[64,312]{0,1:T(8,128)(2,1)S(1)}, u32[]{:S(2)}, u32[]{:S(2)}) collective-permute-start(bf16[64,312]{0,1:T(8,128)(2,1)S(1)} %pad_maximum_fusion), channel_id=1, source_target_pairs={{32,0},{64,32},{96,64},{128,96},{160,128},{192,160},{224,192},{256... | collective-permute-start | bytes 119816 | tf_op jit(solution)/shard_map/ppermute | solution.py:122

commit v10 on v9

--- a/solution.py
+++ b/solution.py
@@ -131,9 +131,9 @@
     partial = lagged_products(left_t, right_t)
 
     per_shard = partial.shape[0] // shard_count
-    blocks = partial.reshape(shard_count, per_shard, LANES)
-    summed = jnp.sum(lax.all_to_all(blocks, "tm", 0, 0, tiled=False), axis=0)
-    return summed[:, :NLAG].T
+    blocks = partial[:, :NLAG].reshape(shard_count, 1, per_shard * NLAG)
+    summed = jnp.sum(lax.all_to_all(blocks, "tm", 0, 0, tiled=False), axis=(0, 1))
+    return summed.reshape(per_shard, NLAG).T
 
 
 def solution(mesh):

time: 70.2 us -> 70.4 us (level)
  local copies, waits for them, and re-layouts: 1.28 us -> 3.29 us
  blocking collectives: 23.6 us -> 21.6 us
    reshape x0 -> x2, local copies, waits for them, and re-layouts: none -> 2.63 us  [the longest x1 1.92 us: local(): blocks = partial[:, :NLAG].reshape(shard_count, 1, per_shard * NLAG)]
    all_to_all x1, blocking collectives: 23.6 us -> 21.6 us  [local(): lax.all_to_all(blocks, 'tm', 0, 0, tiled=False)]
where the time goes in v10:
time: 70.4 us; the launch traced here: 69.8 us
  blocking collectives  21.6 us (31%)
  starting transfers between devices  20.8 us (30%)
  Pallas kernels  9.76 us (14%)
  waiting for transfers between devices  7.24 us (10%)
  matrix products  5.93 us (8%)
  local copies, waits for them, and re-layouts  3.29 us (5%)
  other arithmetic  1.15 us (2%)
    all_to_all x1, blocking collectives, local(): lax.all_to_all(blocks, 'tm', 0, 0, tiled=False)  21.6 us
    all_to_all x1, starting transfers between devices, summed_over(): return jnp.sum(lax.all_to_all(spread, axis, 0, 0, tiled=False), axis=0)  13.7 us
    pallas_call x1, Pallas kernels, lagged_products(): pl.pallas_call(corr_kernel, grid=(pairs // LANES,), in_specs=[pl.BlockSpe...  9.76 us
    all_to_all x1, waiting for transfers between devices, summed_over(): return jnp.sum(lax.all_to_all(spread, axis, 0, 0, tiled=False), axis=0)  5.59 us
    ppermute x1, starting transfers between devices, local(): lax.ppermute(window_own[:BORDER], 'chan', [(i + 1, i) for i in range(grou...  3.91 us
    dot_general x2, matrix products, gather_columns(): lax.dot_general(rows, onehot.astype(rows.dtype), (((0,), (0,)), ((), ()))...  3.32 us
    ppermute x1, starting transfers between devices, local(): left_raw = lax.ppermute(trains[:, BINS_DEV - MAXLAG:], 'tm', to_next)  3.14 us
    dot_general x1, matrix products, local(): lax.dot_general(unit_onehot, weighted, (((1,), (1,)), ((), ())), preferre...  2.61 us
  transfers between devices with their start and end apart: 3, of which 2 were waited for; matrix products, arithmetic and copies ran while one was open for 3% of the time, Pallas kernels for 0%

profile of v10, /device:TPU:1, one launch (start us, length us, event | category | flops | bytes accessed | tf_op | source)
XLA Modules:
  0.0 69.8 jit_solution(11067087114659204127)
XLA Ops:
  0.0 0.7 %broadcast_in_dim.41 = f32[1,4096]{1,0:T(1,128)S(1)} convert(bf16[1,4096]{1,0:T(2,128)(2,1)} %param.6) | non-fusion elementwise | flops 4096 | bytes 24576 | tf_op jit(solution)/shard_map/jit(_where)/broadcast_in_dim | solution.py:102
  0.8 0.0 copy-start
  0.8 2.6 %fusion.33 = (f32[384]{0:T(512)S(1)}, f32[384,256]{0,1:T(8,128)S(1)}) fusion(f32[4096]{0:T(1024)S(1)} %bitcast.8, s32[256]{0:T(256)S(1)} %add_multiply_fusion, s32[4096]{0:T(1024)} %bitcast.11, s32[4096]{0:T(1024)} %bitcast.12, s32[384]{0:T(512)S(1)} %iota_add_fusion), kind=kOutput, calls=%fused_computation.46 | convolution fusion | flops 812220032 | bytes 446464 | tf_op jit(solution)/shard_map/dot_general | solution.py:105
  3.4 0.6 broadcast_in_dim.38
  4.0 13.7 %all-to-all-start = ((f32[32,1,384]{2,1,0:T(1,128)}), f32[32,1,384]{2,1,0:T(1,128)S(1)}, u32[]{:S(2)}, u32[]{:S(2)}) async-start(f32[32,1,384]{2,1,0:T(1,128)} %broadcast_in_dim.38), calls=%async_computation | async-start | bytes 98304 | tf_op jit(solution)/shard_map/all_to_all | solution.py:81
  17.8 3.1 %collective-permute-start = (f32[384,50]{0,1:T(8,128)S(1)}, f32[384,50]{0,1:T(8,128)S(1)}, u32[]{:S(2)}, u32[]{:S(2)}) collective-permute-start(f32[384,50]{0,1:T(8,128)S(1)} %slice.20), channel_id=1, source_target_pairs={{0,1},{1,2},{2,3},{3,4},{4,5},{5,6},{6,7},{7,8},{8,9},{9,10},{10,1... | collective-permute-start | bytes 230408 | tf_op jit(solution)/shard_map/ppermute | solution.py:110
  20.9 0.0 copy-done
  20.9 5.6 %all-to-all-done = f32[32,1,384]{2,1,0:T(1,128)S(1)} async-done(((f32[32,1,384]{2,1,0:T(1,128)}), f32[32,1,384]{2,1,0:T(1,128)S(1)}, u32[]{:S(2)}, u32[]{:S(2)}) %all-to-all-start) | async-done | bytes 49184 | tf_op jit(solution)/shard_map/all_to_all | solution.py:81
  26.5 0.1 reduce_sum.28
  26.6 0.0 collective-permute-done
  26.7 3.9 %collective-permute-start.1 = (bf16[64,312]{0,1:T(8,128)(2,1)S(1)}, bf16[64,312]{0,1:T(8,128)(2,1)S(1)}, u32[]{:S(2)}, u32[]{:S(2)}) collective-permute-start(bf16[64,312]{0,1:T(8,128)(2,1)S(1)} %pad_maximum_fusion), channel_id=1, source_target_pairs={{32,0},{64,32},{96,64},{128,96},{160,128},{192,160},{224,192},{256... | collective-permute-start | bytes 119816 | tf_op jit(solution)/shard_map/ppermute | solution.py:122
  30.6 1.6 %fusion.12.l_ref = f32[312,1024]{1,0:T(8,128)} fusion(s32[1024]{0:T(1024)S(1)} %bitcast.10, bf16[384,6]{0,1:T(8,128)(2,1)S(1)} %broadcast_in_dim.40, bf16[384,256]{0,1:T(8,128)(2,1)S(1)} %subtract_convert_fusion, bf16[384,50]{0,1:T(8,128)(2,1)S(1)} %fusion.27), kind=kOutput, calls=%fused_computation.17 | convolution fusion | flops 246478848 | bytes 1521664 | tf_op jit(solution)/shard_map/dot_general | solution.py:86
  32.3 1.6 %collective-permute-done.1 = bf16[64,312]{0,1:T(8,128)(2,1)S(1)} collective-permute-done((bf16[64,312]{0,1:T(8,128)(2,1)S(1)}, bf16[64,312]{0,1:T(8,128)(2,1)S(1)}, u32[]{:S(2)}, u32[]{:S(2)}) %collective-permute-start.1) | collective-permute-done | bytes 39968 | tf_op jit(solution)/shard_map/ppermute | solution.py:122
  33.9 1.7 %fusion.11.r_ref = f32[312,1024]{1,0:T(8,128)} fusion(s32[1024]{0:T(1024)S(1)} %bitcast.9, bf16[64,312]{0,1:T(8,128)(2,1)S(1)} %collective-permute-done.1, bf16[384,6]{0,1:T(8,128)(2,1)S(1)} %broadcast_in_dim.40, bf16[384,256]{0,1:T(8,128)(2,1)S(1)} %subtract_convert_fusion, bf16[384,50]{0,1:T(8,128)(2,1)S(1)} %fusion.27), kind=kOutput, calls=%fused_computation.15 | convolution fusion | flops 287838208 | bytes 1561600 | tf_op jit(solution)/shard_map/dot_general | solution.py:86
  35.6 9.8 %shard_map.46 = f32[1024,128]{1,0:T(8,128)} custom-call(f32[312,1024]{1,0:T(8,128)} %fusion.12.l_ref, f32[312,1024]{1,0:T(8,128)} %fusion.11.r_ref), custom_call_target="tpu_custom_call" | custom-call | flops 52953088 | bytes 3080192 | tf_op jit(solution)/shard_map/pallas_call | solution.py:56
  45.4 1.9 %reshape.30 = f32[32,1,3232]{2,1,0:T(1,128)S(1)} reshape(f32[1024,101]{1,0:T(8,128)} %bitcast.7) | data formatting | bytes 827392 | tf_op jit(solution)/shard_map/reshape | solution.py:134
  47.3 21.6 %all_to_all.11 = f32[32,1,3232]{2,1,0:T(1,128)S(1)} all-to-all(f32[32,1,3232]{2,1,0:T(1,128)S(1)} %reshape.30), channel_id=1, replica_groups=mesh['chan'=16,'tm'=32] {'tm'}, dimensions={0} | all-to-all | bytes 827392 | tf_op jit(solution)/shard_map/all_to_all | solution.py:135
  68.9 0.3 reduce_sum.29
  69.1 0.7 %reshape.28 = f32[32,101]{1,0:T(8,128)} reshape(f32[3232]{0:T(1024)S(1)} %reduce_sum.29) | data formatting | bytes 25856 | tf_op jit(solution)/shard_map/reshape | solution.py:136
  (9 shorter events, 0.1 us)
Async XLA Ops:
  0.8 20.2 %copy-start = (s32[2,1024]{1,0:T(2,128)S(1)}, s32[2,1024]{1,0:T(2,128)}, u32[]{:S(2)}) copy-start(s32[2,1024]{1,0:T(2,128)} %param.7) | copy-start | bytes 24580
  4.0 22.5 %all-to-all-start = ((f32[32,1,384]{2,1,0:T(1,128)}), f32[32,1,384]{2,1,0:T(1,128)S(1)}, u32[]{:S(2)}, u32[]{:S(2)}) async-start(f32[32,1,384]{2,1,0:T(1,128)} %broadcast_in_dim.38), calls=%async_computation | async-start | bytes 98304 | tf_op jit(solution)/shard_map/all_to_all | solution.py:81
  17.8 8.9 %collective-permute-start = (f32[384,50]{0,1:T(8,128)S(1)}, f32[384,50]{0,1:T(8,128)S(1)}, u32[]{:S(2)}, u32[]{:S(2)}) collective-permute-start(f32[384,50]{0,1:T(8,128)S(1)} %slice.20), channel_id=1, source_target_pairs={{0,1},{1,2},{2,3},{3,4},{4,5},{5,6},{6,7},{7,8},{8,9},{9,10},{10,1... | collective-permute-start | bytes 230408 | tf_op jit(solution)/shard_map/ppermute | solution.py:110
  26.7 7.2 %collective-permute-start.1 = (bf16[64,312]{0,1:T(8,128)(2,1)S(1)}, bf16[64,312]{0,1:T(8,128)(2,1)S(1)}, u32[]{:S(2)}, u32[]{:S(2)}) collective-permute-start(bf16[64,312]{0,1:T(8,128)(2,1)S(1)} %pad_maximum_fusion), channel_id=1, source_target_pairs={{32,0},{64,32},{96,64},{128,96},{160,128},{192,160},{224,192},{256... | collective-permute-start | bytes 119816 | tf_op jit(solution)/shard_map/ppermute | solution.py:122

commit v11 on v9

--- a/solution.py
+++ b/solution.py
@@ -13,15 +13,17 @@
 NLAG = 2 * MAXLAG + 1
 LANES = 128
 KCHUNK = 13
-WINDOW_PAD = 6
+WINDOW_PAD = 14
 
 
-def corr_kernel(l_ref, r_ref, o_ref, left_ref, right_ref, lags_ref):
-    steps = (l_ref.shape[0] - MAXLAG) // 8
+def corr_kernel(l_ref, r_ref, o_ref, lf_ref, rf_ref, left_ref, right_ref, lags_ref):
+    steps = (l_ref.shape[0] - MAXLAG - WINDOW_PAD) // 8
     width = left_ref.shape[1]
+    lf_ref[...] = l_ref[...].astype(jnp.float32)
+    rf_ref[...] = r_ref[...].astype(jnp.float32)
     for r in range(8):
-        left_ref[r] = l_ref[pl.ds(r, width), :]
-        right_ref[r] = r_ref[pl.ds(r, width), :]
+        left_ref[r] = lf_ref[pl.ds(r, width), :]
+        right_ref[r] = rf_ref[pl.ds(r, width), :]
 
     def lag_rows(fixed_ref, moving_ref, lags, shift_of):
         def body(i, accs):
@@ -63,13 +65,15 @@
         out_specs=pl.BlockSpec((LANES, LANES), lambda j: (j, 0)),
         out_shape=jax.ShapeDtypeStruct((pairs, LANES), jnp.float32),
         scratch_shapes=[
+            pltpu.VMEM((left_t.shape[0], LANES), jnp.float32),
+            pltpu.VMEM((left_t.shape[0], LANES), jnp.float32),
             pltpu.VMEM((8, left_t.shape[0] - 8, LANES), jnp.float32),
             pltpu.VMEM((8, left_t.shape[0] - 8, LANES), jnp.float32),
             pltpu.VMEM((LANES, LANES), jnp.float32),
         ],
         cost_estimate=pl.CostEstimate(
             flops=2 * NLAG * pairs * bins,
-            bytes_accessed=4 * pairs * (left_t.shape[0] + right_t.shape[0] + LANES),
+            bytes_accessed=pairs * (2 * left_t.shape[0] + 2 * right_t.shape[0] + 4 * LANES),
             transcendentals=0,
         ),
     )(left_t, right_t)
@@ -86,7 +90,7 @@
     return lax.dot_general(
         rows, onehot.astype(rows.dtype), (((0,), (0,)), ((), ())),
         preferred_element_type=jnp.float32,
-    )
+    ).astype(rows.dtype)
 
 
 def local(spike_sample, spike_unit, spike_amp, pair_units):

time: 70.2 us -> 70 us (level)
  transfers between devices with their start and end apart: 3 -> 3, of which waited for: 2 -> 2; matrix products, arithmetic and copies ran while one was open for 3% -> 2% of each run, Pallas kernels for 0% -> 0%
where the time goes in v11:
time: 70 us; the launch traced here: 69.5 us
  blocking collectives  23.6 us (34%)
  starting transfers between devices  20.8 us (30%)
  Pallas kernels  9.82 us (14%)
  waiting for transfers between devices  7.46 us (11%)
  matrix products  5.51 us (8%)
  local copies, waits for them, and re-layouts  1.28 us (2%)
  other arithmetic  0.94 us (1%)
    all_to_all x1, blocking collectives, local(): summed = jnp.sum(lax.all_to_all(blocks, 'tm', 0, 0, tiled=False), axis=0)  23.6 us
    all_to_all x1, starting transfers between devices, summed_over(): return jnp.sum(lax.all_to_all(spread, axis, 0, 0, tiled=False), axis=0)  13.7 us
    pallas_call x1, Pallas kernels, lagged_products(): pl.pallas_call(corr_kernel, grid=(pairs // LANES,), in_specs=[pl.BlockSpe...  9.82 us
    all_to_all x1, waiting for transfers between devices, summed_over(): return jnp.sum(lax.all_to_all(spread, axis, 0, 0, tiled=False), axis=0)  5.59 us
    ppermute x1, starting transfers between devices, local(): lax.ppermute(window_own[:BORDER], 'chan', [(i + 1, i) for i in range(grou...  3.91 us
    ppermute x1, starting transfers between devices, local(): left_raw = lax.ppermute(trains[:, BINS_DEV - MAXLAG:], 'tm', to_next)  3.14 us
    dot_general x2, matrix products, gather_columns(): lax.dot_general(rows, onehot.astype(rows.dtype), (((0,), (0,)), ((), ()))...  2.9 us
    dot_general x1, matrix products, local(): lax.dot_general(unit_onehot, weighted, (((1,), (1,)), ((), ())), preferre...  2.61 us
  transfers between devices with their start and end apart: 3, of which 2 were waited for; matrix products, arithmetic and copies ran while one was open for 2% of the time, Pallas kernels for 0%

profile of v11, /device:TPU:1, one launch (start us, length us, event | category | flops | bytes accessed | tf_op | source)
XLA Modules:
  0.0 69.5 jit_solution(5182831156180605370)
XLA Ops:
  0.0 0.7 %broadcast_in_dim.41 = f32[1,4096]{1,0:T(1,128)S(1)} convert(bf16[1,4096]{1,0:T(2,128)(2,1)} %param.6) | non-fusion elementwise | flops 4096 | bytes 24576 | tf_op jit(solution)/shard_map/jit(_where)/broadcast_in_dim | solution.py:106
  0.8 0.0 copy-start
  0.8 2.6 %fusion.35 = (f32[384]{0:T(512)S(1)}, f32[384,256]{0,1:T(8,128)S(1)}) fusion(f32[4096]{0:T(1024)S(1)} %bitcast.9, s32[256]{0:T(256)S(1)} %add_multiply_fusion, s32[4096]{0:T(1024)} %bitcast.12, s32[4096]{0:T(1024)} %bitcast.13, s32[384]{0:T(512)S(1)} %iota_add_fusion), kind=kOutput, calls=%fused_computation.49 | convolution fusion | flops 812220032 | bytes 446464 | tf_op jit(solution)/shard_map/dot_general | solution.py:109
  3.4 0.6 broadcast_in_dim.38
  4.0 13.7 %all-to-all-start = ((f32[32,1,384]{2,1,0:T(1,128)}), f32[32,1,384]{2,1,0:T(1,128)S(1)}, u32[]{:S(2)}, u32[]{:S(2)}) async-start(f32[32,1,384]{2,1,0:T(1,128)} %broadcast_in_dim.38), calls=%async_computation | async-start | bytes 98304 | tf_op jit(solution)/shard_map/all_to_all | solution.py:85
  17.8 3.1 %collective-permute-start = (f32[384,50]{0,1:T(8,128)S(1)}, f32[384,50]{0,1:T(8,128)S(1)}, u32[]{:S(2)}, u32[]{:S(2)}) collective-permute-start(f32[384,50]{0,1:T(8,128)S(1)} %slice.20), channel_id=1, source_target_pairs={{0,1},{1,2},{2,3},{3,4},{4,5},{5,6},{6,7},{7,8},{8,9},{9,10},{10,1... | collective-permute-start | bytes 230408 | tf_op jit(solution)/shard_map/ppermute | solution.py:114
  20.9 0.0 copy-done
  20.9 5.6 %all-to-all-done = f32[32,1,384]{2,1,0:T(1,128)S(1)} async-done(((f32[32,1,384]{2,1,0:T(1,128)}), f32[32,1,384]{2,1,0:T(1,128)S(1)}, u32[]{:S(2)}, u32[]{:S(2)}) %all-to-all-start) | async-done | bytes 49184 | tf_op jit(solution)/shard_map/all_to_all | solution.py:85
  26.5 0.1 reduce_sum.28
  26.6 0.0 collective-permute-done
  26.7 3.9 %collective-permute-start.1 = (bf16[64,320]{0,1:T(8,128)(2,1)S(1)}, bf16[64,320]{0,1:T(8,128)(2,1)S(1)}, u32[]{:S(2)}, u32[]{:S(2)}) collective-permute-start(bf16[64,320]{0,1:T(8,128)(2,1)S(1)} %pad_maximum_fusion), channel_id=1, source_target_pairs={{32,0},{64,32},{96,64},{128,96},{160,128},{192,160},{224,192},{256... | collective-permute-start | bytes 122888 | tf_op jit(solution)/shard_map/ppermute | solution.py:126
  30.6 1.4 %fusion.14.l_ref = bf16[320,1024]{1,0:T(8,128)(2,1)} fusion(s32[1024]{0:T(1024)S(1)} %bitcast.11, bf16[384,14]{0,1:T(8,128)(2,1)S(1)} %broadcast_in_dim.40, bf16[384,256]{0,1:T(8,128)(2,1)S(1)} %subtract_convert_fusion, bf16[384,50]{0,1:T(8,128)(2,1)S(1)} %fusion.29), kind=kOutput, calls=%fused_computation.19 | convolution fusion | flops 253116416 | bytes 905216 | tf_op jit(solution)/shard_map/dot_general | solution.py:90
  32.1 1.9 %collective-permute-done.1 = bf16[64,320]{0,1:T(8,128)(2,1)S(1)} collective-permute-done((bf16[64,320]{0,1:T(8,128)(2,1)S(1)}, bf16[64,320]{0,1:T(8,128)(2,1)S(1)}, u32[]{:S(2)}, u32[]{:S(2)}) %collective-permute-start.1) | collective-permute-done | bytes 40992 | tf_op jit(solution)/shard_map/ppermute | solution.py:126
  33.9 1.5 %fusion.13.r_ref = bf16[320,1024]{1,0:T(8,128)(2,1)} fusion(s32[1024]{0:T(1024)S(1)} %bitcast.10, bf16[64,320]{0,1:T(8,128)(2,1)S(1)} %collective-permute-done.1, bf16[384,14]{0,1:T(8,128)(2,1)S(1)} %broadcast_in_dim.40, bf16[384,256]{0,1:T(8,128)(2,1)S(1)} %subtract_convert_fusion, bf16[384,50]{0,1:T(8,128)(2,1)S(1)} %fusion.29), kind=kOutput, calls=%fused_computation.18 | convolution fusion | flops 295534592 | bytes 946176 | tf_op jit(solution)/shard_map/dot_general | solution.py:90
  35.4 9.8 %shard_map.46 = f32[1024,128]{1,0:T(8,128)} custom-call(bf16[320,1024]{1,0:T(8,128)(2,1)} %fusion.14.l_ref, bf16[320,1024]{1,0:T(8,128)(2,1)} %fusion.13.r_ref), custom_call_target="tpu_custom_call" | custom-call | flops 52953088 | bytes 1835008 | tf_op jit(solution)/shard_map/pallas_call | solution.py:58
  45.2 23.6 %all_to_all.11 = f32[32,32,128]{2,1,0:T(8,128)S(1)} all-to-all(f32[32,32,128]{2,1,0:T(8,128)} %bitcast.8), channel_id=1, replica_groups=mesh['chan'=16,'tm'=32] {'tm'}, dimensions={0} | all-to-all | bytes 1048576 | tf_op jit(solution)/shard_map/all_to_all | solution.py:139
  68.8 0.6 slice_bitcast_fusion
  (10 shorter events, 0.2 us)
Async XLA Ops:
  0.8 20.2 %copy-start = (s32[2,1024]{1,0:T(2,128)S(1)}, s32[2,1024]{1,0:T(2,128)}, u32[]{:S(2)}) copy-start(s32[2,1024]{1,0:T(2,128)} %param.7) | copy-start | bytes 24580
  4.0 22.5 %all-to-all-start = ((f32[32,1,384]{2,1,0:T(1,128)}), f32[32,1,384]{2,1,0:T(1,128)S(1)}, u32[]{:S(2)}, u32[]{:S(2)}) async-start(f32[32,1,384]{2,1,0:T(1,128)} %broadcast_in_dim.38), calls=%async_computation | async-start | bytes 98304 | tf_op jit(solution)/shard_map/all_to_all | solution.py:85
  17.8 8.9 %collective-permute-start = (f32[384,50]{0,1:T(8,128)S(1)}, f32[384,50]{0,1:T(8,128)S(1)}, u32[]{:S(2)}, u32[]{:S(2)}) collective-permute-start(f32[384,50]{0,1:T(8,128)S(1)} %slice.20), channel_id=1, source_target_pairs={{0,1},{1,2},{2,3},{3,4},{4,5},{5,6},{6,7},{7,8},{8,9},{9,10},{10,1... | collective-permute-start | bytes 230408 | tf_op jit(solution)/shard_map/ppermute | solution.py:114
  26.7 7.2 %collective-permute-start.1 = (bf16[64,320]{0,1:T(8,128)(2,1)S(1)}, bf16[64,320]{0,1:T(8,128)(2,1)S(1)}, u32[]{:S(2)}, u32[]{:S(2)}) collective-permute-start(bf16[64,320]{0,1:T(8,128)(2,1)S(1)} %pad_maximum_fusion), channel_id=1, source_target_pairs={{32,0},{64,32},{96,64},{128,96},{160,128},{192,160},{224,192},{256... | collective-permute-start | bytes 122888 | tf_op jit(solution)/shard_map/ppermute | solution.py:126

commit v12 on v11

--- a/solution.py
+++ b/solution.py
@@ -123,14 +123,13 @@
     window_own = jnp.concatenate(
         [left_halo, centre(trains), jnp.zeros((U_GRP, WINDOW_PAD), jnp.bfloat16)], axis=1
     )
-    border = lax.ppermute(
-        window_own[:BORDER], "chan", [(i + 1, i) for i in range(group_count - 1)]
-    )
-    window = jnp.concatenate([window_own, border], axis=0)
-
     first_units = pair_units[0] - group_index * U_GRP
     second_units = pair_units[1] - group_index * U_GRP
-    left_t = gather_columns(window_own, first_units)
+    left_t, sent = lax.optimization_barrier(
+        (gather_columns(window_own, first_units), window_own[:BORDER])
+    )
+    border = lax.ppermute(sent, "chan", [(i + 1, i) for i in range(group_count - 1)])
+    window = jnp.concatenate([window_own, border], axis=0)
     right_t = gather_columns(window, second_units)
     partial = lagged_products(left_t, right_t)
 

time: 70 us -> 71.4 us (1.020)
  waiting for transfers between devices: 7.46 us -> 8.89 us
    ppermute x1, waiting for transfers between devices: 1.87 us -> 3.29 us  [local(): lax.ppermute(sent, 'chan', [(i + 1, i) for i in range(group_count - 1)])]
  transfers between devices with their start and end apart: 3 -> 3, of which waited for: 2 -> 2; matrix products, arithmetic and copies ran while one was open for 2% -> 0% of each run, Pallas kernels for 0% -> 0%
where the time goes in v12:
time: 71.4 us; the launch traced here: 70.9 us
  blocking collectives  23.6 us (33%)
  starting transfers between devices  20.8 us (29%)
  Pallas kernels  9.82 us (14%)
  waiting for transfers between devices  8.89 us (12%)
  matrix products  5.51 us (8%)
  local copies, waits for them, and re-layouts  1.28 us (2%)
  other arithmetic  0.94 us (1%)
    all_to_all x1, blocking collectives, local(): summed = jnp.sum(lax.all_to_all(blocks, 'tm', 0, 0, tiled=False), axis=0)  23.6 us
    all_to_all x1, starting transfers between devices, summed_over(): return jnp.sum(lax.all_to_all(spread, axis, 0, 0, tiled=False), axis=0)  13.7 us
    pallas_call x1, Pallas kernels, lagged_products(): pl.pallas_call(corr_kernel, grid=(pairs // LANES,), in_specs=[pl.BlockSpe...  9.82 us
    all_to_all x1, waiting for transfers between devices, summed_over(): return jnp.sum(lax.all_to_all(spread, axis, 0, 0, tiled=False), axis=0)  5.59 us
    ppermute x1, starting transfers between devices, local(): lax.ppermute(sent, 'chan', [(i + 1, i) for i in range(group_count - 1)])  3.9 us
    ppermute x1, waiting for transfers between devices, local(): lax.ppermute(sent, 'chan', [(i + 1, i) for i in range(group_count - 1)])  3.29 us
    ppermute x1, starting transfers between devices, local(): left_raw = lax.ppermute(trains[:, BINS_DEV - MAXLAG:], 'tm', to_next)  3.14 us
    dot_general x2, matrix products, gather_columns(): lax.dot_general(rows, onehot.astype(rows.dtype), (((0,), (0,)), ((), ()))...  2.9 us
  transfers between devices with their start and end apart: 3, of which 2 were waited for; matrix products, arithmetic and copies ran while one was open for 0% of the time, Pallas kernels for 0%

profile of v12, /device:TPU:1, one launch (start us, length us, event | category | flops | bytes accessed | tf_op | source)
XLA Modules:
  0.0 70.9 jit_solution(2746751157020144136)
XLA Ops:
  0.0 0.7 %broadcast_in_dim.41 = f32[1,4096]{1,0:T(1,128)S(1)} convert(bf16[1,4096]{1,0:T(2,128)(2,1)} %param.6) | non-fusion elementwise | flops 4096 | bytes 24576 | tf_op jit(solution)/shard_map/jit(_where)/broadcast_in_dim | solution.py:106
  0.8 0.0 copy-start
  0.8 2.6 %fusion.35 = (f32[384]{0:T(512)S(1)}, f32[384,256]{0,1:T(8,128)S(1)}) fusion(f32[4096]{0:T(1024)S(1)} %bitcast.9, s32[256]{0:T(256)S(1)} %add_multiply_fusion, s32[4096]{0:T(1024)} %bitcast.12, s32[4096]{0:T(1024)} %bitcast.13, s32[384]{0:T(512)S(1)} %iota_add_fusion), kind=kOutput, calls=%fused_computation.49 | convolution fusion | flops 812220032 | bytes 446464 | tf_op jit(solution)/shard_map/dot_general | solution.py:109
  3.4 0.6 broadcast_in_dim.38
  4.0 13.7 %all-to-all-start = ((f32[32,1,384]{2,1,0:T(1,128)}), f32[32,1,384]{2,1,0:T(1,128)S(1)}, u32[]{:S(2)}, u32[]{:S(2)}) async-start(f32[32,1,384]{2,1,0:T(1,128)} %broadcast_in_dim.38), calls=%async_computation | async-start | bytes 98304 | tf_op jit(solution)/shard_map/all_to_all | solution.py:85
  17.8 3.1 %collective-permute-start = (f32[384,50]{0,1:T(8,128)S(1)}, f32[384,50]{0,1:T(8,128)S(1)}, u32[]{:S(2)}, u32[]{:S(2)}) collective-permute-start(f32[384,50]{0,1:T(8,128)S(1)} %slice.20), channel_id=1, source_target_pairs={{0,1},{1,2},{2,3},{3,4},{4,5},{5,6},{6,7},{7,8},{8,9},{9,10},{10,1... | collective-permute-start | bytes 230408 | tf_op jit(solution)/shard_map/ppermute | solution.py:114
  20.9 0.0 copy-done
  20.9 5.6 %all-to-all-done = f32[32,1,384]{2,1,0:T(1,128)S(1)} async-done(((f32[32,1,384]{2,1,0:T(1,128)}), f32[32,1,384]{2,1,0:T(1,128)S(1)}, u32[]{:S(2)}, u32[]{:S(2)}) %all-to-all-start) | async-done | bytes 49184 | tf_op jit(solution)/shard_map/all_to_all | solution.py:85
  26.5 0.1 reduce_sum.28
  26.6 0.0 collective-permute-done
  26.7 1.4 %fusion.14.l_ref = bf16[320,1024]{1,0:T(8,128)(2,1)} fusion(s32[1024]{0:T(1024)S(1)} %bitcast.11, bf16[384,14]{0,1:T(8,128)(2,1)S(1)} %broadcast_in_dim.40, bf16[384,256]{0,1:T(8,128)(2,1)S(1)} %subtract_convert_fusion, bf16[384,50]{0,1:T(8,128)(2,1)S(1)} %fusion.29), kind=kOutput, calls=%fused_computation.19 | convolution fusion | flops 253116416 | bytes 905216 | tf_op jit(solution)/shard_map/dot_general | solution.py:90
  28.1 3.9 %collective-permute-start.1 = (bf16[64,320]{0,1:T(8,128)(2,1)S(1)}, bf16[64,320]{0,1:T(8,128)(2,1)S(1)}, u32[]{:S(2)}, u32[]{:S(2)}) collective-permute-start(bf16[64,320]{0,1:T(8,128)(2,1)S(1)} %pad_maximum_fusion), channel_id=1, source_target_pairs={{32,0},{64,32},{96,64},{128,96},{160,128},{192,160},{224,192},{256... | collective-permute-start | bytes 122888 | tf_op jit(solution)/shard_map/ppermute | solution.py:131
  32.1 3.3 %collective-permute-done.1 = bf16[64,320]{0,1:T(8,128)(2,1)S(1)} collective-permute-done((bf16[64,320]{0,1:T(8,128)(2,1)S(1)}, bf16[64,320]{0,1:T(8,128)(2,1)S(1)}, u32[]{:S(2)}, u32[]{:S(2)}) %collective-permute-start.1) | collective-permute-done | bytes 40992 | tf_op jit(solution)/shard_map/ppermute | solution.py:131
  35.3 1.5 %fusion.13.r_ref = bf16[320,1024]{1,0:T(8,128)(2,1)} fusion(s32[1024]{0:T(1024)S(1)} %bitcast.10, bf16[64,320]{0,1:T(8,128)(2,1)S(1)} %collective-permute-done.1, bf16[384,14]{0,1:T(8,128)(2,1)S(1)} %broadcast_in_dim.40, bf16[384,256]{0,1:T(8,128)(2,1)S(1)} %subtract_convert_fusion, bf16[384,50]{0,1:T(8,128)(2,1)S(1)} %fusion.29), kind=kOutput, calls=%fused_computation.18 | convolution fusion | flops 295534592 | bytes 946176 | tf_op jit(solution)/shard_map/dot_general | solution.py:90
  36.8 9.8 %shard_map.46 = f32[1024,128]{1,0:T(8,128)} custom-call(bf16[320,1024]{1,0:T(8,128)(2,1)} %fusion.14.l_ref, bf16[320,1024]{1,0:T(8,128)(2,1)} %fusion.13.r_ref), custom_call_target="tpu_custom_call" | custom-call | flops 52953088 | bytes 1835008 | tf_op jit(solution)/shard_map/pallas_call | solution.py:58
  46.7 23.6 %all_to_all.11 = f32[32,32,128]{2,1,0:T(8,128)S(1)} all-to-all(f32[32,32,128]{2,1,0:T(8,128)} %bitcast.8), channel_id=1, replica_groups=mesh['chan'=16,'tm'=32] {'tm'}, dimensions={0} | all-to-all | bytes 1048576 | tf_op jit(solution)/shard_map/all_to_all | solution.py:138
  70.3 0.6 slice_bitcast_fusion
  (10 shorter events, 0.2 us)
Async XLA Ops:
  0.8 20.2 %copy-start = (s32[2,1024]{1,0:T(2,128)S(1)}, s32[2,1024]{1,0:T(2,128)}, u32[]{:S(2)}) copy-start(s32[2,1024]{1,0:T(2,128)} %param.7) | copy-start | bytes 24580
  4.0 22.5 %all-to-all-start = ((f32[32,1,384]{2,1,0:T(1,128)}), f32[32,1,384]{2,1,0:T(1,128)S(1)}, u32[]{:S(2)}, u32[]{:S(2)}) async-start(f32[32,1,384]{2,1,0:T(1,128)} %broadcast_in_dim.38), calls=%async_computation | async-start | bytes 98304 | tf_op jit(solution)/shard_map/all_to_all | solution.py:85
  17.8 8.9 %collective-permute-start = (f32[384,50]{0,1:T(8,128)S(1)}, f32[384,50]{0,1:T(8,128)S(1)}, u32[]{:S(2)}, u32[]{:S(2)}) collective-permute-start(f32[384,50]{0,1:T(8,128)S(1)} %slice.20), channel_id=1, source_target_pairs={{0,1},{1,2},{2,3},{3,4},{4,5},{5,6},{6,7},{7,8},{8,9},{9,10},{10,1... | collective-permute-start | bytes 230408 | tf_op jit(solution)/shard_map/ppermute | solution.py:114
  28.1 7.2 %collective-permute-start.1 = (bf16[64,320]{0,1:T(8,128)(2,1)S(1)}, bf16[64,320]{0,1:T(8,128)(2,1)S(1)}, u32[]{:S(2)}, u32[]{:S(2)}) collective-permute-start(bf16[64,320]{0,1:T(8,128)(2,1)S(1)} %pad_maximum_fusion), channel_id=1, source_target_pairs={{32,0},{64,32},{96,64},{128,96},{160,128},{192,160},{224,192},{256... | collective-permute-start | bytes 122888 | tf_op jit(solution)/shard_map/ppermute | solution.py:131

commit v13 on v11

--- a/solution.py
+++ b/solution.py
@@ -14,13 +14,20 @@
 LANES = 128
 KCHUNK = 13
 WINDOW_PAD = 14
+STEP_BLOCKS = 2
 
 
 def corr_kernel(l_ref, r_ref, o_ref, lf_ref, rf_ref, left_ref, right_ref, lags_ref):
+    for sub in range(l_ref.shape[1] // LANES):
+        lane_block(l_ref, r_ref, o_ref, lf_ref, rf_ref, left_ref, right_ref, lags_ref, sub)
+
+
+def lane_block(l_ref, r_ref, o_ref, lf_ref, rf_ref, left_ref, right_ref, lags_ref, sub):
+    lanes = pl.ds(sub * LANES, LANES)
     steps = (l_ref.shape[0] - MAXLAG - WINDOW_PAD) // 8
     width = left_ref.shape[1]
-    lf_ref[...] = l_ref[...].astype(jnp.float32)
-    rf_ref[...] = r_ref[...].astype(jnp.float32)
+    lf_ref[...] = l_ref[:, lanes].astype(jnp.float32)
+    rf_ref[...] = r_ref[:, lanes].astype(jnp.float32)
     for r in range(8):
         left_ref[r] = lf_ref[pl.ds(r, width), :]
         right_ref[r] = rf_ref[pl.ds(r, width), :]
@@ -49,7 +56,7 @@
             lambda k: 2 * MAXLAG - k,
         )
     lags_ref[pl.ds(NLAG, LANES - NLAG), :] = jnp.zeros((LANES - NLAG, LANES), jnp.float32)
-    o_ref[...] = lags_ref[...].T
+    o_ref[pl.ds(sub * LANES, LANES), :] = lags_ref[...].T
 
 
 def lagged_products(left_t, right_t):
@@ -57,12 +64,12 @@
     bins = left_t.shape[0] - MAXLAG - WINDOW_PAD
     return pl.pallas_call(
         corr_kernel,
-        grid=(pairs // LANES,),
+        grid=(pairs // (LANES * STEP_BLOCKS),),
         in_specs=[
-            pl.BlockSpec((left_t.shape[0], LANES), lambda j: (0, j)),
-            pl.BlockSpec((right_t.shape[0], LANES), lambda j: (0, j)),
+            pl.BlockSpec((left_t.shape[0], LANES * STEP_BLOCKS), lambda j: (0, j)),
+            pl.BlockSpec((right_t.shape[0], LANES * STEP_BLOCKS), lambda j: (0, j)),
         ],
-        out_specs=pl.BlockSpec((LANES, LANES), lambda j: (j, 0)),
+        out_specs=pl.BlockSpec((LANES * STEP_BLOCKS, LANES), lambda j: (j, 0)),
         out_shape=jax.ShapeDtypeStruct((pairs, LANES), jnp.float32),
         scratch_shapes=[
             pltpu.VMEM((left_t.shape[0], LANES), jnp.float32),

time: 70 us -> 71 us (1.014)
  Pallas kernels: 9.82 us -> 10.9 us
    pallas_call x1, Pallas kernels: 9.82 us -> 10.9 us  [lagged_products(): pl.pallas_call(corr_kernel, grid=(pairs // (LANES * STEP_BLOCKS),), in_sp...]
where the time goes in v13:
time: 71 us; the launch traced here: 70.5 us
  blocking collectives  23.6 us (33%)
  starting transfers between devices  20.8 us (29%)
  Pallas kernels  10.9 us (15%)
  waiting for transfers between devices  7.46 us (11%)
  matrix products  5.51 us (8%)
  local copies, waits for them, and re-layouts  1.28 us (2%)
  other arithmetic  0.94 us (1%)
    all_to_all x1, blocking collectives, local(): summed = jnp.sum(lax.all_to_all(blocks, 'tm', 0, 0, tiled=False), axis=0)  23.6 us
    all_to_all x1, starting transfers between devices, summed_over(): return jnp.sum(lax.all_to_all(spread, axis, 0, 0, tiled=False), axis=0)  13.7 us
    pallas_call x1, Pallas kernels, lagged_products(): pl.pallas_call(corr_kernel, grid=(pairs // (LANES * STEP_BLOCKS),), in_sp...  10.9 us
    all_to_all x1, waiting for transfers between devices, summed_over(): return jnp.sum(lax.all_to_all(spread, axis, 0, 0, tiled=False), axis=0)  5.59 us
    ppermute x1, starting transfers between devices, local(): lax.ppermute(window_own[:BORDER], 'chan', [(i + 1, i) for i in range(grou...  3.91 us
    ppermute x1, starting transfers between devices, local(): left_raw = lax.ppermute(trains[:, BINS_DEV - MAXLAG:], 'tm', to_next)  3.14 us
    dot_general x2, matrix products, gather_columns(): lax.dot_general(rows, onehot.astype(rows.dtype), (((0,), (0,)), ((), ()))...  2.9 us
    dot_general x1, matrix products, local(): lax.dot_general(unit_onehot, weighted, (((1,), (1,)), ((), ())), preferre...  2.61 us
  transfers between devices with their start and end apart: 3, of which 2 were waited for; matrix products, arithmetic and copies ran while one was open for 2% of the time, Pallas kernels for 0%

profile of v13, /device:TPU:1, one launch (start us, length us, event | category | flops | bytes accessed | tf_op | source)
XLA Modules:
  0.0 70.5 jit_solution(13348766600408460498)
XLA Ops:
  0.0 0.7 %broadcast_in_dim.41 = f32[1,4096]{1,0:T(1,128)S(1)} convert(bf16[1,4096]{1,0:T(2,128)(2,1)} %param.6) | non-fusion elementwise | flops 4096 | bytes 24576 | tf_op jit(solution)/shard_map/jit(_where)/broadcast_in_dim | solution.py:113
  0.8 0.0 copy-start
  0.8 2.6 %fusion.35 = (f32[384]{0:T(512)S(1)}, f32[384,256]{0,1:T(8,128)S(1)}) fusion(f32[4096]{0:T(1024)S(1)} %bitcast.9, s32[256]{0:T(256)S(1)} %add_multiply_fusion, s32[4096]{0:T(1024)} %bitcast.12, s32[4096]{0:T(1024)} %bitcast.13, s32[384]{0:T(512)S(1)} %iota_add_fusion), kind=kOutput, calls=%fused_computation.49 | convolution fusion | flops 812220032 | bytes 446464 | tf_op jit(solution)/shard_map/dot_general | solution.py:116
  3.4 0.6 broadcast_in_dim.38
  4.0 13.7 %all-to-all-start = ((f32[32,1,384]{2,1,0:T(1,128)}), f32[32,1,384]{2,1,0:T(1,128)S(1)}, u32[]{:S(2)}, u32[]{:S(2)}) async-start(f32[32,1,384]{2,1,0:T(1,128)} %broadcast_in_dim.38), calls=%async_computation | async-start | bytes 98304 | tf_op jit(solution)/shard_map/all_to_all | solution.py:92
  17.8 3.1 %collective-permute-start = (f32[384,50]{0,1:T(8,128)S(1)}, f32[384,50]{0,1:T(8,128)S(1)}, u32[]{:S(2)}, u32[]{:S(2)}) collective-permute-start(f32[384,50]{0,1:T(8,128)S(1)} %slice.20), channel_id=1, source_target_pairs={{0,1},{1,2},{2,3},{3,4},{4,5},{5,6},{6,7},{7,8},{8,9},{9,10},{10,1... | collective-permute-start | bytes 230408 | tf_op jit(solution)/shard_map/ppermute | solution.py:121
  20.9 0.0 copy-done
  20.9 5.6 %all-to-all-done = f32[32,1,384]{2,1,0:T(1,128)S(1)} async-done(((f32[32,1,384]{2,1,0:T(1,128)}), f32[32,1,384]{2,1,0:T(1,128)S(1)}, u32[]{:S(2)}, u32[]{:S(2)}) %all-to-all-start) | async-done | bytes 49184 | tf_op jit(solution)/shard_map/all_to_all | solution.py:92
  26.5 0.1 reduce_sum.28
  26.6 0.0 collective-permute-done
  26.7 3.9 %collective-permute-start.1 = (bf16[64,320]{0,1:T(8,128)(2,1)S(1)}, bf16[64,320]{0,1:T(8,128)(2,1)S(1)}, u32[]{:S(2)}, u32[]{:S(2)}) collective-permute-start(bf16[64,320]{0,1:T(8,128)(2,1)S(1)} %pad_maximum_fusion), channel_id=1, source_target_pairs={{32,0},{64,32},{96,64},{128,96},{160,128},{192,160},{224,192},{256... | collective-permute-start | bytes 122888 | tf_op jit(solution)/shard_map/ppermute | solution.py:133
  30.6 1.4 %fusion.14.l_ref = bf16[320,1024]{1,0:T(8,128)(2,1)} fusion(s32[1024]{0:T(1024)S(1)} %bitcast.11, bf16[384,14]{0,1:T(8,128)(2,1)S(1)} %broadcast_in_dim.40, bf16[384,256]{0,1:T(8,128)(2,1)S(1)} %subtract_convert_fusion, bf16[384,50]{0,1:T(8,128)(2,1)S(1)} %fusion.29), kind=kOutput, calls=%fused_computation.19 | convolution fusion | flops 253116416 | bytes 905216 | tf_op jit(solution)/shard_map/dot_general | solution.py:97
  32.1 1.9 %collective-permute-done.1 = bf16[64,320]{0,1:T(8,128)(2,1)S(1)} collective-permute-done((bf16[64,320]{0,1:T(8,128)(2,1)S(1)}, bf16[64,320]{0,1:T(8,128)(2,1)S(1)}, u32[]{:S(2)}, u32[]{:S(2)}) %collective-permute-start.1) | collective-permute-done | bytes 40992 | tf_op jit(solution)/shard_map/ppermute | solution.py:133
  33.9 1.5 %fusion.13.r_ref = bf16[320,1024]{1,0:T(8,128)(2,1)} fusion(s32[1024]{0:T(1024)S(1)} %bitcast.10, bf16[64,320]{0,1:T(8,128)(2,1)S(1)} %collective-permute-done.1, bf16[384,14]{0,1:T(8,128)(2,1)S(1)} %broadcast_in_dim.40, bf16[384,256]{0,1:T(8,128)(2,1)S(1)} %subtract_convert_fusion, bf16[384,50]{0,1:T(8,128)(2,1)S(1)} %fusion.29), kind=kOutput, calls=%fused_computation.18 | convolution fusion | flops 295534592 | bytes 946176 | tf_op jit(solution)/shard_map/dot_general | solution.py:97
  35.4 10.9 %shard_map.46 = f32[1024,128]{1,0:T(8,128)} custom-call(bf16[320,1024]{1,0:T(8,128)(2,1)} %fusion.14.l_ref, bf16[320,1024]{1,0:T(8,128)(2,1)} %fusion.13.r_ref), custom_call_target="tpu_custom_call" | custom-call | flops 52953088 | bytes 1835008 | tf_op jit(solution)/shard_map/pallas_call | solution.py:65
  46.3 23.6 %all_to_all.11 = f32[32,32,128]{2,1,0:T(8,128)S(1)} all-to-all(f32[32,32,128]{2,1,0:T(8,128)} %bitcast.8), channel_id=1, replica_groups=mesh['chan'=16,'tm'=32] {'tm'}, dimensions={0} | all-to-all | bytes 1048576 | tf_op jit(solution)/shard_map/all_to_all | solution.py:146
  69.9 0.6 slice_bitcast_fusion
  (10 shorter events, 0.2 us)
Async XLA Ops:
  0.8 20.2 %copy-start = (s32[2,1024]{1,0:T(2,128)S(1)}, s32[2,1024]{1,0:T(2,128)}, u32[]{:S(2)}) copy-start(s32[2,1024]{1,0:T(2,128)} %param.7) | copy-start | bytes 24580
  4.0 22.5 %all-to-all-start = ((f32[32,1,384]{2,1,0:T(1,128)}), f32[32,1,384]{2,1,0:T(1,128)S(1)}, u32[]{:S(2)}, u32[]{:S(2)}) async-start(f32[32,1,384]{2,1,0:T(1,128)} %broadcast_in_dim.38), calls=%async_computation | async-start | bytes 98304 | tf_op jit(solution)/shard_map/all_to_all | solution.py:92
  17.8 8.9 %collective-permute-start = (f32[384,50]{0,1:T(8,128)S(1)}, f32[384,50]{0,1:T(8,128)S(1)}, u32[]{:S(2)}, u32[]{:S(2)}) collective-permute-start(f32[384,50]{0,1:T(8,128)S(1)} %slice.20), channel_id=1, source_target_pairs={{0,1},{1,2},{2,3},{3,4},{4,5},{5,6},{6,7},{7,8},{8,9},{9,10},{10,1... | collective-permute-start | bytes 230408 | tf_op jit(solution)/shard_map/ppermute | solution.py:121
  26.7 7.2 %collective-permute-start.1 = (bf16[64,320]{0,1:T(8,128)(2,1)S(1)}, bf16[64,320]{0,1:T(8,128)(2,1)S(1)}, u32[]{:S(2)}, u32[]{:S(2)}) collective-permute-start(bf16[64,320]{0,1:T(8,128)(2,1)S(1)} %pad_maximum_fusion), channel_id=1, source_target_pairs={{32,0},{64,32},{96,64},{128,96},{160,128},{192,160},{224,192},{256... | collective-permute-start | bytes 122888 | tf_op jit(solution)/shard_map/ppermute | solution.py:133

commit v14 on v11

--- a/solution.py
+++ b/solution.py
@@ -21,18 +21,19 @@
     width = left_ref.shape[1]
     lf_ref[...] = l_ref[...].astype(jnp.float32)
     rf_ref[...] = r_ref[...].astype(jnp.float32)
-    for r in range(8):
+    for r in range(1, 8):
         left_ref[r] = lf_ref[pl.ds(r, width), :]
         right_ref[r] = rf_ref[pl.ds(r, width), :]
 
-    def lag_rows(fixed_ref, moving_ref, lags, shift_of):
+    def lag_rows(fixed_ref, moving_ref, moving_flat, lags, shift_of):
+        def moved(shift, t):
+            rows = pl.ds(t + 8 * (shift // 8), 8)
+            return moving_flat[rows, :] if shift % 8 == 0 else moving_ref[shift % 8, rows, :]
+
         def body(i, accs):
             t = pl.multiple_of(i * 8, 8)
             fixed = fixed_ref[MAXLAG % 8, pl.ds(t + 8 * (MAXLAG // 8), 8), :]
-            return tuple(
-                a + fixed * moving_ref[shift_of(k) % 8, pl.ds(t + 8 * (shift_of(k) // 8), 8), :]
-                for a, k in zip(accs, lags)
-            )
+            return tuple(a + fixed * moved(shift_of(k), t) for a, k in zip(accs, lags))
 
         accs = lax.fori_loop(
             0, steps, body, tuple(jnp.zeros((8, LANES), jnp.float32) for _ in lags),
@@ -42,10 +43,13 @@
             lags_ref[pl.ds(k, 1), :] = jnp.sum(a, axis=0, keepdims=True)
 
     for first in range(0, MAXLAG, KCHUNK):
-        lag_rows(left_ref, right_ref, list(range(first, min(first + KCHUNK, MAXLAG))), lambda k: k)
+        lag_rows(
+            left_ref, right_ref, rf_ref, list(range(first, min(first + KCHUNK, MAXLAG))),
+            lambda k: k,
+        )
     for first in range(MAXLAG, NLAG, KCHUNK):
         lag_rows(
-            right_ref, left_ref, list(range(first, min(first + KCHUNK, NLAG))),
+            right_ref, left_ref, lf_ref, list(range(first, min(first + KCHUNK, NLAG))),
             lambda k: 2 * MAXLAG - k,
         )
     lags_ref[pl.ds(NLAG, LANES - NLAG), :] = jnp.zeros((LANES - NLAG, LANES), jnp.float32)

time: 70 us -> 70 us (level)
  no operation moved by 1% of the time
where the time goes in v14:
time: 70 us; the launch traced here: 69.5 us
  blocking collectives  23.6 us (34%)
  starting transfers between devices  20.8 us (30%)
  Pallas kernels  9.86 us (14%)
  waiting for transfers between devices  7.46 us (11%)
  matrix products  5.51 us (8%)
  local copies, waits for them, and re-layouts  1.28 us (2%)
  other arithmetic  0.94 us (1%)
    all_to_all x1, blocking collectives, local(): summed = jnp.sum(lax.all_to_all(blocks, 'tm', 0, 0, tiled=False), axis=0)  23.6 us
    all_to_all x1, starting transfers between devices, summed_over(): return jnp.sum(lax.all_to_all(spread, axis, 0, 0, tiled=False), axis=0)  13.7 us
    pallas_call x1, Pallas kernels, lagged_products(): pl.pallas_call(corr_kernel, grid=(pairs // LANES,), in_specs=[pl.BlockSpe...  9.86 us
    all_to_all x1, waiting for transfers between devices, summed_over(): return jnp.sum(lax.all_to_all(spread, axis, 0, 0, tiled=False), axis=0)  5.59 us
    ppermute x1, starting transfers between devices, local(): lax.ppermute(window_own[:BORDER], 'chan', [(i + 1, i) for i in range(grou...  3.91 us
    ppermute x1, starting transfers between devices, local(): left_raw = lax.ppermute(trains[:, BINS_DEV - MAXLAG:], 'tm', to_next)  3.14 us
    dot_general x2, matrix products, gather_columns(): lax.dot_general(rows, onehot.astype(rows.dtype), (((0,), (0,)), ((), ()))...  2.9 us
    dot_general x1, matrix products, local(): lax.dot_general(unit_onehot, weighted, (((1,), (1,)), ((), ())), preferre...  2.61 us
  transfers between devices with their start and end apart: 3, of which 2 were waited for; matrix products, arithmetic and copies ran while one was open for 2% of the time, Pallas kernels for 0%

profile of v14, /device:TPU:1, one launch (start us, length us, event | category | flops | bytes accessed | tf_op | source)
XLA Modules:
  0.0 69.5 jit_solution(12042722219744716162)
XLA Ops:
  0.0 0.7 %broadcast_in_dim.41 = f32[1,4096]{1,0:T(1,128)S(1)} convert(bf16[1,4096]{1,0:T(2,128)(2,1)} %param.6) | non-fusion elementwise | flops 4096 | bytes 24576 | tf_op jit(solution)/shard_map/jit(_where)/broadcast_in_dim | solution.py:110
  0.8 0.0 copy-start
  0.8 2.6 %fusion.35 = (f32[384]{0:T(512)S(1)}, f32[384,256]{0,1:T(8,128)S(1)}) fusion(f32[4096]{0:T(1024)S(1)} %bitcast.9, s32[256]{0:T(256)S(1)} %add_multiply_fusion, s32[4096]{0:T(1024)} %bitcast.12, s32[4096]{0:T(1024)} %bitcast.13, s32[384]{0:T(512)S(1)} %iota_add_fusion), kind=kOutput, calls=%fused_computation.49 | convolution fusion | flops 812220032 | bytes 446464 | tf_op jit(solution)/shard_map/dot_general | solution.py:113
  3.4 0.6 broadcast_in_dim.38
  4.0 13.7 %all-to-all-start = ((f32[32,1,384]{2,1,0:T(1,128)}), f32[32,1,384]{2,1,0:T(1,128)S(1)}, u32[]{:S(2)}, u32[]{:S(2)}) async-start(f32[32,1,384]{2,1,0:T(1,128)} %broadcast_in_dim.38), calls=%async_computation | async-start | bytes 98304 | tf_op jit(solution)/shard_map/all_to_all | solution.py:89
  17.8 3.1 %collective-permute-start = (f32[384,50]{0,1:T(8,128)S(1)}, f32[384,50]{0,1:T(8,128)S(1)}, u32[]{:S(2)}, u32[]{:S(2)}) collective-permute-start(f32[384,50]{0,1:T(8,128)S(1)} %slice.20), channel_id=1, source_target_pairs={{0,1},{1,2},{2,3},{3,4},{4,5},{5,6},{6,7},{7,8},{8,9},{9,10},{10,1... | collective-permute-start | bytes 230408 | tf_op jit(solution)/shard_map/ppermute | solution.py:118
  20.9 0.0 copy-done
  20.9 5.6 %all-to-all-done = f32[32,1,384]{2,1,0:T(1,128)S(1)} async-done(((f32[32,1,384]{2,1,0:T(1,128)}), f32[32,1,384]{2,1,0:T(1,128)S(1)}, u32[]{:S(2)}, u32[]{:S(2)}) %all-to-all-start) | async-done | bytes 49184 | tf_op jit(solution)/shard_map/all_to_all | solution.py:89
  26.5 0.1 reduce_sum.28
  26.6 0.0 collective-permute-done
  26.7 3.9 %collective-permute-start.1 = (bf16[64,320]{0,1:T(8,128)(2,1)S(1)}, bf16[64,320]{0,1:T(8,128)(2,1)S(1)}, u32[]{:S(2)}, u32[]{:S(2)}) collective-permute-start(bf16[64,320]{0,1:T(8,128)(2,1)S(1)} %pad_maximum_fusion), channel_id=1, source_target_pairs={{32,0},{64,32},{96,64},{128,96},{160,128},{192,160},{224,192},{256... | collective-permute-start | bytes 122888 | tf_op jit(solution)/shard_map/ppermute | solution.py:130
  30.6 1.4 %fusion.14.l_ref = bf16[320,1024]{1,0:T(8,128)(2,1)} fusion(s32[1024]{0:T(1024)S(1)} %bitcast.11, bf16[384,14]{0,1:T(8,128)(2,1)S(1)} %broadcast_in_dim.40, bf16[384,256]{0,1:T(8,128)(2,1)S(1)} %subtract_convert_fusion, bf16[384,50]{0,1:T(8,128)(2,1)S(1)} %fusion.29), kind=kOutput, calls=%fused_computation.19 | convolution fusion | flops 253116416 | bytes 905216 | tf_op jit(solution)/shard_map/dot_general | solution.py:94
  32.1 1.9 %collective-permute-done.1 = bf16[64,320]{0,1:T(8,128)(2,1)S(1)} collective-permute-done((bf16[64,320]{0,1:T(8,128)(2,1)S(1)}, bf16[64,320]{0,1:T(8,128)(2,1)S(1)}, u32[]{:S(2)}, u32[]{:S(2)}) %collective-permute-start.1) | collective-permute-done | bytes 40992 | tf_op jit(solution)/shard_map/ppermute | solution.py:130
  33.9 1.5 %fusion.13.r_ref = bf16[320,1024]{1,0:T(8,128)(2,1)} fusion(s32[1024]{0:T(1024)S(1)} %bitcast.10, bf16[64,320]{0,1:T(8,128)(2,1)S(1)} %collective-permute-done.1, bf16[384,14]{0,1:T(8,128)(2,1)S(1)} %broadcast_in_dim.40, bf16[384,256]{0,1:T(8,128)(2,1)S(1)} %subtract_convert_fusion, bf16[384,50]{0,1:T(8,128)(2,1)S(1)} %fusion.29), kind=kOutput, calls=%fused_computation.18 | convolution fusion | flops 295534592 | bytes 946176 | tf_op jit(solution)/shard_map/dot_general | solution.py:94
  35.4 9.9 %shard_map.46 = f32[1024,128]{1,0:T(8,128)} custom-call(bf16[320,1024]{1,0:T(8,128)(2,1)} %fusion.14.l_ref, bf16[320,1024]{1,0:T(8,128)(2,1)} %fusion.13.r_ref), custom_call_target="tpu_custom_call" | custom-call | flops 52953088 | bytes 1835008 | tf_op jit(solution)/shard_map/pallas_call | solution.py:62
  45.3 23.6 %all_to_all.11 = f32[32,32,128]{2,1,0:T(8,128)S(1)} all-to-all(f32[32,32,128]{2,1,0:T(8,128)} %bitcast.8), channel_id=1, replica_groups=mesh['chan'=16,'tm'=32] {'tm'}, dimensions={0} | all-to-all | bytes 1048576 | tf_op jit(solution)/shard_map/all_to_all | solution.py:143
  68.9 0.6 slice_bitcast_fusion
  (10 shorter events, 0.2 us)
Async XLA Ops:
  0.8 20.2 %copy-start = (s32[2,1024]{1,0:T(2,128)S(1)}, s32[2,1024]{1,0:T(2,128)}, u32[]{:S(2)}) copy-start(s32[2,1024]{1,0:T(2,128)} %param.7) | copy-start | bytes 24580
  4.0 22.5 %all-to-all-start = ((f32[32,1,384]{2,1,0:T(1,128)}), f32[32,1,384]{2,1,0:T(1,128)S(1)}, u32[]{:S(2)}, u32[]{:S(2)}) async-start(f32[32,1,384]{2,1,0:T(1,128)} %broadcast_in_dim.38), calls=%async_computation | async-start | bytes 98304 | tf_op jit(solution)/shard_map/all_to_all | solution.py:89
  17.8 8.9 %collective-permute-start = (f32[384,50]{0,1:T(8,128)S(1)}, f32[384,50]{0,1:T(8,128)S(1)}, u32[]{:S(2)}, u32[]{:S(2)}) collective-permute-start(f32[384,50]{0,1:T(8,128)S(1)} %slice.20), channel_id=1, source_target_pairs={{0,1},{1,2},{2,3},{3,4},{4,5},{5,6},{6,7},{7,8},{8,9},{9,10},{10,1... | collective-permute-start | bytes 230408 | tf_op jit(solution)/shard_map/ppermute | solution.py:118
  26.7 7.2 %collective-permute-start.1 = (bf16[64,320]{0,1:T(8,128)(2,1)S(1)}, bf16[64,320]{0,1:T(8,128)(2,1)S(1)}, u32[]{:S(2)}, u32[]{:S(2)}) collective-permute-start(bf16[64,320]{0,1:T(8,128)(2,1)S(1)} %pad_maximum_fusion), channel_id=1, source_target_pairs={{32,0},{64,32},{96,64},{128,96},{160,128},{192,160},{224,192},{256... | collective-permute-start | bytes 122888 | tf_op jit(solution)/shard_map/ppermute | solution.py:130

commit v15 on v11

--- a/solution.py
+++ b/solution.py
@@ -135,9 +135,9 @@
     partial = lagged_products(left_t, right_t)
 
     per_shard = partial.shape[0] // shard_count
-    blocks = partial.reshape(shard_count, per_shard, LANES)
-    summed = jnp.sum(lax.all_to_all(blocks, "tm", 0, 0, tiled=False), axis=0)
-    return summed[:, :NLAG].T
+    blocks = partial.reshape(shard_count, 1, per_shard * LANES)
+    summed = jnp.sum(lax.all_to_all(blocks, "tm", 0, 0, tiled=False), axis=(0, 1))
+    return summed.reshape(per_shard, LANES)[:, :NLAG].T
 
 
 def solution(mesh):

time: 70 us -> 70.3 us (level)
  no operation moved by 1% of the time
where the time goes in v15:
time: 70.3 us; the launch traced here: 69.8 us
  blocking collectives  23.6 us (34%)
  starting transfers between devices  20.8 us (30%)
  Pallas kernels  9.82 us (14%)
  waiting for transfers between devices  7.46 us (11%)
  matrix products  5.51 us (8%)
  local copies, waits for them, and re-layouts  1.28 us (2%)
  other arithmetic  1.25 us (2%)
    all_to_all x1, blocking collectives, local(): lax.all_to_all(blocks, 'tm', 0, 0, tiled=False)  23.6 us
    all_to_all x1, starting transfers between devices, summed_over(): return jnp.sum(lax.all_to_all(spread, axis, 0, 0, tiled=False), axis=0)  13.7 us
    pallas_call x1, Pallas kernels, lagged_products(): pl.pallas_call(corr_kernel, grid=(pairs // LANES,), in_specs=[pl.BlockSpe...  9.82 us
    all_to_all x1, waiting for transfers between devices, summed_over(): return jnp.sum(lax.all_to_all(spread, axis, 0, 0, tiled=False), axis=0)  5.59 us
    ppermute x1, starting transfers between devices, local(): lax.ppermute(window_own[:BORDER], 'chan', [(i + 1, i) for i in range(grou...  3.91 us
    ppermute x1, starting transfers between devices, local(): left_raw = lax.ppermute(trains[:, BINS_DEV - MAXLAG:], 'tm', to_next)  3.14 us
    dot_general x2, matrix products, gather_columns(): lax.dot_general(rows, onehot.astype(rows.dtype), (((0,), (0,)), ((), ()))...  2.9 us
    dot_general x1, matrix products, local(): lax.dot_general(unit_onehot, weighted, (((1,), (1,)), ((), ())), preferre...  2.61 us
  transfers between devices with their start and end apart: 3, of which 2 were waited for; matrix products, arithmetic and copies ran while one was open for 2% of the time, Pallas kernels for 0%

profile of v15, /device:TPU:1, one launch (start us, length us, event | category | flops | bytes accessed | tf_op | source)
XLA Modules:
  0.0 69.8 jit_solution(12394214899865312489)
XLA Ops:
  0.0 0.7 %broadcast_in_dim.41 = f32[1,4096]{1,0:T(1,128)S(1)} convert(bf16[1,4096]{1,0:T(2,128)(2,1)} %param.6) | non-fusion elementwise | flops 4096 | bytes 24576 | tf_op jit(solution)/shard_map/jit(_where)/broadcast_in_dim | solution.py:106
  0.8 0.0 copy-start
  0.8 2.6 %fusion.35 = (f32[384]{0:T(512)S(1)}, f32[384,256]{0,1:T(8,128)S(1)}) fusion(f32[4096]{0:T(1024)S(1)} %bitcast.11, s32[256]{0:T(256)S(1)} %add_multiply_fusion, s32[4096]{0:T(1024)} %bitcast.14, s32[4096]{0:T(1024)} %bitcast.15, s32[384]{0:T(512)S(1)} %iota_add_fusion), kind=kOutput, calls=%fused_computation.49 | convolution fusion | flops 812220032 | bytes 446464 | tf_op jit(solution)/shard_map/dot_general | solution.py:109
  3.4 0.6 broadcast_in_dim.38
  4.0 13.7 %all-to-all-start = ((f32[32,1,384]{2,1,0:T(1,128)}), f32[32,1,384]{2,1,0:T(1,128)S(1)}, u32[]{:S(2)}, u32[]{:S(2)}) async-start(f32[32,1,384]{2,1,0:T(1,128)} %broadcast_in_dim.38), calls=%async_computation | async-start | bytes 98304 | tf_op jit(solution)/shard_map/all_to_all | solution.py:85
  17.8 3.1 %collective-permute-start = (f32[384,50]{0,1:T(8,128)S(1)}, f32[384,50]{0,1:T(8,128)S(1)}, u32[]{:S(2)}, u32[]{:S(2)}) collective-permute-start(f32[384,50]{0,1:T(8,128)S(1)} %slice.20), channel_id=1, source_target_pairs={{0,1},{1,2},{2,3},{3,4},{4,5},{5,6},{6,7},{7,8},{8,9},{9,10},{10,1... | collective-permute-start | bytes 230408 | tf_op jit(solution)/shard_map/ppermute | solution.py:114
  20.9 0.0 copy-done
  20.9 5.6 %all-to-all-done = f32[32,1,384]{2,1,0:T(1,128)S(1)} async-done(((f32[32,1,384]{2,1,0:T(1,128)}), f32[32,1,384]{2,1,0:T(1,128)S(1)}, u32[]{:S(2)}, u32[]{:S(2)}) %all-to-all-start) | async-done | bytes 49184 | tf_op jit(solution)/shard_map/all_to_all | solution.py:85
  26.5 0.1 reduce_sum.28
  26.6 0.0 collective-permute-done
  26.7 3.9 %collective-permute-start.1 = (bf16[64,320]{0,1:T(8,128)(2,1)S(1)}, bf16[64,320]{0,1:T(8,128)(2,1)S(1)}, u32[]{:S(2)}, u32[]{:S(2)}) collective-permute-start(bf16[64,320]{0,1:T(8,128)(2,1)S(1)} %pad_maximum_fusion), channel_id=1, source_target_pairs={{32,0},{64,32},{96,64},{128,96},{160,128},{192,160},{224,192},{256... | collective-permute-start | bytes 122888 | tf_op jit(solution)/shard_map/ppermute | solution.py:126
  30.6 1.4 %fusion.14.l_ref = bf16[320,1024]{1,0:T(8,128)(2,1)} fusion(s32[1024]{0:T(1024)S(1)} %bitcast.13, bf16[384,14]{0,1:T(8,128)(2,1)S(1)} %broadcast_in_dim.40, bf16[384,256]{0,1:T(8,128)(2,1)S(1)} %subtract_convert_fusion, bf16[384,50]{0,1:T(8,128)(2,1)S(1)} %fusion.29), kind=kOutput, calls=%fused_computation.19 | convolution fusion | flops 253116416 | bytes 905216 | tf_op jit(solution)/shard_map/dot_general | solution.py:90
  32.1 1.9 %collective-permute-done.1 = bf16[64,320]{0,1:T(8,128)(2,1)S(1)} collective-permute-done((bf16[64,320]{0,1:T(8,128)(2,1)S(1)}, bf16[64,320]{0,1:T(8,128)(2,1)S(1)}, u32[]{:S(2)}, u32[]{:S(2)}) %collective-permute-start.1) | collective-permute-done | bytes 40992 | tf_op jit(solution)/shard_map/ppermute | solution.py:126
  33.9 1.5 %fusion.13.r_ref = bf16[320,1024]{1,0:T(8,128)(2,1)} fusion(s32[1024]{0:T(1024)S(1)} %bitcast.12, bf16[64,320]{0,1:T(8,128)(2,1)S(1)} %collective-permute-done.1, bf16[384,14]{0,1:T(8,128)(2,1)S(1)} %broadcast_in_dim.40, bf16[384,256]{0,1:T(8,128)(2,1)S(1)} %subtract_convert_fusion, bf16[384,50]{0,1:T(8,128)(2,1)S(1)} %fusion.29), kind=kOutput, calls=%fused_computation.18 | convolution fusion | flops 295534592 | bytes 946176 | tf_op jit(solution)/shard_map/dot_general | solution.py:90
  35.4 9.8 %shard_map.46 = f32[1024,128]{1,0:T(8,128)} custom-call(bf16[320,1024]{1,0:T(8,128)(2,1)} %fusion.14.l_ref, bf16[320,1024]{1,0:T(8,128)(2,1)} %fusion.13.r_ref), custom_call_target="tpu_custom_call" | custom-call | flops 52953088 | bytes 1835008 | tf_op jit(solution)/shard_map/pallas_call | solution.py:58
  45.2 23.6 %all_to_all.11 = f32[32,1,4096]{2,1,0:T(1,128)S(1)} all-to-all(f32[32,1,4096]{2,1,0:T(1,128)} %bitcast.9), channel_id=1, replica_groups=mesh['chan'=16,'tm'=32] {'tm'}, dimensions={0} | all-to-all | bytes 1048576 | tf_op jit(solution)/shard_map/all_to_all | solution.py:139
  68.8 0.4 reduce_sum.29
  69.2 0.6 slice_bitcast_fusion
  (9 shorter events, 0.1 us)
Async XLA Ops:
  0.8 20.2 %copy-start = (s32[2,1024]{1,0:T(2,128)S(1)}, s32[2,1024]{1,0:T(2,128)}, u32[]{:S(2)}) copy-start(s32[2,1024]{1,0:T(2,128)} %param.7) | copy-start | bytes 24580
  4.0 22.5 %all-to-all-start = ((f32[32,1,384]{2,1,0:T(1,128)}), f32[32,1,384]{2,1,0:T(1,128)S(1)}, u32[]{:S(2)}, u32[]{:S(2)}) async-start(f32[32,1,384]{2,1,0:T(1,128)} %broadcast_in_dim.38), calls=%async_computation | async-start | bytes 98304 | tf_op jit(solution)/shard_map/all_to_all | solution.py:85
  17.8 8.9 %collective-permute-start = (f32[384,50]{0,1:T(8,128)S(1)}, f32[384,50]{0,1:T(8,128)S(1)}, u32[]{:S(2)}, u32[]{:S(2)}) collective-permute-start(f32[384,50]{0,1:T(8,128)S(1)} %slice.20), channel_id=1, source_target_pairs={{0,1},{1,2},{2,3},{3,4},{4,5},{5,6},{6,7},{7,8},{8,9},{9,10},{10,1... | collective-permute-start | bytes 230408 | tf_op jit(solution)/shard_map/ppermute | solution.py:114
  26.7 7.2 %collective-permute-start.1 = (bf16[64,320]{0,1:T(8,128)(2,1)S(1)}, bf16[64,320]{0,1:T(8,128)(2,1)S(1)}, u32[]{:S(2)}, u32[]{:S(2)}) collective-permute-start(bf16[64,320]{0,1:T(8,128)(2,1)S(1)} %pad_maximum_fusion), channel_id=1, source_target_pairs={{32,0},{64,32},{96,64},{128,96},{160,128},{192,160},{224,192},{256... | collective-permute-start | bytes 122888 | tf_op jit(solution)/shard_map/ppermute | solution.py:126
